TPU v7x, 1024 devices: a whole 4x4x32 slice. The times are simulated.
1024 devices in a mesh: expert: 32 (over z), dp: 32 (over y, x, core).
Axes of the slice: x: 4, y: 4, z: 32, core: 2. Of those that a mesh axis runs over, the one named last changes fastest.
Arguments:
- grad_out: bfloat16 [8192, 7168], P(('expert', 'dp')), may hold values from -6 to 6
- combine: bfloat16 [8192, 8], P(('expert', 'dp')), may hold values from 0.019897461 to 0.29882812
- expert_ids: int32 [8192, 8], P(('expert', 'dp')), may hold values from 0 to 127, as said below
- saved_hidden: bfloat16 [32, 32, 32, 3, 1024], P('expert', 'dp'), may hold values from -6 to 6
Outputs:
- grad_down: bfloat16 [128, 1024, 7168], P('expert', None, 'dp')
Inputs may be any that keep to these rules, and one draw needn't show every extreme that they name: `expert_ids`: within the 64 entries of one device (an aligned block of 8 tokens), each destination index id // 4 is named at most 3 times, and some destination exactly 3 times; over the devices of one data group every destination is named exactly 8 * 8 times. `saved_hidden`: rows of slots that no entry names hold arbitrary values.
All inputs are finite; a program needn't handle non-finite values.
Results may differ from a plain program's by a relative error of at most 0.0049.
Values may be sent and summed in bfloat16 or wider, within the bound.
No kernel may reach another device: no remote copies, remote signals or barrier semaphores. Data moves between devices by JAX's collectives and lax.ppermute only.
A program may use at most 32 MiB of HBM per device.

v0:
```python
import jax
import jax.numpy as jnp
from jax import lax
from jax.sharding import PartitionSpec as P

D = 7168
FF = 1024
TOP = 8
EXP_DEV = 4
TOK_DEV = 8


def local_slots(block_ids, n_dest, capacity):
    flat_ids = block_ids.reshape(-1)
    destination = flat_ids // EXP_DEV
    onehot = (destination[:, None] == jnp.arange(n_dest, dtype=jnp.int32)[None, :]).astype(
        jnp.int32
    )
    before = jnp.cumsum(onehot, axis=0) - onehot
    slot_rank = jnp.sum(before * onehot, axis=1)
    position = destination * capacity + slot_rank
    slot_numbers = jnp.arange(n_dest * capacity, dtype=jnp.int32)
    select = slot_numbers[:, None] == position[None, :]
    return (select, flat_ids % EXP_DEV)


def expert_product(hidden_piece, weight_piece, label_piece, grad_piece):
    weighted = (
        weight_piece.astype(jnp.float32)[:, None] * hidden_piece.astype(jnp.float32)
    ).astype(jnp.bfloat16)
    expert_mask = (label_piece[:, None] == jnp.arange(EXP_DEV, dtype=jnp.int32)[None, :]).astype(
        jnp.bfloat16
    )
    spread = (expert_mask[:, :, None] * grad_piece[:, None, :]).reshape(grad_piece.shape[0], -1)
    return lax.dot_general(
        weighted, spread, (((0,), (0,)), ((), ())), preferred_element_type=jnp.float32
    )


def per_device(grad_out, combine, expert_ids, saved_hidden):
    n_exp = lax.axis_size("expert")
    n_grp = lax.axis_size("dp")
    capacity = saved_hidden.shape[3]
    slot_count = n_exp * capacity
    slice_width = D // n_grp
    live_count = TOK_DEV * TOP
    hidden = saved_hidden.reshape(slot_count, FF)
    select, local_expert = local_slots(expert_ids, n_exp, capacity)
    token_pick = select.reshape(slot_count, TOK_DEV, TOP).any(axis=2).astype(jnp.bfloat16)
    send_rows = jnp.dot(token_pick, grad_out, preferred_element_type=jnp.float32).astype(
        jnp.bfloat16
    )
    weight_flat = combine.reshape(-1)
    send_weight = jnp.sum(
        jnp.where(select, weight_flat[None, :], jnp.zeros_like(weight_flat)[None, :]), axis=1
    )
    send_label = jnp.sum(jnp.where(select, local_expert[None, :] + 1, 0), axis=1) - 1
    routed, weights, labels = (
        lax.all_to_all(
            send_rows.reshape(n_exp, capacity, D), "expert", split_axis=0, concat_axis=0, tiled=True
        ),
        lax.all_to_all(
            send_weight.reshape(n_exp, capacity), "expert", split_axis=0, concat_axis=0, tiled=True
        ),
        lax.all_to_all(
            send_label.reshape(n_exp, capacity), "expert", split_axis=0, concat_axis=0, tiled=True
        ),
    )
    routed = routed.reshape(slot_count, D)
    weights = weights.reshape(slot_count)
    labels = labels.reshape(slot_count)
    keep_order = jnp.argsort((labels < 0).astype(jnp.int32), stable=True)[:live_count]
    routed = routed[keep_order]
    weights = weights[keep_order]
    labels = labels[keep_order]
    hidden = hidden[keep_order]
    row_count = routed.shape[0]
    shares = lax.all_to_all(
        routed.reshape(1, row_count, D), "dp", split_axis=2, concat_axis=0, tiled=True
    )
    grad_all = shares.reshape(n_grp * row_count, slice_width)
    hidden_piece = lax.all_gather(hidden, "dp", axis=0, tiled=True)
    weight_piece = lax.all_gather(weights, "dp", axis=0, tiled=True)
    label_piece = lax.all_gather(labels, "dp", axis=0, tiled=True)
    gradient = expert_product(hidden_piece, weight_piece, label_piece, grad_all)
    return jnp.transpose(gradient.reshape(FF, EXP_DEV, slice_width), (1, 0, 2)).astype(jnp.bfloat16)


def solution(mesh):
    placed = (
        P(("expert", "dp"), None),
        P(("expert", "dp"), None),
        P(("expert", "dp"), None),
        P("expert", "dp", None, None, None),
    )
    return jax.shard_map(
        per_device, mesh=mesh, in_specs=placed, out_specs=P("expert", None, "dp"), check_vma=False
    )
```

profile of v0, /device:TPU:28, one launch (start us, length us, event | category | flops | bytes accessed | tf_op | source)
XLA Modules:
  0.0 413.9 jit_solution(223902512602245847)
XLA Ops:
  6.5 0.0 copy-start
  6.5 0.8 reshape.168
  7.4 0.1 fusion.12
  7.4 0.1 reduce_window_sum.11
  7.5 0.2 select_reduce_fusion.1
  7.7 0.1 select_reduce_fusion
  7.8 0.7 sub.20
  8.5 28.7 %all-to-all-start.1 = ((s32[32,1,3]{2,1,0:T(1,128)}), s32[32,1,3]{2,1,0:T(1,128)S(1)}, u32[]{:S(2)}, u32[]{:S(2)}) async-start(s32[32,1,3]{2,1,0:T(1,128)} %bitcast), calls=%async_computation.1 | async-start | bytes 32768 | tf_op jit(solution)/shard_map/all_to_all | solution.py:65
  37.3 0.1 reduce_sum.35
  37.4 0.7 fusion.19
  38.1 0.1 fusion.15
  38.2 0.0 copy-done
  38.2 0.6 convolution_convert_fusion
  38.7 0.0 copy-start.1
  38.7 2.2 reshape.172
  40.9 0.0 copy-start.2
  40.9 18.6 %all-to-all-done.1 = s32[32,1,3]{2,1,0:T(1,128)S(1)} async-done(((s32[32,1,3]{2,1,0:T(1,128)}), s32[32,1,3]{2,1,0:T(1,128)S(1)}, u32[]{:S(2)}, u32[]{:S(2)}) %all-to-all-start.1) | async-done | bytes 416 | tf_op jit(solution)/shard_map/all_to_all | solution.py:65
  59.5 4.0 all-to-all-start.2
  63.5 0.0 all-gather.5.cloned.1.call-start
  63.6 0.0 copy-done.1
  63.6 0.2 copy.24
  63.8 0.2 reshape.171
  63.9 0.6 broadcast.189
  64.5 0.7 reduce.5
  65.3 0.1 reshape.170
  65.4 2.6 sort.17
  68.0 1.3 gather_fusion.1
  69.4 0.0 all-gather.5.cloned.1.call-update
  69.4 0.0 copy-done.2
  69.4 0.1 broadcast_in_dim.32
  69.5 0.1 fusion.16
  69.6 0.7 all_to_all.31
  70.3 169.8 %all-to-all-done.2 = bf16[32,3,7168]{2,1,0:T(4,128)(2,1)S(1)} async-done(((bf16[32,3,7168]{2,1,0:T(4,128)(2,1)}), bf16[32,3,7168]{2,1,0:T(4,128)(2,1)S(1)}, u32[]{:S(2)}, u32[]{:S(2)}) %all-to-all-start.2) | async-done | bytes 1376288 | tf_op jit(solution)/shard_map/all_to_all | solution.py:59
  240.1 3.7 all-to-all-start
  243.9 1.2 reshape.173
  245.1 1.1 gather_fusion.3
  246.2 6.0 %copy.25 = bf16[1,64,7168]{1,0,2:T(2,128)(2,1)} copy(bf16[1,64,7168]{2,1,0:T(8,128)(2,1)S(1)} %bitcast.29) | data formatting | bytes 1835008 | tf_op jit(solution)/shard_map/reshape | solution.py:79
  252.3 0.5 broadcast.190
  252.8 39.8 %reduce.6 = bf16[7168,64]{1,0:T(8,128)(2,1)S(1)} reduce(bf16[7168,1,64]{2,1,0:T(2,128)(2,1)} %bitcast.25, bf16[]{:T(256)} %broadcast.190), dimensions={1}, to_apply=%bitcast.21.reduce_sub_computation | reduce | bytes 1835010
  292.6 1.8 reshape.235
  294.4 0.0 all-to-all-done
  294.4 7.3 %all-to-all-start.3 = ((bf16[32,2,7168]{2,1,0:T(2,128)(2,1)}), bf16[32,2,7168]{2,1,0:T(2,128)(2,1)S(1)}, u32[]{:S(2)}, u32[]{:S(2)}) async-start(bf16[32,2,7168]{2,1,0:T(2,128)(2,1)} %reshape.235), calls=%async_computation.3 | async-start | bytes 1835008 | tf_op jit(solution)/shard_map/all_to_all | solution.py:78
  301.7 1.3 dynamic-slice
  303.6 0.1 reduce.1
  303.7 0.1 reshape.169
  303.8 0.8 gather_fusion.2
  304.6 0.8 gather_fusion
  305.4 0.2 dynamic-update-slice
  305.6 56.2 %all-reduce = bf16[2048]{0:T(1024)(128)(2,1)S(1)} all-reduce(bf16[2048]{0:T(1024)(128)(2,1)S(1)} %dynamic-update-slice), channel_id=2, replica_groups=mesh['expert'=32,'dp'=32] {'dp'}, use_global_device_ids=true, to_apply=%add | all-reduce | flops 2048 | bytes 8192
  361.8 0.3 dynamic-update-slice.1
  362.1 23.4 %all-reduce.1 = s32[2048]{0:T(1024)S(1)} all-reduce(s32[2048]{0:T(1024)S(1)} %dynamic-update-slice.1), channel_id=4, replica_groups=mesh['expert'=32,'dp'=32] {'dp'}, use_global_device_ids=true, to_apply=%add.1 | all-reduce | flops 2048 | bytes 16384
  385.5 0.0 all-to-all-done.3
  385.6 4.2 %reshape.236 = bf16[7168,1,64]{2,1,0:T(2,128)(2,1)} reshape(bf16[32,2,7168]{2,1,0:T(2,128)(2,1)S(1)} %all-to-all-done.3) | data formatting | bytes 1835008
  389.7 7.2 %copy.26 = bf16[1,64,7168]{2,1,0:T(8,128)(2,1)S(1)} copy(bf16[1,64,7168]{1,0,2:T(2,128)(2,1)} %bitcast.26) | data formatting | bytes 1835008 | tf_op jit(solution)/shard_map/all_to_all | solution.py:78
  396.9 1.5 all_to_all.29
  398.4 0.6 copy.27
  399.0 0.5 copy.28
  399.5 0.0 all-gather.5.cloned.1.call-done
  399.5 7.5 %convert_bitcast_fusion = bf16[4,1024,224]{1,2,0:T(8,128)(2,1)} fusion(bf16[2048,224]{0,1:T(8,128)(2,1)S(1)} %copy.28, bf16[2048,4]{0,1:T(4,128)(2,1)S(1)} %fusion.14, bf16[2048,1024]{1,0:T(8,128)(2,1)} %all-gather.5.cloned.1.call-done, f32[2048]{0:T(1024)S(1)} %convert_element_type.36), kind=kOutput, calls=%fused_computation.11 | convolution fusion | flops 3772645376 | bytes 6971392 | tf_op jit(solution)/shard_map/dot_general | solution.py:35
  (11 shorter events, 0.1 us)
Async XLA Ops:
  6.5 31.6 %copy-start = (bf16[8,7168]{1,0:T(8,128)(2,1)S(1)}, bf16[8,7168]{1,0:T(8,128)(2,1)}, u32[]{:S(2)}) copy-start(bf16[8,7168]{1,0:T(8,128)(2,1)} %param.4) | copy-start | bytes 344068
  8.5 51.0 %all-to-all-start.1 = ((s32[32,1,3]{2,1,0:T(1,128)}), s32[32,1,3]{2,1,0:T(1,128)S(1)}, u32[]{:S(2)}, u32[]{:S(2)}) async-start(s32[32,1,3]{2,1,0:T(1,128)} %bitcast), calls=%async_computation.1 | async-start | bytes 32768 | tf_op jit(solution)/shard_map/all_to_all | solution.py:65
  38.7 24.9 %copy-start.1 = (bf16[1,1,32,3,1024]{4,2,3,1,0:T(8,128)(2,1)S(1)}, bf16[1,1,32,3,1024]{4,2,3,1,0:T(8,128)(2,1)}, u32[]{:S(2)}) copy-start(bf16[1,1,32,3,1024]{4,2,3,1,0:T(8,128)(2,1)} %param.7) | copy-start | bytes 589828
  40.9 28.5 %copy-start.2 = (bf16[8,8]{1,0:T(8,128)(2,1)S(1)}, bf16[8,8]{1,0:T(8,128)(2,1)}, u32[]{:S(2)}) copy-start(bf16[8,8]{1,0:T(8,128)(2,1)} %param.5) | copy-start | bytes 388
  59.5 180.6 %all-to-all-start.2 = ((bf16[32,3,7168]{2,1,0:T(4,128)(2,1)}), bf16[32,3,7168]{2,1,0:T(4,128)(2,1)S(1)}, u32[]{:S(2)}, u32[]{:S(2)}) async-start(bf16[32,3,7168]{2,1,0:T(4,128)(2,1)} %reshape.172), calls=%async_computation.2 | async-start | bytes 3670016 | tf_op jit(solution)/shard_map/all_to_all | solution.py:59
  63.5 336.0 %all-gather.5.cloned.1.call-start = ((), (), s32[]{:S(2)}) async-start(), calls=%async_computation.4 | async-start | bytes 4325376 | tf_op jit(solution)/shard_map/all_gather | solution.py:82
  240.1 54.3 %all-to-all-start = ((bf16[32,1,3]{2,1,0:T(2,128)(2,1)}), bf16[32,1,3]{2,1,0:T(2,128)(2,1)S(1)}, u32[]{:S(2)}, u32[]{:S(2)}) async-start(bf16[32,1,3]{2,1,0:T(2,128)(2,1)} %all_to_all.31), calls=%async_computation | async-start | bytes 32768 | tf_op jit(solution)/shard_map/all_to_all | solution.py:62
  294.4 91.1 %all-to-all-start.3 = ((bf16[32,2,7168]{2,1,0:T(2,128)(2,1)}), bf16[32,2,7168]{2,1,0:T(2,128)(2,1)S(1)}, u32[]{:S(2)}, u32[]{:S(2)}) async-start(bf16[32,2,7168]{2,1,0:T(2,128)(2,1)} %reshape.235), calls=%async_computation.3 | async-start | bytes 1835008 | tf_op jit(solution)/shard_map/all_to_all | solution.py:78
Sparse Core Ops, SparseCore 0:
  69.5 80.2 all-gather.4
where the time goes:
time: 415 us; the launch traced here: 414 us
  waiting for transfers between devices  188 us (45%)
  blocking collectives  79.6 us (19%)
  other arithmetic  44.6 us (11%)
  starting transfers between devices  43.8 us (11%)
  local copies, waits for them, and re-layouts  35 us (8%)
  between operations  14.2 us (3%)
  matrix products  8.07 us (2%)
    all_to_all x1, waiting for transfers between devices, per_device(): lax.all_to_all(send_rows.reshape(n_exp, capacity, D), 'expert', split_axi...  170 us
    unnamed x2, blocking collectives  79.6 us
    unnamed x1, other arithmetic  39.8 us
    all_to_all x1, starting transfers between devices, per_device(): lax.all_to_all(send_label.reshape(n_exp, capacity), 'expert', split_axis=...  28.7 us
    all_to_all x1, waiting for transfers between devices, per_device(): lax.all_to_all(send_label.reshape(n_exp, capacity), 'expert', split_axis=...  18.6 us
    all_to_all x3, local copies, waits for them, and re-layouts, per_device(): lax.all_to_all(routed.reshape(1, row_count, D), 'dp', split_axis=2, conca...  9.23 us
    unnamed x15, local copies, waits for them, and re-layouts  8.46 us
  transfers between devices with their start and end apart: 5, of which 2 were waited for; matrix products, arithmetic and copies ran while one was open for 18% of the time, Pallas kernels for 0%

commit v1 on v0

v1 whole, which is shorter than its diff:
```python
import jax
import jax.numpy as jnp
from jax import lax
from jax.sharding import PartitionSpec as P

D = 7168
FF = 1024
TOP = 8
EXP_DEV = 4
TOK_DEV = 8


def slot_tables(meta_all, me_exp, me_grp, capacity):
    n_src = meta_all.shape[0]
    per_block = TOK_DEV * TOP
    ids = meta_all[:, :, :TOP].astype(jnp.int32).reshape(n_src, per_block)
    wts = meta_all[:, :, TOP:].reshape(n_src, per_block)
    n_dest = lax.axis_size("expert")
    destination = ids // EXP_DEV
    local = ids % EXP_DEV
    onehot = (destination[:, :, None] == jnp.arange(n_dest, dtype=jnp.int32)[None, None, :]).astype(
        jnp.int32
    )
    before = jnp.cumsum(onehot, axis=1) - onehot
    rank = jnp.sum(before * onehot, axis=2)
    mine = destination == me_exp
    select = mine[:, None, :] & (
        rank[:, None, :] == jnp.arange(capacity, dtype=jnp.int32)[None, :, None]
    )
    weight = jnp.sum(jnp.where(select, wts[:, None, :], 0.0), axis=2)
    label = jnp.sum(jnp.where(select, local[:, None, :], 0), axis=2)
    token_in_block = jnp.arange(per_block, dtype=jnp.int32) // TOP
    token = jnp.sum(jnp.where(select, token_in_block[None, None, :], 0), axis=2)
    block = jnp.arange(n_src, dtype=jnp.int32) * lax.axis_size("dp") + me_grp
    token = token + block[:, None] * TOK_DEV
    live = jnp.any(select, axis=2)
    return weight.reshape(-1), label.reshape(-1), token.reshape(-1), live.reshape(-1)


def per_device(grad_out, combine, expert_ids, saved_hidden):
    n_grp = lax.axis_size("dp")
    capacity = saved_hidden.shape[3]
    width = D // n_grp
    live_count = TOK_DEV * TOP
    me_exp = lax.axis_index("expert")
    me_grp = lax.axis_index("dp")

    cols = jnp.transpose(grad_out.reshape(TOK_DEV, n_grp, width), (1, 0, 2))
    cols = lax.all_to_all(cols, "dp", 0, 0, tiled=True)
    tokens = lax.all_gather(cols, "expert", axis=0, tiled=False).reshape(-1, width)

    meta = jnp.concatenate(
        [expert_ids.astype(jnp.float32), combine.astype(jnp.float32)], axis=1
    )
    meta_all = lax.all_gather(meta, "expert", axis=0, tiled=False)
    weight, label, token, live = slot_tables(meta_all, me_exp, me_grp, capacity)

    hidden = saved_hidden.reshape(-1, FF)
    weighted = (weight[:, None] * hidden.astype(jnp.float32)).astype(jnp.bfloat16)
    position = jnp.cumsum(live.astype(jnp.int32)) - 1
    pick = live[None, :] & (position[None, :] == jnp.arange(live_count, dtype=jnp.int32)[:, None])
    packed = jnp.dot(
        pick.astype(jnp.bfloat16), weighted, preferred_element_type=jnp.float32
    ).astype(jnp.bfloat16)
    label_c = jnp.sum(jnp.where(pick, label[None, :], 0), axis=1)
    token_c = jnp.sum(jnp.where(pick, token[None, :], 0), axis=1)
    extra = jnp.stack([label_c, token_c // 128, token_c % 128], axis=1).astype(jnp.bfloat16)
    extra = jnp.pad(extra, ((0, 0), (0, 128 - extra.shape[1])))
    payload = jnp.concatenate([packed, extra], axis=1)
    gathered = lax.all_gather(payload, "dp", axis=0, tiled=True)

    rows = gathered[:, :FF]
    labels = gathered[:, FF].astype(jnp.int32)
    picks = gathered[:, FF + 1].astype(jnp.int32) * 128 + gathered[:, FF + 2].astype(jnp.int32)
    grad_rows = jnp.take(tokens, picks, axis=0, mode="clip")
    mask = labels[:, None] == jnp.arange(EXP_DEV, dtype=jnp.int32)[None, :]
    spread = jnp.where(mask[:, :, None], rows[:, None, :], jnp.zeros_like(rows)[:, None, :])
    spread = spread.reshape(rows.shape[0], EXP_DEV * FF)
    gradient = lax.dot_general(
        spread, grad_rows, (((0,), (0,)), ((), ())), preferred_element_type=jnp.float32
    )
    return gradient.reshape(EXP_DEV, FF, width).astype(jnp.bfloat16)


def solution(mesh):
    placed = (
        P(("expert", "dp"), None),
        P(("expert", "dp"), None),
        P(("expert", "dp"), None),
        P("expert", "dp", None, None, None),
    )
    return jax.shard_map(
        per_device, mesh=mesh, in_specs=placed, out_specs=P("expert", None, "dp"), check_vma=False
    )
```

time: 415 us -> 329 us (0.79)
  the two profiles are of different devices: /device:TPU:28 before, /device:TPU:4 now
where the time goes in v1:
time: 329 us; the launch traced here: 328 us
  waiting for transfers between devices  194 us (59%)
  blocking collectives  81.7 us (25%)
  local copies, waits for them, and re-layouts  23.7 us (7%)
  between operations  13.6 us (4%)
  matrix products  8.39 us (3%)
  other arithmetic  7.45 us (2%)
    all_gather x1, waiting for transfers between devices, per_device(): lax.all_gather(cols, 'expert', axis=0, tiled=False).reshape(-1, width)  134 us
    all_gather x1, blocking collectives, per_device(): meta_all = lax.all_gather(meta, 'expert', axis=0, tiled=False)  68.6 us
    all_gather x1, waiting for transfers between devices, per_device(): gathered = lax.all_gather(payload, 'dp', axis=0, tiled=True)  60.1 us
    all_to_all x1, blocking collectives, per_device(): cols = lax.all_to_all(cols, 'dp', 0, 0, tiled=True)  13.1 us
    slice x2, local copies, waits for them, and re-layouts, per_device(): rows = gathered[:, :FF]  11.1 us
    gather x1, local copies, waits for them, and re-layouts, per_device(): grad_rows = jnp.take(tokens, picks, axis=0, mode='clip')  9.36 us
    dot_general x1, matrix products, per_device(): lax.dot_general(spread, grad_rows, (((0,), (0,)), ((), ())), preferred_el...  8.15 us
  transfers between devices with their start and end apart: 2, of which 2 were waited for; matrix products, arithmetic and copies ran while one was open for 4% of the time, Pallas kernels for 0%

profile of v1, /device:TPU:4, one launch (start us, length us, event | category | flops | bytes accessed | tf_op | source)
XLA Modules:
  0.0 328.4 jit_solution(5987120840019349571)
XLA Ops:
  6.5 0.0 copy-start
  6.5 0.0 all-gather.5.cloned.1.call-start
  6.5 0.7 convert_element_type.61
  7.3 0.7 convert_element_type.60
  8.0 0.1 pad_maximum_fusion
  8.0 68.6 %all-gather = f32[256,16]{1,0:T(8,128)S(1)} all-gather(f32[8,16]{1,0:T(8,128)S(1)} %pad_maximum_fusion), channel_id=2, replica_groups=mesh['expert'=32,'dp'=32] {'expert'}, dimensions={0}, use_global_device_ids=true | all-gather | bytes 16896 | tf_op jit(solution)/shard_map/all_gather | solution.py:55
  76.6 0.1 fusion.29
  76.7 0.1 copy.124
  76.8 0.1 copy.103
  77.0 0.1 copy.107
  77.0 1.7 select_reduce_fusion
  78.8 0.1 copy.108
  78.8 0.2 fusion.19
  79.0 0.1 copy.109
  79.1 0.2 select_reduce_fusion.2
  79.3 0.1 copy.116
  79.4 0.1 broadcast_in_dim.101
  79.5 0.1 copy.110
  79.6 0.1 reshape.285
  79.7 0.1 reduce-window.8
  79.8 0.1 add_reduce_fusion.1
  79.9 0.1 and.103
  80.1 0.1 copy.117
  80.2 0.1 add.87
  80.3 0.1 select_reduce_fusion.5
  80.4 0.1 copy.118
  80.5 1.1 copy.115
  81.6 0.2 reshape.271
  81.9 0.1 copy.112
  81.9 0.1 copy.113
  82.0 0.1 select_reduce_fusion.3
  82.1 0.1 copy.114
  82.2 0.1 mul.42
  82.3 0.2 convolution_convert_fusion
  82.6 0.7 fusion.17
  83.3 0.0 all-gather.5.cloned.1.call-update
  83.3 0.0 all-gather.7.cloned.1.call-start
  83.3 0.0 copy-done
  83.3 0.2 reshape.268
  83.5 0.1 copy.120
  83.6 13.1 %all_to_all.5 = bf16[32,8,224]{2,1,0:T(8,128)(2,1)} all-to-all(bf16[32,8,224]{2,1,0:T(8,128)(2,1)S(1)} %copy.120), channel_id=1, replica_groups=mesh['expert'=32,'dp'=32] {'dp'}, dimensions={0} | all-to-all | bytes 229376 | tf_op jit(solution)/shard_map/all_to_all | solution.py:49
  96.7 0.0 all-gather.7.cloned.1.call-update
  96.7 60.1 %all-gather.5.cloned.1.call-done = bf16[2048,1152]{1,0:T(8,128)(2,1)} async-done(((bf16[64,1152]{1,0:T(8,128)(2,1)}), bf16[2048,1152]{1,0:T(8,128)(2,1)}) %all-gather.5.cloned.1.call-update) | async-done | bytes 4718608 | tf_op jit(solution)/shard_map/all_gather | solution.py:70
  156.8 4.6 %slice.29 = bf16[2048,1024]{1,0:T(8,128)(2,1)} slice(bf16[2048,1152]{1,0:T(8,128)(2,1)} %all-gather.5.cloned.1.call-done), slice={[0:2048], [0:1024]} | slice | bytes 8388608 | tf_op jit(solution)/shard_map/slice | solution.py:72
  161.4 6.5 %copy.119 = bf16[2048,1024]{0,1:T(8,128)(2,1)} copy(bf16[2048,1024]{1,0:T(8,128)(2,1)} %slice.29) | data formatting | bytes 8388608 | tf_op jit(solution)/shard_map/slice | solution.py:72
  167.9 2.6 add_reduce_fusion
  170.6 133.5 %all-gather.7.cloned.1.call-done = bf16[1024,8,224]{2,1,0:T(8,128)(2,1)} async-done(((bf16[32,8,224]{2,1,0:T(8,128)(2,1)}), bf16[1024,8,224]{2,1,0:T(8,128)(2,1)}) %all-gather.7.cloned.1.call-update) | async-done | bytes 3670032 | tf_op jit(solution)/shard_map/all_gather | solution.py:50
  304.1 9.4 %gather_fusion = bf16[2048,224]{1,0:T(8,128)(2,1)S(1)} fusion(bf16[8192,224]{1,0:T(8,128)(2,1)} %bitcast.37, s32[2048]{0:T(1024)S(1)} %broadcast_clamp_fusion), kind=kCustom, calls=%fused_computation | custom fusion | bytes 1843200 | tf_op jit(solution)/shard_map/jit(_take)/gather | solution.py:75
  313.4 8.1 %fusion.6 = bf16[4,1024,224]{1,2,0:T(8,128)(2,1)} fusion(pred[2048,4]{0,1:T(4,128)(4,1)S(1)} %iota_compare_fusion.4, bf16[2048,1024]{0,1:T(8,128)(2,1)} %copy.119, bf16[2048,224]{1,0:T(8,128)(2,1)S(1)} %gather_fusion), kind=kOutput, calls=%fused_computation.7 | convolution fusion | flops 3767402496 | bytes 6955008 | tf_op jit(solution)/shard_map/dot_general | solution.py:79
  (12 shorter events, 0.1 us)
Async XLA Ops:
  6.5 76.8 %copy-start = (bf16[8,7168]{1,0:T(8,128)(2,1)S(1)}, bf16[8,7168]{1,0:T(8,128)(2,1)}, u32[]{:S(2)}) copy-start(bf16[8,7168]{1,0:T(8,128)(2,1)} %param.4) | copy-start | bytes 344068
  6.5 150.3 %all-gather.5.cloned.1.call-start = ((), (), s32[]{:S(2)}) async-start(), calls=%async_computation.1 | async-start | bytes 4866048 | tf_op jit(solution)/shard_map/all_gather | solution.py:70
  83.3 220.8 %all-gather.7.cloned.1.call-start = ((), (), s32[]{:S(2)}) async-start(), calls=%async_computation.2 | async-start | bytes 4325376 | tf_op jit(solution)/shard_map/all_gather | solution.py:50
Sparse Core Ops, SparseCore 0:
  83.4 73.3 all-gather.4
  159.5 144.5 all-gather.6

commit v2 on v1

--- a/solution.py
+++ b/solution.py
@@ -10,11 +10,11 @@
 TOK_DEV = 8
 
 
-def slot_tables(meta_all, me_exp, me_grp, capacity):
+def slot_tables(meta_all, me_exp, me_grp, capacity, chunks):
     n_src = meta_all.shape[0]
     per_block = TOK_DEV * TOP
     ids = meta_all[:, :, :TOP].astype(jnp.int32).reshape(n_src, per_block)
-    wts = meta_all[:, :, TOP:].reshape(n_src, per_block)
+    wts = meta_all[:, :, TOP:].astype(jnp.float32).reshape(n_src, per_block)
     n_dest = lax.axis_size("expert")
     destination = ids // EXP_DEV
     local = ids % EXP_DEV
@@ -31,7 +31,7 @@
     label = jnp.sum(jnp.where(select, local[:, None, :], 0), axis=2)
     token_in_block = jnp.arange(per_block, dtype=jnp.int32) // TOP
     token = jnp.sum(jnp.where(select, token_in_block[None, None, :], 0), axis=2)
-    block = jnp.arange(n_src, dtype=jnp.int32) * lax.axis_size("dp") + me_grp
+    block = jnp.arange(n_src, dtype=jnp.int32) * chunks + me_grp
     token = token + block[:, None] * TOK_DEV
     live = jnp.any(select, axis=2)
     return weight.reshape(-1), label.reshape(-1), token.reshape(-1), live.reshape(-1)
@@ -47,13 +47,15 @@
 
     cols = jnp.transpose(grad_out.reshape(TOK_DEV, n_grp, width), (1, 0, 2))
     cols = lax.all_to_all(cols, "dp", 0, 0, tiled=True)
-    tokens = lax.all_gather(cols, "expert", axis=0, tiled=False).reshape(-1, width)
-
-    meta = jnp.concatenate(
-        [expert_ids.astype(jnp.float32), combine.astype(jnp.float32)], axis=1
+    meta = jnp.concatenate([expert_ids.astype(jnp.bfloat16), combine], axis=1)
+    meta = jnp.pad(meta, ((0, 0), (0, width - meta.shape[1])))[None]
+    chunks = n_grp + 1
+    everything = lax.all_gather(
+        jnp.concatenate([cols, meta], axis=0), "expert", axis=0, tiled=False
     )
-    meta_all = lax.all_gather(meta, "expert", axis=0, tiled=False)
-    weight, label, token, live = slot_tables(meta_all, me_exp, me_grp, capacity)
+    tokens = everything.reshape(-1, width)
+    meta_all = everything[:, n_grp, :, : 2 * TOP]
+    weight, label, token, live = slot_tables(meta_all, me_exp, me_grp, capacity, chunks)
 
     hidden = saved_hidden.reshape(-1, FF)
     weighted = (weight[:, None] * hidden.astype(jnp.float32)).astype(jnp.bfloat16)

time: 329 us -> 292 us (0.89)
  the two profiles are of different devices: /device:TPU:4 before, /device:TPU:1 now
where the time goes in v2:
time: 292 us
  waiting for transfers between devices  218 us (75%)
  local copies, waits for them, and re-layouts  26 us (9%)
  starting transfers between devices  17.8 us (6%)
  between operations  13.6 us (5%)
  matrix products  8.38 us (3%)
  other arithmetic  8.09 us (3%)
    all_gather x1, waiting for transfers between devices, per_device(): lax.all_gather(jnp.concatenate([cols, meta], axis=0), 'expert', axis=0, t...  119 us
    all_gather x1, waiting for transfers between devices, per_device(): gathered = lax.all_gather(payload, 'dp', axis=0, tiled=True)  92.4 us
    all_to_all x1, starting transfers between devices, per_device(): cols = lax.all_to_all(cols, 'dp', 0, 0, tiled=True)  17.7 us
    slice x2, local copies, waits for them, and re-layouts, per_device(): rows = gathered[:, :FF]  11.1 us
    gather x1, local copies, waits for them, and re-layouts, per_device(): grad_rows = jnp.take(tokens, picks, axis=0, mode='clip')  9.42 us
    dot_general x1, matrix products, per_device(): lax.dot_general(spread, grad_rows, (((0,), (0,)), ((), ())), preferred_el...  8.14 us
    all_to_all x1, waiting for transfers between devices, per_device(): cols = lax.all_to_all(cols, 'dp', 0, 0, tiled=True)  6.24 us
  transfers between devices with their start and end apart: 3, of which 3 were waited for; matrix products, arithmetic and copies ran while one was open for 1% of the time, Pallas kernels for 0%

profile of v2, /device:TPU:1, one launch (start us, length us, event | category | flops | bytes accessed | tf_op | source)
XLA Modules:
  0.0 291.7 jit_solution(3565294467444116061)
XLA Ops:
  6.5 1.1 reshape.270
  7.6 0.7 copy.107
  8.4 17.7 %all-to-all-start = ((bf16[32,8,224]{2,1,0:T(8,128)(2,1)}), bf16[32,8,224]{2,1,0:T(8,128)(2,1)S(1)}, u32[]{:S(2)}, u32[]{:S(2)}) async-start(bf16[32,8,224]{2,1,0:T(8,128)(2,1)} %copy.107), calls=%async_computation | async-start | bytes 262144 | tf_op jit(solution)/shard_map/all_to_all | solution.py:49
  26.1 0.0 all-gather.6.cloned.1.call-start
  26.1 0.7 convert_element_type.58
  26.8 0.8 fusion.31
  27.5 6.2 %all-to-all-done = bf16[32,8,224]{2,1,0:T(8,128)(2,1)S(1)} async-done(((bf16[32,8,224]{2,1,0:T(8,128)(2,1)}), bf16[32,8,224]{2,1,0:T(8,128)(2,1)S(1)}, u32[]{:S(2)}, u32[]{:S(2)}) %all-to-all-start) | async-done | bytes 114720 | tf_op jit(solution)/shard_map/all_to_all | solution.py:49
  33.8 0.7 pad_maximum_fusion
  34.5 0.0 all-gather.6.cloned.1.call-update
  34.5 0.0 all-gather.4.cloned.1.call-start
  34.6 1.1 copy.120
  35.7 0.2 reshape.278
  35.9 119.3 %all-gather.6.cloned.1.call-done = bf16[1056,8,224]{2,1,0:T(8,128)(2,1)} async-done(((bf16[33,8,224]{2,1,0:T(8,128)(2,1)}), bf16[1056,8,224]{2,1,0:T(8,128)(2,1)}) %all-gather.6.cloned.1.call-update) | async-done | bytes 3784720 | tf_op jit(solution)/shard_map/all_gather | solution.py:53
  155.2 0.8 slice.30
  156.0 0.1 copy.128
  156.2 0.1 copy.109
  156.3 0.1 copy.113
  156.4 1.7 select_reduce_fusion
  158.1 0.1 copy.114
  158.2 0.2 fusion.19
  158.3 0.1 copy.115
  158.4 0.1 copy.118
  158.5 0.1 select_reduce_fusion.3
  158.6 0.1 and.103
  158.7 0.1 copy.116
  158.8 0.2 select_reduce_fusion.2
  159.0 0.1 copy.122
  159.1 0.1 add.89
  159.2 0.1 copy.121
  159.3 0.1 broadcast_in_dim.109
  159.4 0.1 copy.119
  159.5 0.1 mul.42
  159.6 0.1 reshape.291
  159.7 0.1 reduce-window.8
  159.8 0.1 add_reduce_fusion.1
  159.9 0.1 select_reduce_fusion.5
  160.1 0.1 copy.123
  160.2 0.2 convolution_convert_fusion
  160.5 0.7 fusion.17
  161.1 0.0 all-gather.4.cloned.1.call-update
  161.2 92.4 %all-gather.4.cloned.1.call-done = bf16[2048,1152]{1,0:T(8,128)(2,1)} async-done(((bf16[64,1152]{1,0:T(8,128)(2,1)}), bf16[2048,1152]{1,0:T(8,128)(2,1)}) %all-gather.4.cloned.1.call-update) | async-done | bytes 4718608 | tf_op jit(solution)/shard_map/all_gather | solution.py:72
  253.5 4.6 %slice.34 = bf16[2048,1024]{1,0:T(8,128)(2,1)} slice(bf16[2048,1152]{1,0:T(8,128)(2,1)} %all-gather.4.cloned.1.call-done), slice={[0:2048], [0:1024]} | slice | bytes 8388608 | tf_op jit(solution)/shard_map/slice | solution.py:74
  258.1 6.5 %copy.124 = bf16[2048,1024]{0,1:T(8,128)(2,1)} copy(bf16[2048,1024]{1,0:T(8,128)(2,1)} %slice.34) | data formatting | bytes 8388608 | tf_op jit(solution)/shard_map/slice | solution.py:74
  264.6 2.6 add_reduce_fusion
  267.3 9.4 %gather_fusion = bf16[2048,224]{1,0:T(8,128)(2,1)S(1)} fusion(bf16[8448,224]{1,0:T(8,128)(2,1)} %bitcast.48, s32[2048]{0:T(1024)S(1)} %broadcast_clamp_fusion), kind=kCustom, calls=%fused_computation | custom fusion | bytes 1843200 | tf_op jit(solution)/shard_map/jit(_take)/gather | solution.py:77
  276.7 8.1 %fusion.6 = bf16[4,1024,224]{1,2,0:T(8,128)(2,1)} fusion(pred[2048,4]{0,1:T(4,128)(4,1)S(1)} %iota_compare_fusion.4, bf16[2048,1024]{0,1:T(8,128)(2,1)} %copy.124, bf16[2048,224]{1,0:T(8,128)(2,1)S(1)} %gather_fusion), kind=kOutput, calls=%fused_computation.7 | convolution fusion | flops 3767402496 | bytes 6955008 | tf_op jit(solution)/shard_map/dot_general | solution.py:81
  (12 shorter events, 0.1 us)
Async XLA Ops:
  8.4 25.4 %all-to-all-start = ((bf16[32,8,224]{2,1,0:T(8,128)(2,1)}), bf16[32,8,224]{2,1,0:T(8,128)(2,1)S(1)}, u32[]{:S(2)}, u32[]{:S(2)}) async-start(bf16[32,8,224]{2,1,0:T(8,128)(2,1)} %copy.107), calls=%async_computation | async-start | bytes 262144 | tf_op jit(solution)/shard_map/all_to_all | solution.py:49
  26.1 129.1 %all-gather.6.cloned.1.call-start = ((), (), s32[]{:S(2)}) async-start(), calls=%async_computation.2 | async-start | bytes 4460544 | tf_op jit(solution)/shard_map/all_gather | solution.py:53
  34.5 219.1 %all-gather.4.cloned.1.call-start = ((), (), s32[]{:S(2)}) async-start(), calls=%async_computation.1 | async-start | bytes 4866048 | tf_op jit(solution)/shard_map/all_gather | solution.py:72
Sparse Core Ops, SparseCore 0:
  34.6 120.5 all-gather.5
  161.3 92.2 all-gather.3

commit v3 on v1

v3 whole, which is shorter than its diff:
```python
import jax
import jax.numpy as jnp
from jax import lax
from jax.sharding import PartitionSpec as P

D = 7168
FF = 1024
TOP = 8
EXP_DEV = 4
TOK_DEV = 8


def slot_tables(meta_gs, me_exp, relative, capacity):
    n_grp, n_src = meta_gs.shape[:2]
    per_block = TOK_DEV * TOP
    ids = meta_gs[..., :TOP].astype(jnp.int32).reshape(n_grp, n_src, per_block)
    wts = meta_gs[..., TOP:].astype(jnp.float32).reshape(n_grp, n_src, per_block)
    destination = ids // EXP_DEV
    local = ids % EXP_DEV
    entry = jnp.arange(per_block, dtype=jnp.int32)
    earlier = entry[None, :] < entry[:, None]
    same = destination[..., :, None] == destination[..., None, :]
    rank = jnp.sum((same & earlier).astype(jnp.int32), axis=-1)
    mine = destination == me_exp
    select = mine[:, :, None, :] & (
        rank[:, :, None, :] == jnp.arange(capacity, dtype=jnp.int32)[None, None, :, None]
    )
    weight = jnp.sum(jnp.where(select, wts[:, :, None, :], 0.0), axis=-1)
    label = jnp.sum(jnp.where(select, local[:, :, None, :] + 1, 0), axis=-1) - 1
    token_in_block = jnp.sum(jnp.where(select, (entry // TOP)[None, None, None, :], 0), axis=-1)
    block = relative[None, :] * n_grp + jnp.arange(n_grp, dtype=jnp.int32)[:, None]
    token = token_in_block + block[:, :, None] * TOK_DEV
    return weight.reshape(-1), label.reshape(-1), token.reshape(-1)


def per_device(grad_out, combine, expert_ids, saved_hidden):
    n_exp = lax.axis_size("expert")
    n_grp = lax.axis_size("dp")
    capacity = saved_hidden.shape[3]
    width = D // n_grp
    me_exp = lax.axis_index("expert")

    hidden = lax.all_gather(saved_hidden.reshape(-1, FF), "dp", axis=0, tiled=True)

    meta = jnp.concatenate([expert_ids.astype(jnp.bfloat16), combine], axis=1)
    cols = jnp.transpose(grad_out.reshape(TOK_DEV, n_grp, width), (1, 0, 2))
    cols = jnp.concatenate(
        [cols, jnp.broadcast_to(meta[None], (n_grp,) + meta.shape)], axis=2
    )
    cols = lax.all_to_all(cols, "dp", 0, 0, tiled=True)

    half = n_exp // 2
    fwd_perm = [(i, (i + 1) % n_exp) for i in range(n_exp)]
    bwd_perm = [(i, (i - 1) % n_exp) for i in range(n_exp)]
    ahead = [cols]
    behind = []
    fwd = cols
    bwd = cols
    for step in range(1, half + 1):
        fwd = lax.ppermute(fwd, "expert", fwd_perm)
        behind.append(fwd)
        if step < n_exp - half:
            bwd = lax.ppermute(bwd, "expert", bwd_perm)
            ahead.append(bwd)
    ring = jnp.stack(ahead + behind[::-1], axis=0)
    tokens = ring.reshape(-1, ring.shape[-1])

    relative = (jnp.arange(n_exp, dtype=jnp.int32) - me_exp) % n_exp
    meta_src = jnp.take(ring[:, :, :, width:], relative, axis=0)
    meta_gs = jnp.transpose(meta_src, (1, 0, 2, 3))
    weight, label, token = slot_tables(meta_gs, me_exp, relative, capacity)

    rows = (weight[:, None] * hidden.astype(jnp.float32)).astype(jnp.bfloat16)
    grad_rows = jnp.take(tokens, token, axis=0, mode="clip")[:, :width]
    mask = label[:, None] == jnp.arange(EXP_DEV, dtype=jnp.int32)[None, :]
    spread = jnp.where(mask[:, :, None], rows[:, None, :], jnp.zeros_like(rows)[:, None, :])
    spread = spread.reshape(rows.shape[0], EXP_DEV * FF)
    gradient = lax.dot_general(
        spread, grad_rows, (((0,), (0,)), ((), ())), preferred_element_type=jnp.float32
    )
    return gradient.reshape(EXP_DEV, FF, width).astype(jnp.bfloat16)


def solution(mesh):
    placed = (
        P(("expert", "dp"), None),
        P(("expert", "dp"), None),
        P(("expert", "dp"), None),
        P("expert", "dp", None, None, None),
    )
    return jax.shard_map(
        per_device, mesh=mesh, in_specs=placed, out_specs=P("expert", None, "dp"), check_vma=False
    )
```

time: 329 us -> 270 us (0.82)
  the two profiles are of different devices: /device:TPU:4 before, /device:TPU:2 now
where the time goes in v3:
time: 270 us; the launch traced here: 269 us
  starting transfers between devices  135 us (50%)
  other arithmetic  43.4 us (16%)
  local copies, waits for them, and re-layouts  34.4 us (13%)
  waiting for transfers between devices  31.4 us (12%)
  between operations  14.1 us (5%)
  matrix products  11 us (4%)
    ppermute x15, starting transfers between devices, per_device(): bwd = lax.ppermute(bwd, 'expert', bwd_perm)  87.2 us
    ppermute x16, starting transfers between devices, per_device(): fwd = lax.ppermute(fwd, 'expert', fwd_perm)  30.7 us
    reduce_sum x1, other arithmetic, slot_tables(): rank = jnp.sum((same & earlier).astype(jnp.int32), axis=-1)  29.7 us
    ppermute x16, waiting for transfers between devices, per_device(): fwd = lax.ppermute(fwd, 'expert', fwd_perm)  17.1 us
    all_to_all x1, starting transfers between devices, per_device(): cols = lax.all_to_all(cols, 'dp', 0, 0, tiled=True)  16.7 us
    gather x1, local copies, waits for them, and re-layouts, per_device(): grad_rows = jnp.take(tokens, token, axis=0, mode='clip')[:, :width]  12.5 us
    dot_general x1, matrix products, per_device(): lax.dot_general(spread, grad_rows, (((0,), (0,)), ((), ())), preferred_el...  11 us
    convert_element_type x1, local copies, waits for them, and re-layouts, per_device(): rows = (weight[:, None] * hidden.astype(jnp.float32)).astype(jnp.bfloat16)  8.63 us
  transfers between devices with their start and end apart: 33, of which 25 were waited for; matrix products, arithmetic and copies ran while one was open for 22% of the time, Pallas kernels for 0%

profile of v3, /device:TPU:2, one launch (start us, length us, event | category | flops | bytes accessed | tf_op | source)
XLA Modules:
  0.0 269.0 jit_solution(2630944829506044026)
XLA Ops:
  6.5 1.1 copy.82
  7.6 0.8 reshape.286
  8.5 1.1 reshape.283
  9.7 0.7 convert_element_type.17
  10.4 0.8 pad_maximum_fusion.1
  11.2 0.7 pad_maximum_fusion
  11.9 16.7 %all-to-all-start = ((bf16[32,8,240]{2,1,0:T(8,128)(2,1)}), bf16[32,8,240]{2,1,0:T(8,128)(2,1)S(1)}, u32[]{:S(2)}, u32[]{:S(2)}) async-start(bf16[32,8,240]{2,1,0:T(8,128)(2,1)} %pad_maximum_fusion), calls=%async_computation | async-start | bytes 262144 | tf_op jit(solution)/shard_map/all_to_all | solution.py:50
  28.7 6.6 %all-to-all-done = bf16[32,8,240]{2,1,0:T(8,128)(2,1)S(1)} async-done(((bf16[32,8,240]{2,1,0:T(8,128)(2,1)}), bf16[32,8,240]{2,1,0:T(8,128)(2,1)S(1)}, u32[]{:S(2)}, u32[]{:S(2)}) %all-to-all-start) | async-done | bytes 122912 | tf_op jit(solution)/shard_map/all_to_all | solution.py:50
  35.3 9.5 %collective-permute-start = (bf16[32,8,240]{2,1,0:T(8,128)(2,1)S(1)}, bf16[32,8,240]{2,1,0:T(8,128)(2,1)S(1)}, u32[]{:S(2)}, u32[]{:S(2)}) collective-permute-start(bf16[32,8,240]{2,1,0:T(8,128)(2,1)S(1)} %all-to-all-done), channel_id=1, source_target_pairs={{0,992},{32,0},{64,32},{96,64},{128,96},{160,128},{192,160},{224,1... | collective-permute-start | bytes 368648 | tf_op jit(solution)/shard_map/ppermute | solution.py:63
  44.8 1.9 collective-permute-start.15
  46.8 1.1 collective-permute-done
  47.9 5.6 %collective-permute-start.1 = (bf16[32,8,240]{2,1,0:T(8,128)(2,1)S(1)}, bf16[32,8,240]{2,1,0:T(8,128)(2,1)S(1)}, u32[]{:S(2)}, u32[]{:S(2)}) collective-permute-start(bf16[32,8,240]{2,1,0:T(8,128)(2,1)S(1)} %collective-permute-done), channel_id=1, source_target_pairs={{0,992},{32,0},{64,32},{96,64},{128,96},{160,128},{192,160},{224,1... | collective-permute-start | bytes 368648 | tf_op jit(solution)/shard_map/ppermute | solution.py:63
  53.5 1.9 collective-permute-start.16
  55.4 0.5 collective-permute-done.1
  56.0 5.6 %collective-permute-start.2 = (bf16[32,8,240]{2,1,0:T(8,128)(2,1)S(1)}, bf16[32,8,240]{2,1,0:T(8,128)(2,1)S(1)}, u32[]{:S(2)}, u32[]{:S(2)}) collective-permute-start(bf16[32,8,240]{2,1,0:T(8,128)(2,1)S(1)} %collective-permute-done.1), channel_id=1, source_target_pairs={{0,992},{32,0},{64,32},{96,64},{128,96},{160,128},{192,160},{224,1... | collective-permute-start | bytes 368648 | tf_op jit(solution)/shard_map/ppermute | solution.py:63
  61.6 1.9 collective-permute-start.17
  63.5 0.5 collective-permute-done.2
  64.0 5.6 %collective-permute-start.3 = (bf16[32,8,240]{2,1,0:T(8,128)(2,1)S(1)}, bf16[32,8,240]{2,1,0:T(8,128)(2,1)S(1)}, u32[]{:S(2)}, u32[]{:S(2)}) collective-permute-start(bf16[32,8,240]{2,1,0:T(8,128)(2,1)S(1)} %collective-permute-done.2), channel_id=1, source_target_pairs={{0,992},{32,0},{64,32},{96,64},{128,96},{160,128},{192,160},{224,1... | collective-permute-start | bytes 368648 | tf_op jit(solution)/shard_map/ppermute | solution.py:63
  69.6 1.9 collective-permute-start.18
  71.6 0.5 collective-permute-done.3
  72.1 5.6 %collective-permute-start.4 = (bf16[32,8,240]{2,1,0:T(8,128)(2,1)S(1)}, bf16[32,8,240]{2,1,0:T(8,128)(2,1)S(1)}, u32[]{:S(2)}, u32[]{:S(2)}) collective-permute-start(bf16[32,8,240]{2,1,0:T(8,128)(2,1)S(1)} %collective-permute-done.3), channel_id=1, source_target_pairs={{0,992},{32,0},{64,32},{96,64},{128,96},{160,128},{192,160},{224,1... | collective-permute-start | bytes 368648 | tf_op jit(solution)/shard_map/ppermute | solution.py:63
  77.7 1.9 collective-permute-start.19
  79.6 0.5 collective-permute-done.4
  80.2 5.6 %collective-permute-start.5 = (bf16[32,8,240]{2,1,0:T(8,128)(2,1)S(1)}, bf16[32,8,240]{2,1,0:T(8,128)(2,1)S(1)}, u32[]{:S(2)}, u32[]{:S(2)}) collective-permute-start(bf16[32,8,240]{2,1,0:T(8,128)(2,1)S(1)} %collective-permute-done.4), channel_id=1, source_target_pairs={{0,992},{32,0},{64,32},{96,64},{128,96},{160,128},{192,160},{224,1... | collective-permute-start | bytes 368648 | tf_op jit(solution)/shard_map/ppermute | solution.py:63
  85.7 1.9 collective-permute-start.20
  87.7 0.9 collective-permute-done.5
  88.6 5.6 %collective-permute-start.6 = (bf16[32,8,240]{2,1,0:T(8,128)(2,1)S(1)}, bf16[32,8,240]{2,1,0:T(8,128)(2,1)S(1)}, u32[]{:S(2)}, u32[]{:S(2)}) collective-permute-start(bf16[32,8,240]{2,1,0:T(8,128)(2,1)S(1)} %collective-permute-done.5), channel_id=1, source_target_pairs={{0,992},{32,0},{64,32},{96,64},{128,96},{160,128},{192,160},{224,1... | collective-permute-start | bytes 368648 | tf_op jit(solution)/shard_map/ppermute | solution.py:63
  94.5 1.9 collective-permute-start.21
  96.4 1.5 collective-permute-done.6
  97.9 5.6 %collective-permute-start.7 = (bf16[32,8,240]{2,1,0:T(8,128)(2,1)S(1)}, bf16[32,8,240]{2,1,0:T(8,128)(2,1)S(1)}, u32[]{:S(2)}, u32[]{:S(2)}) collective-permute-start(bf16[32,8,240]{2,1,0:T(8,128)(2,1)S(1)} %collective-permute-done.6), channel_id=1, source_target_pairs={{0,992},{32,0},{64,32},{96,64},{128,96},{160,128},{192,160},{224,1... | collective-permute-start | bytes 368648 | tf_op jit(solution)/shard_map/ppermute | solution.py:63
  103.9 1.9 collective-permute-start.22
  105.9 0.6 collective-permute-done.7
  106.5 5.6 %collective-permute-start.8 = (bf16[32,8,240]{2,1,0:T(8,128)(2,1)S(1)}, bf16[32,8,240]{2,1,0:T(8,128)(2,1)S(1)}, u32[]{:S(2)}, u32[]{:S(2)}) collective-permute-start(bf16[32,8,240]{2,1,0:T(8,128)(2,1)S(1)} %collective-permute-done.7), channel_id=1, source_target_pairs={{0,992},{32,0},{64,32},{96,64},{128,96},{160,128},{192,160},{224,1... | collective-permute-start | bytes 368648 | tf_op jit(solution)/shard_map/ppermute | solution.py:63
  112.5 1.9 collective-permute-start.23
  114.6 5.6 %collective-permute-start.9 = (bf16[32,8,240]{2,1,0:T(8,128)(2,1)S(1)}, bf16[32,8,240]{2,1,0:T(8,128)(2,1)S(1)}, u32[]{:S(2)}, u32[]{:S(2)}) collective-permute-start(bf16[32,8,240]{2,1,0:T(8,128)(2,1)S(1)} %collective-permute-done.8), channel_id=1, source_target_pairs={{0,992},{32,0},{64,32},{96,64},{128,96},{160,128},{192,160},{224,1... | collective-permute-start | bytes 368648 | tf_op jit(solution)/shard_map/ppermute | solution.py:63
  120.6 1.9 collective-permute-start.24
  122.7 5.6 %collective-permute-start.10 = (bf16[32,8,240]{2,1,0:T(8,128)(2,1)S(1)}, bf16[32,8,240]{2,1,0:T(8,128)(2,1)S(1)}, u32[]{:S(2)}, u32[]{:S(2)}) collective-permute-start(bf16[32,8,240]{2,1,0:T(8,128)(2,1)S(1)} %collective-permute-done.9), channel_id=1, source_target_pairs={{0,992},{32,0},{64,32},{96,64},{128,96},{160,128},{192,160},{224,1... | collective-permute-start | bytes 368648 | tf_op jit(solution)/shard_map/ppermute | solution.py:63
  128.6 1.9 collective-permute-start.25
  130.7 5.6 %collective-permute-start.11 = (bf16[32,8,240]{2,1,0:T(8,128)(2,1)S(1)}, bf16[32,8,240]{2,1,0:T(8,128)(2,1)S(1)}, u32[]{:S(2)}, u32[]{:S(2)}) collective-permute-start(bf16[32,8,240]{2,1,0:T(8,128)(2,1)S(1)} %collective-permute-done.10), channel_id=1, source_target_pairs={{0,992},{32,0},{64,32},{96,64},{128,96},{160,128},{192,160},{224,1... | collective-permute-start | bytes 368648 | tf_op jit(solution)/shard_map/ppermute | solution.py:63
  136.7 1.9 collective-permute-start.26
  138.8 5.6 %collective-permute-start.12 = (bf16[32,8,240]{2,1,0:T(8,128)(2,1)S(1)}, bf16[32,8,240]{2,1,0:T(8,128)(2,1)S(1)}, u32[]{:S(2)}, u32[]{:S(2)}) collective-permute-start(bf16[32,8,240]{2,1,0:T(8,128)(2,1)S(1)} %collective-permute-done.11), channel_id=1, source_target_pairs={{0,992},{32,0},{64,32},{96,64},{128,96},{160,128},{192,160},{224,1... | collective-permute-start | bytes 368648 | tf_op jit(solution)/shard_map/ppermute | solution.py:63
  144.7 1.9 collective-permute-start.27
  146.7 0.7 collective-permute-done.12
  147.4 5.6 %collective-permute-start.13 = (bf16[32,8,240]{2,1,0:T(8,128)(2,1)S(1)}, bf16[32,8,240]{2,1,0:T(8,128)(2,1)S(1)}, u32[]{:S(2)}, u32[]{:S(2)}) collective-permute-start(bf16[32,8,240]{2,1,0:T(8,128)(2,1)S(1)} %collective-permute-done.12), channel_id=1, source_target_pairs={{0,992},{32,0},{64,32},{96,64},{128,96},{160,128},{192,160},{224,1... | collective-permute-start | bytes 368648 | tf_op jit(solution)/shard_map/ppermute | solution.py:63
  153.0 0.7 collective-permute-done.27
  153.7 1.9 collective-permute-start.28
  155.6 5.4 %collective-permute-start.14 = (bf16[32,8,240]{2,1,0:T(8,128)(2,1)S(1)}, bf16[32,8,240]{2,1,0:T(8,128)(2,1)S(1)}, u32[]{:S(2)}, u32[]{:S(2)}) collective-permute-start(bf16[32,8,240]{2,1,0:T(8,128)(2,1)S(1)} %collective-permute-done.13), channel_id=1, source_target_pairs={{0,992},{32,0},{64,32},{96,64},{128,96},{160,128},{192,160},{224,1... | collective-permute-start | bytes 368648 | tf_op jit(solution)/shard_map/ppermute | solution.py:63
  161.0 1.5 collective-permute-done.28
  162.5 1.9 collective-permute-start.29
  164.5 6.1 %collective-permute-done.29 = bf16[32,8,240]{2,1,0:T(8,128)(2,1)S(1)} collective-permute-done((bf16[32,8,240]{2,1,0:T(8,128)(2,1)S(1)}, bf16[32,8,240]{2,1,0:T(8,128)(2,1)S(1)}, u32[]{:S(2)}, u32[]{:S(2)}) %collective-permute-start.29) | collective-permute-done | bytes 122912 | tf_op jit(solution)/shard_map/ppermute | solution.py:60
  170.6 2.1 collective-permute-start.30
  172.7 5.9 %collective-permute-done.30 = bf16[32,8,240]{2,1,0:T(8,128)(2,1)S(1)} collective-permute-done((bf16[32,8,240]{2,1,0:T(8,128)(2,1)S(1)}, bf16[32,8,240]{2,1,0:T(8,128)(2,1)S(1)}, u32[]{:S(2)}, u32[]{:S(2)}) %collective-permute-start.30) | collective-permute-done | bytes 122912 | tf_op jit(solution)/shard_map/ppermute | solution.py:60
  179.0 2.0 copy-done
  181.0 2.0 slice.20
  183.0 2.3 copy.92
  185.3 0.7 gather_fusion
  187.5 29.7 %convert_reduce_fusion = s32[32,32,64]{2,1,0:T(8,128)S(1)} fusion(s32[32,32,64]{2,1,0:T(8,128)S(1)} %get-tuple-element.8, pred[64,64]{1,0:T(8,128)(4,1)S(1)} %iota_compare_fusion.2), kind=kLoop, calls=%fused_computation.2 | loop fusion | flops 16711680 | bytes 528384 | tf_op jit(solution)/shard_map/reduce_sum | solution.py:23
  217.2 3.4 %select_reduce_fusion = (s32[32,32,3]{1,2,0:T(4,128)S(1)}, s32[32,32,3]{1,2,0:T(4,128)S(1)}) fusion(s32[64]{0:T(128)S(1)} %and_select_fusion, s32[32,32,64]{2,1,0:T(8,128)S(1)} %convert_reduce_fusion, pred[32,32,64]{2,1,0:T(8,128)(4,1)S(1)} %get-tuple-element.7, s32[32,32,64]{2,1,0:T(8,128)S(1)} %fusion.10), kind=kLoop, calls=%fused_computation.12 | loop fusion | flops 1173504 | bytes 614656 | tf_op jit(solution)/shard_map/reduce_sum | solution.py:30
  221.2 0.5 copy.80
  221.7 0.6 select_reduce_fusion.1
  223.4 12.5 %gather_fusion.1 = bf16[3072,240]{1,0:T(8,128)(2,1)S(1)} fusion(bf16[8192,240]{1,0:T(8,128)(2,1)} %bitcast.97, s32[3072]{0:T(1024)S(1)} %broadcast_clamp_fusion), kind=kCustom, calls=%fused_computation.1 | custom fusion | bytes 2961408 | tf_op jit(solution)/shard_map/jit(_take)/gather | solution.py:74
  236.0 6.5 %multiply_convert_fusion = bf16[3072,1024]{1,0:T(8,128)(2,1)} fusion(bf16[3072,1024]{1,0:T(8,128)(2,1)} %all-gather.2.cloned.1.call-done, f32[3072]{0:T(1024)S(1)} %mul.30), kind=kLoop, calls=%fused_computation.9 | loop fusion | flops 9437184 | bytes 12595200 | tf_op jit(solution)/shard_map/convert_element_type | solution.py:73
  242.5 8.6 %copy.83 = bf16[3072,1024]{0,1:T(8,128)(2,1)} copy(bf16[3072,1024]{1,0:T(8,128)(2,1)} %multiply_convert_fusion) | data formatting | bytes 12582912 | tf_op jit(solution)/shard_map/convert_element_type | solution.py:73
  251.1 11.0 %fusion.6 = bf16[4,1024,224]{1,2,0:T(8,128)(2,1)} fusion(pred[3072,4]{0,1:T(4,128)(4,1)S(1)} %iota_compare_fusion.1, bf16[3072,1024]{0,1:T(8,128)(2,1)} %copy.83, bf16[3072,240]{1,0:T(8,128)(2,1)S(1)} %gather_fusion.1), kind=kOutput, calls=%fused_computation.10 | convolution fusion | flops 5650644992 | bytes 9613312 | tf_op jit(solution)/shard_map/dot_general | solution.py:78
  (78 shorter events, 7.1 us)
Async XLA Ops:
  6.5 229.5 %all-gather.2.cloned.1.call-start = ((), (), s32[]{:S(2)}) async-start(), calls=%async_computation.1 | async-start | bytes 6488064 | tf_op jit(solution)/shard_map/all_gather | solution.py:43
  11.9 23.4 %all-to-all-start = ((bf16[32,8,240]{2,1,0:T(8,128)(2,1)}), bf16[32,8,240]{2,1,0:T(8,128)(2,1)S(1)}, u32[]{:S(2)}, u32[]{:S(2)}) async-start(bf16[32,8,240]{2,1,0:T(8,128)(2,1)} %pad_maximum_fusion), calls=%async_computation | async-start | bytes 262144 | tf_op jit(solution)/shard_map/all_to_all | solution.py:50
  35.3 12.6 %collective-permute-start = (bf16[32,8,240]{2,1,0:T(8,128)(2,1)S(1)}, bf16[32,8,240]{2,1,0:T(8,128)(2,1)S(1)}, u32[]{:S(2)}, u32[]{:S(2)}) collective-permute-start(bf16[32,8,240]{2,1,0:T(8,128)(2,1)S(1)} %all-to-all-done), channel_id=1, source_target_pairs={{0,992},{32,0},{64,32},{96,64},{128,96},{160,128},{192,160},{224,1... | collective-permute-start | bytes 368648 | tf_op jit(solution)/shard_map/ppermute | solution.py:63
  44.8 8.7 %collective-permute-start.15 = (bf16[32,8,240]{2,1,0:T(8,128)(2,1)S(1)}, bf16[32,8,240]{2,1,0:T(8,128)(2,1)S(1)}, u32[]{:S(2)}, u32[]{:S(2)}) collective-permute-start(bf16[32,8,240]{2,1,0:T(8,128)(2,1)S(1)} %all-to-all-done), channel_id=1, source_target_pairs={{0,32},{32,64},{64,96},{96,128},{128,160},{160,192},{192,224},{224... | collective-permute-start | bytes 368648 | tf_op jit(solution)/shard_map/ppermute | solution.py:60
  47.9 8.1 %collective-permute-start.1 = (bf16[32,8,240]{2,1,0:T(8,128)(2,1)S(1)}, bf16[32,8,240]{2,1,0:T(8,128)(2,1)S(1)}, u32[]{:S(2)}, u32[]{:S(2)}) collective-permute-start(bf16[32,8,240]{2,1,0:T(8,128)(2,1)S(1)} %collective-permute-done), channel_id=1, source_target_pairs={{0,992},{32,0},{64,32},{96,64},{128,96},{160,128},{192,160},{224,1... | collective-permute-start | bytes 368648 | tf_op jit(solution)/shard_map/ppermute | solution.py:63
  53.5 8.1 %collective-permute-start.16 = (bf16[32,8,240]{2,1,0:T(8,128)(2,1)S(1)}, bf16[32,8,240]{2,1,0:T(8,128)(2,1)S(1)}, u32[]{:S(2)}, u32[]{:S(2)}) collective-permute-start(bf16[32,8,240]{2,1,0:T(8,128)(2,1)S(1)} %collective-permute-done.15), channel_id=1, source_target_pairs={{0,32},{32,64},{64,96},{96,128},{128,160},{160,192},{192,224},{224... | collective-permute-start | bytes 368648 | tf_op jit(solution)/shard_map/ppermute | solution.py:60
  56.0 8.1 %collective-permute-start.2 = (bf16[32,8,240]{2,1,0:T(8,128)(2,1)S(1)}, bf16[32,8,240]{2,1,0:T(8,128)(2,1)S(1)}, u32[]{:S(2)}, u32[]{:S(2)}) collective-permute-start(bf16[32,8,240]{2,1,0:T(8,128)(2,1)S(1)} %collective-permute-done.1), channel_id=1, source_target_pairs={{0,992},{32,0},{64,32},{96,64},{128,96},{160,128},{192,160},{224,1... | collective-permute-start | bytes 368648 | tf_op jit(solution)/shard_map/ppermute | solution.py:63
  61.6 8.1 %collective-permute-start.17 = (bf16[32,8,240]{2,1,0:T(8,128)(2,1)S(1)}, bf16[32,8,240]{2,1,0:T(8,128)(2,1)S(1)}, u32[]{:S(2)}, u32[]{:S(2)}) collective-permute-start(bf16[32,8,240]{2,1,0:T(8,128)(2,1)S(1)} %collective-permute-done.16), channel_id=1, source_target_pairs={{0,32},{32,64},{64,96},{96,128},{128,160},{160,192},{192,224},{224... | collective-permute-start | bytes 368648 | tf_op jit(solution)/shard_map/ppermute | solution.py:60
  64.0 8.1 %collective-permute-start.3 = (bf16[32,8,240]{2,1,0:T(8,128)(2,1)S(1)}, bf16[32,8,240]{2,1,0:T(8,128)(2,1)S(1)}, u32[]{:S(2)}, u32[]{:S(2)}) collective-permute-start(bf16[32,8,240]{2,1,0:T(8,128)(2,1)S(1)} %collective-permute-done.2), channel_id=1, source_target_pairs={{0,992},{32,0},{64,32},{96,64},{128,96},{160,128},{192,160},{224,1... | collective-permute-start | bytes 368648 | tf_op jit(solution)/shard_map/ppermute | solution.py:63
  69.6 8.1 %collective-permute-start.18 = (bf16[32,8,240]{2,1,0:T(8,128)(2,1)S(1)}, bf16[32,8,240]{2,1,0:T(8,128)(2,1)S(1)}, u32[]{:S(2)}, u32[]{:S(2)}) collective-permute-start(bf16[32,8,240]{2,1,0:T(8,128)(2,1)S(1)} %collective-permute-done.17), channel_id=1, source_target_pairs={{0,32},{32,64},{64,96},{96,128},{128,160},{160,192},{192,224},{224... | collective-permute-start | bytes 368648 | tf_op jit(solution)/shard_map/ppermute | solution.py:60
  72.1 8.1 %collective-permute-start.4 = (bf16[32,8,240]{2,1,0:T(8,128)(2,1)S(1)}, bf16[32,8,240]{2,1,0:T(8,128)(2,1)S(1)}, u32[]{:S(2)}, u32[]{:S(2)}) collective-permute-start(bf16[32,8,240]{2,1,0:T(8,128)(2,1)S(1)} %collective-permute-done.3), channel_id=1, source_target_pairs={{0,992},{32,0},{64,32},{96,64},{128,96},{160,128},{192,160},{224,1... | collective-permute-start | bytes 368648 | tf_op jit(solution)/shard_map/ppermute | solution.py:63
  77.7 8.1 %collective-permute-start.19 = (bf16[32,8,240]{2,1,0:T(8,128)(2,1)S(1)}, bf16[32,8,240]{2,1,0:T(8,128)(2,1)S(1)}, u32[]{:S(2)}, u32[]{:S(2)}) collective-permute-start(bf16[32,8,240]{2,1,0:T(8,128)(2,1)S(1)} %collective-permute-done.18), channel_id=1, source_target_pairs={{0,32},{32,64},{64,96},{96,128},{128,160},{160,192},{192,224},{224... | collective-permute-start | bytes 368648 | tf_op jit(solution)/shard_map/ppermute | solution.py:60
  80.2 8.4 %collective-permute-start.5 = (bf16[32,8,240]{2,1,0:T(8,128)(2,1)S(1)}, bf16[32,8,240]{2,1,0:T(8,128)(2,1)S(1)}, u32[]{:S(2)}, u32[]{:S(2)}) collective-permute-start(bf16[32,8,240]{2,1,0:T(8,128)(2,1)S(1)} %collective-permute-done.4), channel_id=1, source_target_pairs={{0,992},{32,0},{64,32},{96,64},{128,96},{160,128},{192,160},{224,1... | collective-permute-start | bytes 368648 | tf_op jit(solution)/shard_map/ppermute | solution.py:63
  85.7 8.8 %collective-permute-start.20 = (bf16[32,8,240]{2,1,0:T(8,128)(2,1)S(1)}, bf16[32,8,240]{2,1,0:T(8,128)(2,1)S(1)}, u32[]{:S(2)}, u32[]{:S(2)}) collective-permute-start(bf16[32,8,240]{2,1,0:T(8,128)(2,1)S(1)} %collective-permute-done.19), channel_id=1, source_target_pairs={{0,32},{32,64},{64,96},{96,128},{128,160},{160,192},{192,224},{224... | collective-permute-start | bytes 368648 | tf_op jit(solution)/shard_map/ppermute | solution.py:60
  88.6 9.3 %collective-permute-start.6 = (bf16[32,8,240]{2,1,0:T(8,128)(2,1)S(1)}, bf16[32,8,240]{2,1,0:T(8,128)(2,1)S(1)}, u32[]{:S(2)}, u32[]{:S(2)}) collective-permute-start(bf16[32,8,240]{2,1,0:T(8,128)(2,1)S(1)} %collective-permute-done.5), channel_id=1, source_target_pairs={{0,992},{32,0},{64,32},{96,64},{128,96},{160,128},{192,160},{224,1... | collective-permute-start | bytes 368648 | tf_op jit(solution)/shard_map/ppermute | solution.py:63
  94.5 9.4 %collective-permute-start.21 = (bf16[32,8,240]{2,1,0:T(8,128)(2,1)S(1)}, bf16[32,8,240]{2,1,0:T(8,128)(2,1)S(1)}, u32[]{:S(2)}, u32[]{:S(2)}) collective-permute-start(bf16[32,8,240]{2,1,0:T(8,128)(2,1)S(1)} %collective-permute-done.20), channel_id=1, source_target_pairs={{0,32},{32,64},{64,96},{96,128},{128,160},{160,192},{192,224},{224... | collective-permute-start | bytes 368648 | tf_op jit(solution)/shard_map/ppermute | solution.py:60
  97.9 8.6 %collective-permute-start.7 = (bf16[32,8,240]{2,1,0:T(8,128)(2,1)S(1)}, bf16[32,8,240]{2,1,0:T(8,128)(2,1)S(1)}, u32[]{:S(2)}, u32[]{:S(2)}) collective-permute-start(bf16[32,8,240]{2,1,0:T(8,128)(2,1)S(1)} %collective-permute-done.6), channel_id=1, source_target_pairs={{0,992},{32,0},{64,32},{96,64},{128,96},{160,128},{192,160},{224,1... | collective-permute-start | bytes 368648 | tf_op jit(solution)/shard_map/ppermute | solution.py:63
  103.9 8.6 %collective-permute-start.22 = (bf16[32,8,240]{2,1,0:T(8,128)(2,1)S(1)}, bf16[32,8,240]{2,1,0:T(8,128)(2,1)S(1)}, u32[]{:S(2)}, u32[]{:S(2)}) collective-permute-start(bf16[32,8,240]{2,1,0:T(8,128)(2,1)S(1)} %collective-permute-done.21), channel_id=1, source_target_pairs={{0,32},{32,64},{64,96},{96,128},{128,160},{160,192},{192,224},{224... | collective-permute-start | bytes 368648 | tf_op jit(solution)/shard_map/ppermute | solution.py:60
  106.5 8.1 %collective-permute-start.8 = (bf16[32,8,240]{2,1,0:T(8,128)(2,1)S(1)}, bf16[32,8,240]{2,1,0:T(8,128)(2,1)S(1)}, u32[]{:S(2)}, u32[]{:S(2)}) collective-permute-start(bf16[32,8,240]{2,1,0:T(8,128)(2,1)S(1)} %collective-permute-done.7), channel_id=1, source_target_pairs={{0,992},{32,0},{64,32},{96,64},{128,96},{160,128},{192,160},{224,1... | collective-permute-start | bytes 368648 | tf_op jit(solution)/shard_map/ppermute | solution.py:63
  112.5 8.1 %collective-permute-start.23 = (bf16[32,8,240]{2,1,0:T(8,128)(2,1)S(1)}, bf16[32,8,240]{2,1,0:T(8,128)(2,1)S(1)}, u32[]{:S(2)}, u32[]{:S(2)}) collective-permute-start(bf16[32,8,240]{2,1,0:T(8,128)(2,1)S(1)} %collective-permute-done.22), channel_id=1, source_target_pairs={{0,32},{32,64},{64,96},{96,128},{128,160},{160,192},{192,224},{224... | collective-permute-start | bytes 368648 | tf_op jit(solution)/shard_map/ppermute | solution.py:60
  114.6 8.1 %collective-permute-start.9 = (bf16[32,8,240]{2,1,0:T(8,128)(2,1)S(1)}, bf16[32,8,240]{2,1,0:T(8,128)(2,1)S(1)}, u32[]{:S(2)}, u32[]{:S(2)}) collective-permute-start(bf16[32,8,240]{2,1,0:T(8,128)(2,1)S(1)} %collective-permute-done.8), channel_id=1, source_target_pairs={{0,992},{32,0},{64,32},{96,64},{128,96},{160,128},{192,160},{224,1... | collective-permute-start | bytes 368648 | tf_op jit(solution)/shard_map/ppermute | solution.py:63
  120.6 8.1 %collective-permute-start.24 = (bf16[32,8,240]{2,1,0:T(8,128)(2,1)S(1)}, bf16[32,8,240]{2,1,0:T(8,128)(2,1)S(1)}, u32[]{:S(2)}, u32[]{:S(2)}) collective-permute-start(bf16[32,8,240]{2,1,0:T(8,128)(2,1)S(1)} %collective-permute-done.23), channel_id=1, source_target_pairs={{0,32},{32,64},{64,96},{96,128},{128,160},{160,192},{192,224},{224... | collective-permute-start | bytes 368648 | tf_op jit(solution)/shard_map/ppermute | solution.py:60
  122.7 8.1 %collective-permute-start.10 = (bf16[32,8,240]{2,1,0:T(8,128)(2,1)S(1)}, bf16[32,8,240]{2,1,0:T(8,128)(2,1)S(1)}, u32[]{:S(2)}, u32[]{:S(2)}) collective-permute-start(bf16[32,8,240]{2,1,0:T(8,128)(2,1)S(1)} %collective-permute-done.9), channel_id=1, source_target_pairs={{0,992},{32,0},{64,32},{96,64},{128,96},{160,128},{192,160},{224,1... | collective-permute-start | bytes 368648 | tf_op jit(solution)/shard_map/ppermute | solution.py:63
  128.6 8.1 %collective-permute-start.25 = (bf16[32,8,240]{2,1,0:T(8,128)(2,1)S(1)}, bf16[32,8,240]{2,1,0:T(8,128)(2,1)S(1)}, u32[]{:S(2)}, u32[]{:S(2)}) collective-permute-start(bf16[32,8,240]{2,1,0:T(8,128)(2,1)S(1)} %collective-permute-done.24), channel_id=1, source_target_pairs={{0,32},{32,64},{64,96},{96,128},{128,160},{160,192},{192,224},{224... | collective-permute-start | bytes 368648 | tf_op jit(solution)/shard_map/ppermute | solution.py:60
  130.7 8.1 %collective-permute-start.11 = (bf16[32,8,240]{2,1,0:T(8,128)(2,1)S(1)}, bf16[32,8,240]{2,1,0:T(8,128)(2,1)S(1)}, u32[]{:S(2)}, u32[]{:S(2)}) collective-permute-start(bf16[32,8,240]{2,1,0:T(8,128)(2,1)S(1)} %collective-permute-done.10), channel_id=1, source_target_pairs={{0,992},{32,0},{64,32},{96,64},{128,96},{160,128},{192,160},{224,1... | collective-permute-start | bytes 368648 | tf_op jit(solution)/shard_map/ppermute | solution.py:63
  136.7 8.1 %collective-permute-start.26 = (bf16[32,8,240]{2,1,0:T(8,128)(2,1)S(1)}, bf16[32,8,240]{2,1,0:T(8,128)(2,1)S(1)}, u32[]{:S(2)}, u32[]{:S(2)}) collective-permute-start(bf16[32,8,240]{2,1,0:T(8,128)(2,1)S(1)} %collective-permute-done.25), channel_id=1, source_target_pairs={{0,32},{32,64},{64,96},{96,128},{128,160},{160,192},{192,224},{224... | collective-permute-start | bytes 368648 | tf_op jit(solution)/shard_map/ppermute | solution.py:60
  138.8 8.6 %collective-permute-start.12 = (bf16[32,8,240]{2,1,0:T(8,128)(2,1)S(1)}, bf16[32,8,240]{2,1,0:T(8,128)(2,1)S(1)}, u32[]{:S(2)}, u32[]{:S(2)}) collective-permute-start(bf16[32,8,240]{2,1,0:T(8,128)(2,1)S(1)} %collective-permute-done.11), channel_id=1, source_target_pairs={{0,992},{32,0},{64,32},{96,64},{128,96},{160,128},{192,160},{224,1... | collective-permute-start | bytes 368648 | tf_op jit(solution)/shard_map/ppermute | solution.py:63
  144.7 8.9 %collective-permute-start.27 = (bf16[32,8,240]{2,1,0:T(8,128)(2,1)S(1)}, bf16[32,8,240]{2,1,0:T(8,128)(2,1)S(1)}, u32[]{:S(2)}, u32[]{:S(2)}) collective-permute-start(bf16[32,8,240]{2,1,0:T(8,128)(2,1)S(1)} %collective-permute-done.26), channel_id=1, source_target_pairs={{0,32},{32,64},{64,96},{96,128},{128,160},{160,192},{192,224},{224... | collective-permute-start | bytes 368648 | tf_op jit(solution)/shard_map/ppermute | solution.py:60
  147.4 8.3 %collective-permute-start.13 = (bf16[32,8,240]{2,1,0:T(8,128)(2,1)S(1)}, bf16[32,8,240]{2,1,0:T(8,128)(2,1)S(1)}, u32[]{:S(2)}, u32[]{:S(2)}) collective-permute-start(bf16[32,8,240]{2,1,0:T(8,128)(2,1)S(1)} %collective-permute-done.12), channel_id=1, source_target_pairs={{0,992},{32,0},{64,32},{96,64},{128,96},{160,128},{192,160},{224,1... | collective-permute-start | bytes 368648 | tf_op jit(solution)/shard_map/ppermute | solution.py:63
  153.7 8.8 %collective-permute-start.28 = (bf16[32,8,240]{2,1,0:T(8,128)(2,1)S(1)}, bf16[32,8,240]{2,1,0:T(8,128)(2,1)S(1)}, u32[]{:S(2)}, u32[]{:S(2)}) collective-permute-start(bf16[32,8,240]{2,1,0:T(8,128)(2,1)S(1)} %collective-permute-done.27), channel_id=1, source_target_pairs={{0,32},{32,64},{64,96},{96,128},{128,160},{160,192},{192,224},{224... | collective-permute-start | bytes 368648 | tf_op jit(solution)/shard_map/ppermute | solution.py:60
  155.6 17.1 %collective-permute-start.14 = (bf16[32,8,240]{2,1,0:T(8,128)(2,1)S(1)}, bf16[32,8,240]{2,1,0:T(8,128)(2,1)S(1)}, u32[]{:S(2)}, u32[]{:S(2)}) collective-permute-start(bf16[32,8,240]{2,1,0:T(8,128)(2,1)S(1)} %collective-permute-done.13), channel_id=1, source_target_pairs={{0,992},{32,0},{64,32},{96,64},{128,96},{160,128},{192,160},{224,1... | collective-permute-start | bytes 368648 | tf_op jit(solution)/shard_map/ppermute | solution.py:63
  162.5 8.1 %collective-permute-start.29 = (bf16[32,8,240]{2,1,0:T(8,128)(2,1)S(1)}, bf16[32,8,240]{2,1,0:T(8,128)(2,1)S(1)}, u32[]{:S(2)}, u32[]{:S(2)}) collective-permute-start(bf16[32,8,240]{2,1,0:T(8,128)(2,1)S(1)} %collective-permute-done.28), channel_id=1, source_target_pairs={{0,32},{32,64},{64,96},{96,128},{128,160},{160,192},{192,224},{224... | collective-permute-start | bytes 368648 | tf_op jit(solution)/shard_map/ppermute | solution.py:60
  170.6 8.1 %collective-permute-start.30 = (bf16[32,8,240]{2,1,0:T(8,128)(2,1)S(1)}, bf16[32,8,240]{2,1,0:T(8,128)(2,1)S(1)}, u32[]{:S(2)}, u32[]{:S(2)}) collective-permute-start(bf16[32,8,240]{2,1,0:T(8,128)(2,1)S(1)} %collective-permute-done.29), channel_id=1, source_target_pairs={{0,32},{32,64},{64,96},{96,128},{128,160},{160,192},{192,224},{224... | collective-permute-start | bytes 368648 | tf_op jit(solution)/shard_map/ppermute | solution.py:60
  178.9 2.1 copy-start
Sparse Core Ops, SparseCore 0:
  11.6 91.7 all-gather.1

commit v4 on v3

--- a/solution.py
+++ b/solution.py
@@ -18,10 +18,8 @@
     destination = ids // EXP_DEV
     local = ids % EXP_DEV
     entry = jnp.arange(per_block, dtype=jnp.int32)
-    earlier = entry[None, :] < entry[:, None]
-    same = destination[..., :, None] == destination[..., None, :]
-    rank = jnp.sum((same & earlier).astype(jnp.int32), axis=-1)
     mine = destination == me_exp
+    rank = jnp.cumsum(mine.astype(jnp.int32), axis=-1) - mine.astype(jnp.int32)
     select = mine[:, :, None, :] & (
         rank[:, :, None, :] == jnp.arange(capacity, dtype=jnp.int32)[None, None, :, None]
     )

time: 270 us -> 248 us (0.919)
  other arithmetic: 43.4 us -> 20.9 us
    reduce_sum x1 -> x0, other arithmetic: 29.7 us -> none  [slot_tables(): rank = jnp.sum((same & earlier).astype(jnp.int32), axis=-1)]
    another operation x0 -> x1, other arithmetic: none -> 7.21 us  [slot_tables(): rank = jnp.cumsum(mine.astype(jnp.int32), axis=-1) - mine.astype(jnp.int32)]
  transfers between devices with their start and end apart: 33 -> 33, of which waited for: 25 -> 25; matrix products, arithmetic and copies ran while one was open for 22% -> 15% of each run, Pallas kernels for 0% -> 0%
where the time goes in v4:
time: 248 us; the launch traced here: 247 us
  starting transfers between devices  135 us (54%)
  local copies, waits for them, and re-layouts  34.4 us (14%)
  waiting for transfers between devices  31.4 us (13%)
  other arithmetic  20.9 us (8%)
  between operations  14.1 us (6%)
  matrix products  11 us (4%)
    ppermute x15, starting transfers between devices, per_device(): bwd = lax.ppermute(bwd, 'expert', bwd_perm)  87.2 us
    ppermute x16, starting transfers between devices, per_device(): fwd = lax.ppermute(fwd, 'expert', fwd_perm)  30.7 us
    ppermute x16, waiting for transfers between devices, per_device(): fwd = lax.ppermute(fwd, 'expert', fwd_perm)  17.1 us
    all_to_all x1, starting transfers between devices, per_device(): cols = lax.all_to_all(cols, 'dp', 0, 0, tiled=True)  16.7 us
    gather x1, local copies, waits for them, and re-layouts, per_device(): grad_rows = jnp.take(tokens, token, axis=0, mode='clip')[:, :width]  12.5 us
    dot_general x1, matrix products, per_device(): lax.dot_general(spread, grad_rows, (((0,), (0,)), ((), ())), preferred_el...  11 us
    convert_element_type x1, local copies, waits for them, and re-layouts, per_device(): rows = (weight[:, None] * hidden.astype(jnp.float32)).astype(jnp.bfloat16)  8.63 us
    ppermute x15, waiting for transfers between devices, per_device(): bwd = lax.ppermute(bwd, 'expert', bwd_perm)  7.61 us
  transfers between devices with their start and end apart: 33, of which 25 were waited for; matrix products, arithmetic and copies ran while one was open for 15% of the time, Pallas kernels for 0%

profile of v4, /device:TPU:2, one launch (start us, length us, event | category | flops | bytes accessed | tf_op | source)
XLA Modules:
  0.0 246.6 jit_solution(5327680958023967260)
XLA Ops:
  6.5 1.1 copy.68
  7.6 0.8 reshape.282
  8.5 1.1 reshape.279
  9.7 0.7 convert_element_type.26
  10.4 0.8 pad_maximum_fusion.1
  11.2 0.7 pad_maximum_fusion
  11.9 16.7 %all-to-all-start = ((bf16[32,8,240]{2,1,0:T(8,128)(2,1)}), bf16[32,8,240]{2,1,0:T(8,128)(2,1)S(1)}, u32[]{:S(2)}, u32[]{:S(2)}) async-start(bf16[32,8,240]{2,1,0:T(8,128)(2,1)} %pad_maximum_fusion), calls=%async_computation | async-start | bytes 262144 | tf_op jit(solution)/shard_map/all_to_all | solution.py:48
  28.7 6.6 %all-to-all-done = bf16[32,8,240]{2,1,0:T(8,128)(2,1)S(1)} async-done(((bf16[32,8,240]{2,1,0:T(8,128)(2,1)}), bf16[32,8,240]{2,1,0:T(8,128)(2,1)S(1)}, u32[]{:S(2)}, u32[]{:S(2)}) %all-to-all-start) | async-done | bytes 122912 | tf_op jit(solution)/shard_map/all_to_all | solution.py:48
  35.3 9.5 %collective-permute-start = (bf16[32,8,240]{2,1,0:T(8,128)(2,1)S(1)}, bf16[32,8,240]{2,1,0:T(8,128)(2,1)S(1)}, u32[]{:S(2)}, u32[]{:S(2)}) collective-permute-start(bf16[32,8,240]{2,1,0:T(8,128)(2,1)S(1)} %all-to-all-done), channel_id=1, source_target_pairs={{0,992},{32,0},{64,32},{96,64},{128,96},{160,128},{192,160},{224,1... | collective-permute-start | bytes 368648 | tf_op jit(solution)/shard_map/ppermute | solution.py:61
  44.8 1.9 collective-permute-start.15
  46.8 1.1 collective-permute-done
  47.9 5.6 %collective-permute-start.1 = (bf16[32,8,240]{2,1,0:T(8,128)(2,1)S(1)}, bf16[32,8,240]{2,1,0:T(8,128)(2,1)S(1)}, u32[]{:S(2)}, u32[]{:S(2)}) collective-permute-start(bf16[32,8,240]{2,1,0:T(8,128)(2,1)S(1)} %collective-permute-done), channel_id=1, source_target_pairs={{0,992},{32,0},{64,32},{96,64},{128,96},{160,128},{192,160},{224,1... | collective-permute-start | bytes 368648 | tf_op jit(solution)/shard_map/ppermute | solution.py:61
  53.5 1.9 collective-permute-start.16
  55.4 0.5 collective-permute-done.1
  56.0 5.6 %collective-permute-start.2 = (bf16[32,8,240]{2,1,0:T(8,128)(2,1)S(1)}, bf16[32,8,240]{2,1,0:T(8,128)(2,1)S(1)}, u32[]{:S(2)}, u32[]{:S(2)}) collective-permute-start(bf16[32,8,240]{2,1,0:T(8,128)(2,1)S(1)} %collective-permute-done.1), channel_id=1, source_target_pairs={{0,992},{32,0},{64,32},{96,64},{128,96},{160,128},{192,160},{224,1... | collective-permute-start | bytes 368648 | tf_op jit(solution)/shard_map/ppermute | solution.py:61
  61.6 1.9 collective-permute-start.17
  63.5 0.5 collective-permute-done.2
  64.0 5.6 %collective-permute-start.3 = (bf16[32,8,240]{2,1,0:T(8,128)(2,1)S(1)}, bf16[32,8,240]{2,1,0:T(8,128)(2,1)S(1)}, u32[]{:S(2)}, u32[]{:S(2)}) collective-permute-start(bf16[32,8,240]{2,1,0:T(8,128)(2,1)S(1)} %collective-permute-done.2), channel_id=1, source_target_pairs={{0,992},{32,0},{64,32},{96,64},{128,96},{160,128},{192,160},{224,1... | collective-permute-start | bytes 368648 | tf_op jit(solution)/shard_map/ppermute | solution.py:61
  69.6 1.9 collective-permute-start.18
  71.6 0.5 collective-permute-done.3
  72.1 5.6 %collective-permute-start.4 = (bf16[32,8,240]{2,1,0:T(8,128)(2,1)S(1)}, bf16[32,8,240]{2,1,0:T(8,128)(2,1)S(1)}, u32[]{:S(2)}, u32[]{:S(2)}) collective-permute-start(bf16[32,8,240]{2,1,0:T(8,128)(2,1)S(1)} %collective-permute-done.3), channel_id=1, source_target_pairs={{0,992},{32,0},{64,32},{96,64},{128,96},{160,128},{192,160},{224,1... | collective-permute-start | bytes 368648 | tf_op jit(solution)/shard_map/ppermute | solution.py:61
  77.7 1.9 collective-permute-start.19
  79.6 0.5 collective-permute-done.4
  80.2 5.6 %collective-permute-start.5 = (bf16[32,8,240]{2,1,0:T(8,128)(2,1)S(1)}, bf16[32,8,240]{2,1,0:T(8,128)(2,1)S(1)}, u32[]{:S(2)}, u32[]{:S(2)}) collective-permute-start(bf16[32,8,240]{2,1,0:T(8,128)(2,1)S(1)} %collective-permute-done.4), channel_id=1, source_target_pairs={{0,992},{32,0},{64,32},{96,64},{128,96},{160,128},{192,160},{224,1... | collective-permute-start | bytes 368648 | tf_op jit(solution)/shard_map/ppermute | solution.py:61
  85.7 1.9 collective-permute-start.20
  87.7 0.9 collective-permute-done.5
  88.6 5.6 %collective-permute-start.6 = (bf16[32,8,240]{2,1,0:T(8,128)(2,1)S(1)}, bf16[32,8,240]{2,1,0:T(8,128)(2,1)S(1)}, u32[]{:S(2)}, u32[]{:S(2)}) collective-permute-start(bf16[32,8,240]{2,1,0:T(8,128)(2,1)S(1)} %collective-permute-done.5), channel_id=1, source_target_pairs={{0,992},{32,0},{64,32},{96,64},{128,96},{160,128},{192,160},{224,1... | collective-permute-start | bytes 368648 | tf_op jit(solution)/shard_map/ppermute | solution.py:61
  94.5 1.9 collective-permute-start.21
  96.4 1.5 collective-permute-done.6
  97.9 5.6 %collective-permute-start.7 = (bf16[32,8,240]{2,1,0:T(8,128)(2,1)S(1)}, bf16[32,8,240]{2,1,0:T(8,128)(2,1)S(1)}, u32[]{:S(2)}, u32[]{:S(2)}) collective-permute-start(bf16[32,8,240]{2,1,0:T(8,128)(2,1)S(1)} %collective-permute-done.6), channel_id=1, source_target_pairs={{0,992},{32,0},{64,32},{96,64},{128,96},{160,128},{192,160},{224,1... | collective-permute-start | bytes 368648 | tf_op jit(solution)/shard_map/ppermute | solution.py:61
  103.9 1.9 collective-permute-start.22
  105.9 0.6 collective-permute-done.7
  106.5 5.6 %collective-permute-start.8 = (bf16[32,8,240]{2,1,0:T(8,128)(2,1)S(1)}, bf16[32,8,240]{2,1,0:T(8,128)(2,1)S(1)}, u32[]{:S(2)}, u32[]{:S(2)}) collective-permute-start(bf16[32,8,240]{2,1,0:T(8,128)(2,1)S(1)} %collective-permute-done.7), channel_id=1, source_target_pairs={{0,992},{32,0},{64,32},{96,64},{128,96},{160,128},{192,160},{224,1... | collective-permute-start | bytes 368648 | tf_op jit(solution)/shard_map/ppermute | solution.py:61
  112.5 1.9 collective-permute-start.23
  114.6 5.6 %collective-permute-start.9 = (bf16[32,8,240]{2,1,0:T(8,128)(2,1)S(1)}, bf16[32,8,240]{2,1,0:T(8,128)(2,1)S(1)}, u32[]{:S(2)}, u32[]{:S(2)}) collective-permute-start(bf16[32,8,240]{2,1,0:T(8,128)(2,1)S(1)} %collective-permute-done.8), channel_id=1, source_target_pairs={{0,992},{32,0},{64,32},{96,64},{128,96},{160,128},{192,160},{224,1... | collective-permute-start | bytes 368648 | tf_op jit(solution)/shard_map/ppermute | solution.py:61
  120.6 1.9 collective-permute-start.24
  122.7 5.6 %collective-permute-start.10 = (bf16[32,8,240]{2,1,0:T(8,128)(2,1)S(1)}, bf16[32,8,240]{2,1,0:T(8,128)(2,1)S(1)}, u32[]{:S(2)}, u32[]{:S(2)}) collective-permute-start(bf16[32,8,240]{2,1,0:T(8,128)(2,1)S(1)} %collective-permute-done.9), channel_id=1, source_target_pairs={{0,992},{32,0},{64,32},{96,64},{128,96},{160,128},{192,160},{224,1... | collective-permute-start | bytes 368648 | tf_op jit(solution)/shard_map/ppermute | solution.py:61
  128.6 1.9 collective-permute-start.25
  130.7 5.6 %collective-permute-start.11 = (bf16[32,8,240]{2,1,0:T(8,128)(2,1)S(1)}, bf16[32,8,240]{2,1,0:T(8,128)(2,1)S(1)}, u32[]{:S(2)}, u32[]{:S(2)}) collective-permute-start(bf16[32,8,240]{2,1,0:T(8,128)(2,1)S(1)} %collective-permute-done.10), channel_id=1, source_target_pairs={{0,992},{32,0},{64,32},{96,64},{128,96},{160,128},{192,160},{224,1... | collective-permute-start | bytes 368648 | tf_op jit(solution)/shard_map/ppermute | solution.py:61
  136.7 1.9 collective-permute-start.26
  138.8 5.6 %collective-permute-start.12 = (bf16[32,8,240]{2,1,0:T(8,128)(2,1)S(1)}, bf16[32,8,240]{2,1,0:T(8,128)(2,1)S(1)}, u32[]{:S(2)}, u32[]{:S(2)}) collective-permute-start(bf16[32,8,240]{2,1,0:T(8,128)(2,1)S(1)} %collective-permute-done.11), channel_id=1, source_target_pairs={{0,992},{32,0},{64,32},{96,64},{128,96},{160,128},{192,160},{224,1... | collective-permute-start | bytes 368648 | tf_op jit(solution)/shard_map/ppermute | solution.py:61
  144.7 1.9 collective-permute-start.27
  146.7 0.7 collective-permute-done.12
  147.4 5.6 %collective-permute-start.13 = (bf16[32,8,240]{2,1,0:T(8,128)(2,1)S(1)}, bf16[32,8,240]{2,1,0:T(8,128)(2,1)S(1)}, u32[]{:S(2)}, u32[]{:S(2)}) collective-permute-start(bf16[32,8,240]{2,1,0:T(8,128)(2,1)S(1)} %collective-permute-done.12), channel_id=1, source_target_pairs={{0,992},{32,0},{64,32},{96,64},{128,96},{160,128},{192,160},{224,1... | collective-permute-start | bytes 368648 | tf_op jit(solution)/shard_map/ppermute | solution.py:61
  153.0 0.7 collective-permute-done.27
  153.7 1.9 collective-permute-start.28
  155.6 5.4 %collective-permute-start.14 = (bf16[32,8,240]{2,1,0:T(8,128)(2,1)S(1)}, bf16[32,8,240]{2,1,0:T(8,128)(2,1)S(1)}, u32[]{:S(2)}, u32[]{:S(2)}) collective-permute-start(bf16[32,8,240]{2,1,0:T(8,128)(2,1)S(1)} %collective-permute-done.13), channel_id=1, source_target_pairs={{0,992},{32,0},{64,32},{96,64},{128,96},{160,128},{192,160},{224,1... | collective-permute-start | bytes 368648 | tf_op jit(solution)/shard_map/ppermute | solution.py:61
  161.0 1.5 collective-permute-done.28
  162.5 1.9 collective-permute-start.29
  164.5 6.1 %collective-permute-done.29 = bf16[32,8,240]{2,1,0:T(8,128)(2,1)S(1)} collective-permute-done((bf16[32,8,240]{2,1,0:T(8,128)(2,1)S(1)}, bf16[32,8,240]{2,1,0:T(8,128)(2,1)S(1)}, u32[]{:S(2)}, u32[]{:S(2)}) %collective-permute-start.29) | collective-permute-done | bytes 122912 | tf_op jit(solution)/shard_map/ppermute | solution.py:58
  170.6 2.1 collective-permute-start.30
  172.7 5.9 %collective-permute-done.30 = bf16[32,8,240]{2,1,0:T(8,128)(2,1)S(1)} collective-permute-done((bf16[32,8,240]{2,1,0:T(8,128)(2,1)S(1)}, bf16[32,8,240]{2,1,0:T(8,128)(2,1)S(1)}, u32[]{:S(2)}, u32[]{:S(2)}) %collective-permute-start.30) | collective-permute-done | bytes 122912 | tf_op jit(solution)/shard_map/ppermute | solution.py:58
  179.0 2.0 copy-done
  181.0 2.0 slice.20
  183.0 2.3 copy.78
  185.3 0.7 gather_fusion
  187.3 7.2 %reduce_window_sum.11 = s32[32,32,64]{2,1,0:T(8,128)S(1)} reduce-window(s32[32,32,64]{2,1,0:T(8,128)S(1)} %get-tuple-element.7, s32[]{:T(128)} %constant.79.clone.1), window={size=1x1x64 pad=0_0x0_0x63_0}, to_apply=%region_0.1 | reduce-window | flops 4128768 | bytes 524292 | tf_op jit(solution)/shard_map/jit(cumsum)/reduce_window_sum | solution.py:22
  194.7 3.4 %select_reduce_fusion = (s32[32,32,3]{1,2,0:T(4,128)S(1)}, s32[32,32,3]{1,2,0:T(4,128)S(1)}) fusion(s32[64]{0:T(128)S(1)} %and_select_fusion, s32[32,32,64]{2,1,0:T(8,128)S(1)} %get-tuple-element.12, pred[32,32,64]{2,1,0:T(8,128)(4,1)S(1)} %get-tuple-element.8, s32[32,32,64]{2,1,0:T(8,128)S(1)} %get-tuple-element.11), kind=kLoop, calls=%fused_computation.11 | loop fusion | flops 1173504 | bytes 614656 | tf_op jit(solution)/shard_map/reduce_sum | solution.py:28
  198.7 0.5 copy.66
  199.2 0.6 select_reduce_fusion.1
  201.0 12.5 %gather_fusion.1 = bf16[3072,240]{1,0:T(8,128)(2,1)S(1)} fusion(bf16[8192,240]{1,0:T(8,128)(2,1)} %bitcast.97, s32[3072]{0:T(1024)S(1)} %broadcast_clamp_fusion), kind=kCustom, calls=%fused_computation.1 | custom fusion | bytes 2961408 | tf_op jit(solution)/shard_map/jit(_take)/gather | solution.py:72
  213.6 6.5 %multiply_convert_fusion = bf16[3072,1024]{1,0:T(8,128)(2,1)} fusion(bf16[3072,1024]{1,0:T(8,128)(2,1)} %all-gather.2.cloned.1.call-done, f32[3072]{0:T(1024)S(1)} %mul.30), kind=kLoop, calls=%fused_computation.8 | loop fusion | flops 9437184 | bytes 12595200 | tf_op jit(solution)/shard_map/convert_element_type | solution.py:71
  220.1 8.6 %copy.69 = bf16[3072,1024]{0,1:T(8,128)(2,1)} copy(bf16[3072,1024]{1,0:T(8,128)(2,1)} %multiply_convert_fusion) | data formatting | bytes 12582912 | tf_op jit(solution)/shard_map/convert_element_type | solution.py:71
  228.7 11.0 %fusion.6 = bf16[4,1024,224]{1,2,0:T(8,128)(2,1)} fusion(pred[3072,4]{0,1:T(4,128)(4,1)S(1)} %iota_compare_fusion.1, bf16[3072,1024]{0,1:T(8,128)(2,1)} %copy.69, bf16[3072,240]{1,0:T(8,128)(2,1)S(1)} %gather_fusion.1), kind=kOutput, calls=%fused_computation.9 | convolution fusion | flops 5650644992 | bytes 9613312 | tf_op jit(solution)/shard_map/dot_general | solution.py:76
  (77 shorter events, 7.1 us)
Async XLA Ops:
  6.5 207.0 %all-gather.2.cloned.1.call-start = ((), (), s32[]{:S(2)}) async-start(), calls=%async_computation.1 | async-start | bytes 6488064 | tf_op jit(solution)/shard_map/all_gather | solution.py:41
  11.9 23.4 %all-to-all-start = ((bf16[32,8,240]{2,1,0:T(8,128)(2,1)}), bf16[32,8,240]{2,1,0:T(8,128)(2,1)S(1)}, u32[]{:S(2)}, u32[]{:S(2)}) async-start(bf16[32,8,240]{2,1,0:T(8,128)(2,1)} %pad_maximum_fusion), calls=%async_computation | async-start | bytes 262144 | tf_op jit(solution)/shard_map/all_to_all | solution.py:48
  35.3 12.5 %collective-permute-start = (bf16[32,8,240]{2,1,0:T(8,128)(2,1)S(1)}, bf16[32,8,240]{2,1,0:T(8,128)(2,1)S(1)}, u32[]{:S(2)}, u32[]{:S(2)}) collective-permute-start(bf16[32,8,240]{2,1,0:T(8,128)(2,1)S(1)} %all-to-all-done), channel_id=1, source_target_pairs={{0,992},{32,0},{64,32},{96,64},{128,96},{160,128},{192,160},{224,1... | collective-permute-start | bytes 368648 | tf_op jit(solution)/shard_map/ppermute | solution.py:61
  44.8 8.7 %collective-permute-start.15 = (bf16[32,8,240]{2,1,0:T(8,128)(2,1)S(1)}, bf16[32,8,240]{2,1,0:T(8,128)(2,1)S(1)}, u32[]{:S(2)}, u32[]{:S(2)}) collective-permute-start(bf16[32,8,240]{2,1,0:T(8,128)(2,1)S(1)} %all-to-all-done), channel_id=1, source_target_pairs={{0,32},{32,64},{64,96},{96,128},{128,160},{160,192},{192,224},{224... | collective-permute-start | bytes 368648 | tf_op jit(solution)/shard_map/ppermute | solution.py:58
  47.9 8.1 %collective-permute-start.1 = (bf16[32,8,240]{2,1,0:T(8,128)(2,1)S(1)}, bf16[32,8,240]{2,1,0:T(8,128)(2,1)S(1)}, u32[]{:S(2)}, u32[]{:S(2)}) collective-permute-start(bf16[32,8,240]{2,1,0:T(8,128)(2,1)S(1)} %collective-permute-done), channel_id=1, source_target_pairs={{0,992},{32,0},{64,32},{96,64},{128,96},{160,128},{192,160},{224,1... | collective-permute-start | bytes 368648 | tf_op jit(solution)/shard_map/ppermute | solution.py:61
  53.5 8.1 %collective-permute-start.16 = (bf16[32,8,240]{2,1,0:T(8,128)(2,1)S(1)}, bf16[32,8,240]{2,1,0:T(8,128)(2,1)S(1)}, u32[]{:S(2)}, u32[]{:S(2)}) collective-permute-start(bf16[32,8,240]{2,1,0:T(8,128)(2,1)S(1)} %collective-permute-done.15), channel_id=1, source_target_pairs={{0,32},{32,64},{64,96},{96,128},{128,160},{160,192},{192,224},{224... | collective-permute-start | bytes 368648 | tf_op jit(solution)/shard_map/ppermute | solution.py:58
  56.0 8.1 %collective-permute-start.2 = (bf16[32,8,240]{2,1,0:T(8,128)(2,1)S(1)}, bf16[32,8,240]{2,1,0:T(8,128)(2,1)S(1)}, u32[]{:S(2)}, u32[]{:S(2)}) collective-permute-start(bf16[32,8,240]{2,1,0:T(8,128)(2,1)S(1)} %collective-permute-done.1), channel_id=1, source_target_pairs={{0,992},{32,0},{64,32},{96,64},{128,96},{160,128},{192,160},{224,1... | collective-permute-start | bytes 368648 | tf_op jit(solution)/shard_map/ppermute | solution.py:61
  61.6 8.1 %collective-permute-start.17 = (bf16[32,8,240]{2,1,0:T(8,128)(2,1)S(1)}, bf16[32,8,240]{2,1,0:T(8,128)(2,1)S(1)}, u32[]{:S(2)}, u32[]{:S(2)}) collective-permute-start(bf16[32,8,240]{2,1,0:T(8,128)(2,1)S(1)} %collective-permute-done.16), channel_id=1, source_target_pairs={{0,32},{32,64},{64,96},{96,128},{128,160},{160,192},{192,224},{224... | collective-permute-start | bytes 368648 | tf_op jit(solution)/shard_map/ppermute | solution.py:58
  64.0 8.1 %collective-permute-start.3 = (bf16[32,8,240]{2,1,0:T(8,128)(2,1)S(1)}, bf16[32,8,240]{2,1,0:T(8,128)(2,1)S(1)}, u32[]{:S(2)}, u32[]{:S(2)}) collective-permute-start(bf16[32,8,240]{2,1,0:T(8,128)(2,1)S(1)} %collective-permute-done.2), channel_id=1, source_target_pairs={{0,992},{32,0},{64,32},{96,64},{128,96},{160,128},{192,160},{224,1... | collective-permute-start | bytes 368648 | tf_op jit(solution)/shard_map/ppermute | solution.py:61
  69.6 8.1 %collective-permute-start.18 = (bf16[32,8,240]{2,1,0:T(8,128)(2,1)S(1)}, bf16[32,8,240]{2,1,0:T(8,128)(2,1)S(1)}, u32[]{:S(2)}, u32[]{:S(2)}) collective-permute-start(bf16[32,8,240]{2,1,0:T(8,128)(2,1)S(1)} %collective-permute-done.17), channel_id=1, source_target_pairs={{0,32},{32,64},{64,96},{96,128},{128,160},{160,192},{192,224},{224... | collective-permute-start | bytes 368648 | tf_op jit(solution)/shard_map/ppermute | solution.py:58
  72.1 8.1 %collective-permute-start.4 = (bf16[32,8,240]{2,1,0:T(8,128)(2,1)S(1)}, bf16[32,8,240]{2,1,0:T(8,128)(2,1)S(1)}, u32[]{:S(2)}, u32[]{:S(2)}) collective-permute-start(bf16[32,8,240]{2,1,0:T(8,128)(2,1)S(1)} %collective-permute-done.3), channel_id=1, source_target_pairs={{0,992},{32,0},{64,32},{96,64},{128,96},{160,128},{192,160},{224,1... | collective-permute-start | bytes 368648 | tf_op jit(solution)/shard_map/ppermute | solution.py:61
  77.7 8.1 %collective-permute-start.19 = (bf16[32,8,240]{2,1,0:T(8,128)(2,1)S(1)}, bf16[32,8,240]{2,1,0:T(8,128)(2,1)S(1)}, u32[]{:S(2)}, u32[]{:S(2)}) collective-permute-start(bf16[32,8,240]{2,1,0:T(8,128)(2,1)S(1)} %collective-permute-done.18), channel_id=1, source_target_pairs={{0,32},{32,64},{64,96},{96,128},{128,160},{160,192},{192,224},{224... | collective-permute-start | bytes 368648 | tf_op jit(solution)/shard_map/ppermute | solution.py:58
  80.2 8.4 %collective-permute-start.5 = (bf16[32,8,240]{2,1,0:T(8,128)(2,1)S(1)}, bf16[32,8,240]{2,1,0:T(8,128)(2,1)S(1)}, u32[]{:S(2)}, u32[]{:S(2)}) collective-permute-start(bf16[32,8,240]{2,1,0:T(8,128)(2,1)S(1)} %collective-permute-done.4), channel_id=1, source_target_pairs={{0,992},{32,0},{64,32},{96,64},{128,96},{160,128},{192,160},{224,1... | collective-permute-start | bytes 368648 | tf_op jit(solution)/shard_map/ppermute | solution.py:61
  85.7 8.8 %collective-permute-start.20 = (bf16[32,8,240]{2,1,0:T(8,128)(2,1)S(1)}, bf16[32,8,240]{2,1,0:T(8,128)(2,1)S(1)}, u32[]{:S(2)}, u32[]{:S(2)}) collective-permute-start(bf16[32,8,240]{2,1,0:T(8,128)(2,1)S(1)} %collective-permute-done.19), channel_id=1, source_target_pairs={{0,32},{32,64},{64,96},{96,128},{128,160},{160,192},{192,224},{224... | collective-permute-start | bytes 368648 | tf_op jit(solution)/shard_map/ppermute | solution.py:58
  88.6 9.3 %collective-permute-start.6 = (bf16[32,8,240]{2,1,0:T(8,128)(2,1)S(1)}, bf16[32,8,240]{2,1,0:T(8,128)(2,1)S(1)}, u32[]{:S(2)}, u32[]{:S(2)}) collective-permute-start(bf16[32,8,240]{2,1,0:T(8,128)(2,1)S(1)} %collective-permute-done.5), channel_id=1, source_target_pairs={{0,992},{32,0},{64,32},{96,64},{128,96},{160,128},{192,160},{224,1... | collective-permute-start | bytes 368648 | tf_op jit(solution)/shard_map/ppermute | solution.py:61
  94.5 9.4 %collective-permute-start.21 = (bf16[32,8,240]{2,1,0:T(8,128)(2,1)S(1)}, bf16[32,8,240]{2,1,0:T(8,128)(2,1)S(1)}, u32[]{:S(2)}, u32[]{:S(2)}) collective-permute-start(bf16[32,8,240]{2,1,0:T(8,128)(2,1)S(1)} %collective-permute-done.20), channel_id=1, source_target_pairs={{0,32},{32,64},{64,96},{96,128},{128,160},{160,192},{192,224},{224... | collective-permute-start | bytes 368648 | tf_op jit(solution)/shard_map/ppermute | solution.py:58
  97.9 8.6 %collective-permute-start.7 = (bf16[32,8,240]{2,1,0:T(8,128)(2,1)S(1)}, bf16[32,8,240]{2,1,0:T(8,128)(2,1)S(1)}, u32[]{:S(2)}, u32[]{:S(2)}) collective-permute-start(bf16[32,8,240]{2,1,0:T(8,128)(2,1)S(1)} %collective-permute-done.6), channel_id=1, source_target_pairs={{0,992},{32,0},{64,32},{96,64},{128,96},{160,128},{192,160},{224,1... | collective-permute-start | bytes 368648 | tf_op jit(solution)/shard_map/ppermute | solution.py:61
  103.9 8.6 %collective-permute-start.22 = (bf16[32,8,240]{2,1,0:T(8,128)(2,1)S(1)}, bf16[32,8,240]{2,1,0:T(8,128)(2,1)S(1)}, u32[]{:S(2)}, u32[]{:S(2)}) collective-permute-start(bf16[32,8,240]{2,1,0:T(8,128)(2,1)S(1)} %collective-permute-done.21), channel_id=1, source_target_pairs={{0,32},{32,64},{64,96},{96,128},{128,160},{160,192},{192,224},{224... | collective-permute-start | bytes 368648 | tf_op jit(solution)/shard_map/ppermute | solution.py:58
  106.5 8.1 %collective-permute-start.8 = (bf16[32,8,240]{2,1,0:T(8,128)(2,1)S(1)}, bf16[32,8,240]{2,1,0:T(8,128)(2,1)S(1)}, u32[]{:S(2)}, u32[]{:S(2)}) collective-permute-start(bf16[32,8,240]{2,1,0:T(8,128)(2,1)S(1)} %collective-permute-done.7), channel_id=1, source_target_pairs={{0,992},{32,0},{64,32},{96,64},{128,96},{160,128},{192,160},{224,1... | collective-permute-start | bytes 368648 | tf_op jit(solution)/shard_map/ppermute | solution.py:61
  112.5 8.1 %collective-permute-start.23 = (bf16[32,8,240]{2,1,0:T(8,128)(2,1)S(1)}, bf16[32,8,240]{2,1,0:T(8,128)(2,1)S(1)}, u32[]{:S(2)}, u32[]{:S(2)}) collective-permute-start(bf16[32,8,240]{2,1,0:T(8,128)(2,1)S(1)} %collective-permute-done.22), channel_id=1, source_target_pairs={{0,32},{32,64},{64,96},{96,128},{128,160},{160,192},{192,224},{224... | collective-permute-start | bytes 368648 | tf_op jit(solution)/shard_map/ppermute | solution.py:58
  114.6 8.1 %collective-permute-start.9 = (bf16[32,8,240]{2,1,0:T(8,128)(2,1)S(1)}, bf16[32,8,240]{2,1,0:T(8,128)(2,1)S(1)}, u32[]{:S(2)}, u32[]{:S(2)}) collective-permute-start(bf16[32,8,240]{2,1,0:T(8,128)(2,1)S(1)} %collective-permute-done.8), channel_id=1, source_target_pairs={{0,992},{32,0},{64,32},{96,64},{128,96},{160,128},{192,160},{224,1... | collective-permute-start | bytes 368648 | tf_op jit(solution)/shard_map/ppermute | solution.py:61
  120.6 8.1 %collective-permute-start.24 = (bf16[32,8,240]{2,1,0:T(8,128)(2,1)S(1)}, bf16[32,8,240]{2,1,0:T(8,128)(2,1)S(1)}, u32[]{:S(2)}, u32[]{:S(2)}) collective-permute-start(bf16[32,8,240]{2,1,0:T(8,128)(2,1)S(1)} %collective-permute-done.23), channel_id=1, source_target_pairs={{0,32},{32,64},{64,96},{96,128},{128,160},{160,192},{192,224},{224... | collective-permute-start | bytes 368648 | tf_op jit(solution)/shard_map/ppermute | solution.py:58
  122.7 8.1 %collective-permute-start.10 = (bf16[32,8,240]{2,1,0:T(8,128)(2,1)S(1)}, bf16[32,8,240]{2,1,0:T(8,128)(2,1)S(1)}, u32[]{:S(2)}, u32[]{:S(2)}) collective-permute-start(bf16[32,8,240]{2,1,0:T(8,128)(2,1)S(1)} %collective-permute-done.9), channel_id=1, source_target_pairs={{0,992},{32,0},{64,32},{96,64},{128,96},{160,128},{192,160},{224,1... | collective-permute-start | bytes 368648 | tf_op jit(solution)/shard_map/ppermute | solution.py:61
  128.6 8.1 %collective-permute-start.25 = (bf16[32,8,240]{2,1,0:T(8,128)(2,1)S(1)}, bf16[32,8,240]{2,1,0:T(8,128)(2,1)S(1)}, u32[]{:S(2)}, u32[]{:S(2)}) collective-permute-start(bf16[32,8,240]{2,1,0:T(8,128)(2,1)S(1)} %collective-permute-done.24), channel_id=1, source_target_pairs={{0,32},{32,64},{64,96},{96,128},{128,160},{160,192},{192,224},{224... | collective-permute-start | bytes 368648 | tf_op jit(solution)/shard_map/ppermute | solution.py:58
  130.7 8.1 %collective-permute-start.11 = (bf16[32,8,240]{2,1,0:T(8,128)(2,1)S(1)}, bf16[32,8,240]{2,1,0:T(8,128)(2,1)S(1)}, u32[]{:S(2)}, u32[]{:S(2)}) collective-permute-start(bf16[32,8,240]{2,1,0:T(8,128)(2,1)S(1)} %collective-permute-done.10), channel_id=1, source_target_pairs={{0,992},{32,0},{64,32},{96,64},{128,96},{160,128},{192,160},{224,1... | collective-permute-start | bytes 368648 | tf_op jit(solution)/shard_map/ppermute | solution.py:61
  136.7 8.1 %collective-permute-start.26 = (bf16[32,8,240]{2,1,0:T(8,128)(2,1)S(1)}, bf16[32,8,240]{2,1,0:T(8,128)(2,1)S(1)}, u32[]{:S(2)}, u32[]{:S(2)}) collective-permute-start(bf16[32,8,240]{2,1,0:T(8,128)(2,1)S(1)} %collective-permute-done.25), channel_id=1, source_target_pairs={{0,32},{32,64},{64,96},{96,128},{128,160},{160,192},{192,224},{224... | collective-permute-start | bytes 368648 | tf_op jit(solution)/shard_map/ppermute | solution.py:58
  138.8 8.6 %collective-permute-start.12 = (bf16[32,8,240]{2,1,0:T(8,128)(2,1)S(1)}, bf16[32,8,240]{2,1,0:T(8,128)(2,1)S(1)}, u32[]{:S(2)}, u32[]{:S(2)}) collective-permute-start(bf16[32,8,240]{2,1,0:T(8,128)(2,1)S(1)} %collective-permute-done.11), channel_id=1, source_target_pairs={{0,992},{32,0},{64,32},{96,64},{128,96},{160,128},{192,160},{224,1... | collective-permute-start | bytes 368648 | tf_op jit(solution)/shard_map/ppermute | solution.py:61
  144.7 8.9 %collective-permute-start.27 = (bf16[32,8,240]{2,1,0:T(8,128)(2,1)S(1)}, bf16[32,8,240]{2,1,0:T(8,128)(2,1)S(1)}, u32[]{:S(2)}, u32[]{:S(2)}) collective-permute-start(bf16[32,8,240]{2,1,0:T(8,128)(2,1)S(1)} %collective-permute-done.26), channel_id=1, source_target_pairs={{0,32},{32,64},{64,96},{96,128},{128,160},{160,192},{192,224},{224... | collective-permute-start | bytes 368648 | tf_op jit(solution)/shard_map/ppermute | solution.py:58
  147.4 8.3 %collective-permute-start.13 = (bf16[32,8,240]{2,1,0:T(8,128)(2,1)S(1)}, bf16[32,8,240]{2,1,0:T(8,128)(2,1)S(1)}, u32[]{:S(2)}, u32[]{:S(2)}) collective-permute-start(bf16[32,8,240]{2,1,0:T(8,128)(2,1)S(1)} %collective-permute-done.12), channel_id=1, source_target_pairs={{0,992},{32,0},{64,32},{96,64},{128,96},{160,128},{192,160},{224,1... | collective-permute-start | bytes 368648 | tf_op jit(solution)/shard_map/ppermute | solution.py:61
  153.7 8.8 %collective-permute-start.28 = (bf16[32,8,240]{2,1,0:T(8,128)(2,1)S(1)}, bf16[32,8,240]{2,1,0:T(8,128)(2,1)S(1)}, u32[]{:S(2)}, u32[]{:S(2)}) collective-permute-start(bf16[32,8,240]{2,1,0:T(8,128)(2,1)S(1)} %collective-permute-done.27), channel_id=1, source_target_pairs={{0,32},{32,64},{64,96},{96,128},{128,160},{160,192},{192,224},{224... | collective-permute-start | bytes 368648 | tf_op jit(solution)/shard_map/ppermute | solution.py:58
  155.6 17.1 %collective-permute-start.14 = (bf16[32,8,240]{2,1,0:T(8,128)(2,1)S(1)}, bf16[32,8,240]{2,1,0:T(8,128)(2,1)S(1)}, u32[]{:S(2)}, u32[]{:S(2)}) collective-permute-start(bf16[32,8,240]{2,1,0:T(8,128)(2,1)S(1)} %collective-permute-done.13), channel_id=1, source_target_pairs={{0,992},{32,0},{64,32},{96,64},{128,96},{160,128},{192,160},{224,1... | collective-permute-start | bytes 368648 | tf_op jit(solution)/shard_map/ppermute | solution.py:61
  162.5 8.1 %collective-permute-start.29 = (bf16[32,8,240]{2,1,0:T(8,128)(2,1)S(1)}, bf16[32,8,240]{2,1,0:T(8,128)(2,1)S(1)}, u32[]{:S(2)}, u32[]{:S(2)}) collective-permute-start(bf16[32,8,240]{2,1,0:T(8,128)(2,1)S(1)} %collective-permute-done.28), channel_id=1, source_target_pairs={{0,32},{32,64},{64,96},{96,128},{128,160},{160,192},{192,224},{224... | collective-permute-start | bytes 368648 | tf_op jit(solution)/shard_map/ppermute | solution.py:58
  170.6 8.1 %collective-permute-start.30 = (bf16[32,8,240]{2,1,0:T(8,128)(2,1)S(1)}, bf16[32,8,240]{2,1,0:T(8,128)(2,1)S(1)}, u32[]{:S(2)}, u32[]{:S(2)}) collective-permute-start(bf16[32,8,240]{2,1,0:T(8,128)(2,1)S(1)} %collective-permute-done.29), channel_id=1, source_target_pairs={{0,32},{32,64},{64,96},{96,128},{128,160},{160,192},{192,224},{224... | collective-permute-start | bytes 368648 | tf_op jit(solution)/shard_map/ppermute | solution.py:58
  178.9 2.1 copy-start
Sparse Core Ops, SparseCore 0:
  11.6 91.7 all-gather.1

commit v5 on v4

--- a/solution.py
+++ b/solution.py
@@ -19,7 +19,11 @@
     local = ids % EXP_DEV
     entry = jnp.arange(per_block, dtype=jnp.int32)
     mine = destination == me_exp
-    rank = jnp.cumsum(mine.astype(jnp.int32), axis=-1) - mine.astype(jnp.int32)
+    upper = (entry[:, None] < entry[None, :]).astype(jnp.bfloat16)
+    rank = jnp.dot(
+        mine.astype(jnp.bfloat16).reshape(-1, per_block), upper, preferred_element_type=jnp.float32
+    )
+    rank = rank.astype(jnp.int32).reshape(mine.shape)
     select = mine[:, :, None, :] & (
         rank[:, :, None, :] == jnp.arange(capacity, dtype=jnp.int32)[None, None, :, None]
     )
@@ -68,15 +72,15 @@
     meta_gs = jnp.transpose(meta_src, (1, 0, 2, 3))
     weight, label, token = slot_tables(meta_gs, me_exp, relative, capacity)
 
-    rows = (weight[:, None] * hidden.astype(jnp.float32)).astype(jnp.bfloat16)
+    hidden_t = jnp.transpose(hidden)
+    rows_t = (weight[None, :] * hidden_t.astype(jnp.float32)).astype(jnp.bfloat16)
     grad_rows = jnp.take(tokens, token, axis=0, mode="clip")[:, :width]
     mask = label[:, None] == jnp.arange(EXP_DEV, dtype=jnp.int32)[None, :]
-    spread = jnp.where(mask[:, :, None], rows[:, None, :], jnp.zeros_like(rows)[:, None, :])
-    spread = spread.reshape(rows.shape[0], EXP_DEV * FF)
-    gradient = lax.dot_general(
-        spread, grad_rows, (((0,), (0,)), ((), ())), preferred_element_type=jnp.float32
-    )
-    return gradient.reshape(EXP_DEV, FF, width).astype(jnp.bfloat16)
+    spread = jnp.where(mask[:, :, None], grad_rows[:, None, :], jnp.zeros_like(grad_rows)[:, None, :])
+    spread = spread.reshape(grad_rows.shape[0], EXP_DEV * width)
+    gradient = jnp.dot(rows_t, spread, preferred_element_type=jnp.float32)
+    gradient = gradient.astype(jnp.bfloat16).reshape(FF, EXP_DEV, width)
+    return jnp.transpose(gradient, (1, 0, 2))
 
 
 def solution(mesh):

time: 248 us -> 232 us (0.935)
  other arithmetic: 20.9 us -> 11.1 us
  local copies, waits for them, and re-layouts: 34.4 us -> 28.9 us
    another operation x1 -> x0, other arithmetic: 7.21 us -> none  [slot_tables(): rank = jnp.cumsum(mine.astype(jnp.int32), axis=-1) - mine.astype(jnp.int32)]
    convert_element_type x2 -> x0, other arithmetic: 6.84 us -> none  [the longest x1 6.47 us: per_device(): rows = (weight[:, None] * hidden.astype(jnp.float32)).astype(jnp.bfloat16)]
    convert_element_type x1 -> x2, local copies, waits for them, and re-layouts: 8.63 us -> 1.92 us  [the longest x1 1.73 us: slot_tables(): ids = meta_gs[..., :TOP].astype(jnp.int32).reshape(n_grp, n_src, per_block)]
    select_n x0 -> x1, other arithmetic: none -> 2.79 us  [per_device(): jnp.where(mask[:, :, None], grad_rows[:, None, :], jnp.zeros_like(grad_ro...]
    dot_general x1 -> x2, matrix products: 11 us -> 11.1 us  [the longest x1 10.7 us: per_device(): gradient = jnp.dot(rows_t, spread, preferred_element_type=jnp.float32)]
  transfers between devices with their start and end apart: 33 -> 33, of which waited for: 25 -> 25; matrix products, arithmetic and copies ran while one was open for 15% -> 16% of each run, Pallas kernels for 0% -> 0%
where the time goes in v5:
time: 232 us; the launch traced here: 231 us
  starting transfers between devices  135 us (58%)
  waiting for transfers between devices  31.4 us (14%)
  local copies, waits for them, and re-layouts  28.9 us (12%)
  between operations  14.1 us (6%)
  other arithmetic  11.1 us (5%)
  matrix products  11.1 us (5%)
    ppermute x15, starting transfers between devices, per_device(): bwd = lax.ppermute(bwd, 'expert', bwd_perm)  87.2 us
    ppermute x16, starting transfers between devices, per_device(): fwd = lax.ppermute(fwd, 'expert', fwd_perm)  30.7 us
    ppermute x16, waiting for transfers between devices, per_device(): fwd = lax.ppermute(fwd, 'expert', fwd_perm)  17.1 us
    all_to_all x1, starting transfers between devices, per_device(): cols = lax.all_to_all(cols, 'dp', 0, 0, tiled=True)  16.7 us
    gather x1, local copies, waits for them, and re-layouts, per_device(): grad_rows = jnp.take(tokens, token, axis=0, mode='clip')[:, :width]  12.5 us
    dot_general x1, matrix products, per_device(): gradient = jnp.dot(rows_t, spread, preferred_element_type=jnp.float32)  10.7 us
    ppermute x15, waiting for transfers between devices, per_device(): bwd = lax.ppermute(bwd, 'expert', bwd_perm)  7.61 us
    all_to_all x1, waiting for transfers between devices, per_device(): cols = lax.all_to_all(cols, 'dp', 0, 0, tiled=True)  6.63 us
  transfers between devices with their start and end apart: 33, of which 25 were waited for; matrix products, arithmetic and copies ran while one was open for 16% of the time, Pallas kernels for 0%

profile of v5, /device:TPU:2, one launch (start us, length us, event | category | flops | bytes accessed | tf_op | source)
XLA Modules:
  0.0 231.2 jit_solution(14173204473512468081)
XLA Ops:
  6.5 1.1 copy.75
  7.6 0.8 reshape.239
  8.5 1.1 reshape.236
  9.7 0.7 convert_element_type.23
  10.4 0.8 pad_maximum_fusion.1
  11.2 0.7 pad_maximum_fusion
  11.9 16.7 %all-to-all-start = ((bf16[32,8,240]{2,1,0:T(8,128)(2,1)}), bf16[32,8,240]{2,1,0:T(8,128)(2,1)S(1)}, u32[]{:S(2)}, u32[]{:S(2)}) async-start(bf16[32,8,240]{2,1,0:T(8,128)(2,1)} %pad_maximum_fusion), calls=%async_computation | async-start | bytes 262144 | tf_op jit(solution)/shard_map/all_to_all | solution.py:52
  28.7 6.6 %all-to-all-done = bf16[32,8,240]{2,1,0:T(8,128)(2,1)S(1)} async-done(((bf16[32,8,240]{2,1,0:T(8,128)(2,1)}), bf16[32,8,240]{2,1,0:T(8,128)(2,1)S(1)}, u32[]{:S(2)}, u32[]{:S(2)}) %all-to-all-start) | async-done | bytes 122912 | tf_op jit(solution)/shard_map/all_to_all | solution.py:52
  35.4 9.5 %collective-permute-start = (bf16[32,8,240]{2,1,0:T(8,128)(2,1)S(1)}, bf16[32,8,240]{2,1,0:T(8,128)(2,1)S(1)}, u32[]{:S(2)}, u32[]{:S(2)}) collective-permute-start(bf16[32,8,240]{2,1,0:T(8,128)(2,1)S(1)} %all-to-all-done), channel_id=1, source_target_pairs={{0,992},{32,0},{64,32},{96,64},{128,96},{160,128},{192,160},{224,1... | collective-permute-start | bytes 368648 | tf_op jit(solution)/shard_map/ppermute | solution.py:65
  44.8 1.9 collective-permute-start.15
  46.8 1.1 collective-permute-done
  47.9 5.6 %collective-permute-start.1 = (bf16[32,8,240]{2,1,0:T(8,128)(2,1)S(1)}, bf16[32,8,240]{2,1,0:T(8,128)(2,1)S(1)}, u32[]{:S(2)}, u32[]{:S(2)}) collective-permute-start(bf16[32,8,240]{2,1,0:T(8,128)(2,1)S(1)} %collective-permute-done), channel_id=1, source_target_pairs={{0,992},{32,0},{64,32},{96,64},{128,96},{160,128},{192,160},{224,1... | collective-permute-start | bytes 368648 | tf_op jit(solution)/shard_map/ppermute | solution.py:65
  53.5 1.9 collective-permute-start.16
  55.4 0.5 collective-permute-done.1
  56.0 5.6 %collective-permute-start.2 = (bf16[32,8,240]{2,1,0:T(8,128)(2,1)S(1)}, bf16[32,8,240]{2,1,0:T(8,128)(2,1)S(1)}, u32[]{:S(2)}, u32[]{:S(2)}) collective-permute-start(bf16[32,8,240]{2,1,0:T(8,128)(2,1)S(1)} %collective-permute-done.1), channel_id=1, source_target_pairs={{0,992},{32,0},{64,32},{96,64},{128,96},{160,128},{192,160},{224,1... | collective-permute-start | bytes 368648 | tf_op jit(solution)/shard_map/ppermute | solution.py:65
  61.6 1.9 collective-permute-start.17
  63.5 0.5 collective-permute-done.2
  64.1 5.6 %collective-permute-start.3 = (bf16[32,8,240]{2,1,0:T(8,128)(2,1)S(1)}, bf16[32,8,240]{2,1,0:T(8,128)(2,1)S(1)}, u32[]{:S(2)}, u32[]{:S(2)}) collective-permute-start(bf16[32,8,240]{2,1,0:T(8,128)(2,1)S(1)} %collective-permute-done.2), channel_id=1, source_target_pairs={{0,992},{32,0},{64,32},{96,64},{128,96},{160,128},{192,160},{224,1... | collective-permute-start | bytes 368648 | tf_op jit(solution)/shard_map/ppermute | solution.py:65
  69.6 1.9 collective-permute-start.18
  71.6 0.5 collective-permute-done.3
  72.1 5.6 %collective-permute-start.4 = (bf16[32,8,240]{2,1,0:T(8,128)(2,1)S(1)}, bf16[32,8,240]{2,1,0:T(8,128)(2,1)S(1)}, u32[]{:S(2)}, u32[]{:S(2)}) collective-permute-start(bf16[32,8,240]{2,1,0:T(8,128)(2,1)S(1)} %collective-permute-done.3), channel_id=1, source_target_pairs={{0,992},{32,0},{64,32},{96,64},{128,96},{160,128},{192,160},{224,1... | collective-permute-start | bytes 368648 | tf_op jit(solution)/shard_map/ppermute | solution.py:65
  77.7 1.9 collective-permute-start.19
  79.6 0.5 collective-permute-done.4
  80.2 5.6 %collective-permute-start.5 = (bf16[32,8,240]{2,1,0:T(8,128)(2,1)S(1)}, bf16[32,8,240]{2,1,0:T(8,128)(2,1)S(1)}, u32[]{:S(2)}, u32[]{:S(2)}) collective-permute-start(bf16[32,8,240]{2,1,0:T(8,128)(2,1)S(1)} %collective-permute-done.4), channel_id=1, source_target_pairs={{0,992},{32,0},{64,32},{96,64},{128,96},{160,128},{192,160},{224,1... | collective-permute-start | bytes 368648 | tf_op jit(solution)/shard_map/ppermute | solution.py:65
  85.8 1.9 collective-permute-start.20
  87.7 0.9 collective-permute-done.5
  88.6 5.6 %collective-permute-start.6 = (bf16[32,8,240]{2,1,0:T(8,128)(2,1)S(1)}, bf16[32,8,240]{2,1,0:T(8,128)(2,1)S(1)}, u32[]{:S(2)}, u32[]{:S(2)}) collective-permute-start(bf16[32,8,240]{2,1,0:T(8,128)(2,1)S(1)} %collective-permute-done.5), channel_id=1, source_target_pairs={{0,992},{32,0},{64,32},{96,64},{128,96},{160,128},{192,160},{224,1... | collective-permute-start | bytes 368648 | tf_op jit(solution)/shard_map/ppermute | solution.py:65
  94.5 1.9 collective-permute-start.21
  96.5 1.5 collective-permute-done.6
  97.9 5.6 %collective-permute-start.7 = (bf16[32,8,240]{2,1,0:T(8,128)(2,1)S(1)}, bf16[32,8,240]{2,1,0:T(8,128)(2,1)S(1)}, u32[]{:S(2)}, u32[]{:S(2)}) collective-permute-start(bf16[32,8,240]{2,1,0:T(8,128)(2,1)S(1)} %collective-permute-done.6), channel_id=1, source_target_pairs={{0,992},{32,0},{64,32},{96,64},{128,96},{160,128},{192,160},{224,1... | collective-permute-start | bytes 368648 | tf_op jit(solution)/shard_map/ppermute | solution.py:65
  103.9 1.9 collective-permute-start.22
  105.9 0.6 collective-permute-done.7
  106.5 5.6 %collective-permute-start.8 = (bf16[32,8,240]{2,1,0:T(8,128)(2,1)S(1)}, bf16[32,8,240]{2,1,0:T(8,128)(2,1)S(1)}, u32[]{:S(2)}, u32[]{:S(2)}) collective-permute-start(bf16[32,8,240]{2,1,0:T(8,128)(2,1)S(1)} %collective-permute-done.7), channel_id=1, source_target_pairs={{0,992},{32,0},{64,32},{96,64},{128,96},{160,128},{192,160},{224,1... | collective-permute-start | bytes 368648 | tf_op jit(solution)/shard_map/ppermute | solution.py:65
  112.5 1.9 collective-permute-start.23
  114.6 5.6 %collective-permute-start.9 = (bf16[32,8,240]{2,1,0:T(8,128)(2,1)S(1)}, bf16[32,8,240]{2,1,0:T(8,128)(2,1)S(1)}, u32[]{:S(2)}, u32[]{:S(2)}) collective-permute-start(bf16[32,8,240]{2,1,0:T(8,128)(2,1)S(1)} %collective-permute-done.8), channel_id=1, source_target_pairs={{0,992},{32,0},{64,32},{96,64},{128,96},{160,128},{192,160},{224,1... | collective-permute-start | bytes 368648 | tf_op jit(solution)/shard_map/ppermute | solution.py:65
  120.6 1.9 collective-permute-start.24
  122.7 5.6 %collective-permute-start.10 = (bf16[32,8,240]{2,1,0:T(8,128)(2,1)S(1)}, bf16[32,8,240]{2,1,0:T(8,128)(2,1)S(1)}, u32[]{:S(2)}, u32[]{:S(2)}) collective-permute-start(bf16[32,8,240]{2,1,0:T(8,128)(2,1)S(1)} %collective-permute-done.9), channel_id=1, source_target_pairs={{0,992},{32,0},{64,32},{96,64},{128,96},{160,128},{192,160},{224,1... | collective-permute-start | bytes 368648 | tf_op jit(solution)/shard_map/ppermute | solution.py:65
  128.6 1.9 collective-permute-start.25
  130.7 5.6 %collective-permute-start.11 = (bf16[32,8,240]{2,1,0:T(8,128)(2,1)S(1)}, bf16[32,8,240]{2,1,0:T(8,128)(2,1)S(1)}, u32[]{:S(2)}, u32[]{:S(2)}) collective-permute-start(bf16[32,8,240]{2,1,0:T(8,128)(2,1)S(1)} %collective-permute-done.10), channel_id=1, source_target_pairs={{0,992},{32,0},{64,32},{96,64},{128,96},{160,128},{192,160},{224,1... | collective-permute-start | bytes 368648 | tf_op jit(solution)/shard_map/ppermute | solution.py:65
  136.7 1.9 collective-permute-start.26
  138.8 5.6 %collective-permute-start.12 = (bf16[32,8,240]{2,1,0:T(8,128)(2,1)S(1)}, bf16[32,8,240]{2,1,0:T(8,128)(2,1)S(1)}, u32[]{:S(2)}, u32[]{:S(2)}) collective-permute-start(bf16[32,8,240]{2,1,0:T(8,128)(2,1)S(1)} %collective-permute-done.11), channel_id=1, source_target_pairs={{0,992},{32,0},{64,32},{96,64},{128,96},{160,128},{192,160},{224,1... | collective-permute-start | bytes 368648 | tf_op jit(solution)/shard_map/ppermute | solution.py:65
  144.7 1.9 collective-permute-start.27
  146.7 0.7 collective-permute-done.12
  147.4 5.6 %collective-permute-start.13 = (bf16[32,8,240]{2,1,0:T(8,128)(2,1)S(1)}, bf16[32,8,240]{2,1,0:T(8,128)(2,1)S(1)}, u32[]{:S(2)}, u32[]{:S(2)}) collective-permute-start(bf16[32,8,240]{2,1,0:T(8,128)(2,1)S(1)} %collective-permute-done.12), channel_id=1, source_target_pairs={{0,992},{32,0},{64,32},{96,64},{128,96},{160,128},{192,160},{224,1... | collective-permute-start | bytes 368648 | tf_op jit(solution)/shard_map/ppermute | solution.py:65
  153.0 0.7 collective-permute-done.27
  153.7 1.9 collective-permute-start.28
  155.6 5.4 %collective-permute-start.14 = (bf16[32,8,240]{2,1,0:T(8,128)(2,1)S(1)}, bf16[32,8,240]{2,1,0:T(8,128)(2,1)S(1)}, u32[]{:S(2)}, u32[]{:S(2)}) collective-permute-start(bf16[32,8,240]{2,1,0:T(8,128)(2,1)S(1)} %collective-permute-done.13), channel_id=1, source_target_pairs={{0,992},{32,0},{64,32},{96,64},{128,96},{160,128},{192,160},{224,1... | collective-permute-start | bytes 368648 | tf_op jit(solution)/shard_map/ppermute | solution.py:65
  161.0 1.5 collective-permute-done.28
  162.5 1.9 collective-permute-start.29
  164.5 6.1 %collective-permute-done.29 = bf16[32,8,240]{2,1,0:T(8,128)(2,1)S(1)} collective-permute-done((bf16[32,8,240]{2,1,0:T(8,128)(2,1)S(1)}, bf16[32,8,240]{2,1,0:T(8,128)(2,1)S(1)}, u32[]{:S(2)}, u32[]{:S(2)}) %collective-permute-start.29) | collective-permute-done | bytes 122912 | tf_op jit(solution)/shard_map/ppermute | solution.py:62
  170.6 2.1 collective-permute-start.30
  172.7 5.9 %collective-permute-done.30 = bf16[32,8,240]{2,1,0:T(8,128)(2,1)S(1)} collective-permute-done((bf16[32,8,240]{2,1,0:T(8,128)(2,1)S(1)}, bf16[32,8,240]{2,1,0:T(8,128)(2,1)S(1)}, u32[]{:S(2)}, u32[]{:S(2)}) %collective-permute-start.30) | collective-permute-done | bytes 122912 | tf_op jit(solution)/shard_map/ppermute | solution.py:62
  179.0 2.1 copy-done
  181.0 2.0 slice.20
  183.1 2.3 copy.86
  185.4 0.7 gather_fusion
  186.3 1.2 fusion.6
  187.5 1.7 copy.70
  191.6 0.6 select_reduce_fusion.2
  193.0 3.4 %select_reduce_fusion = (s32[32,32,3]{1,2,0:T(4,128)S(1)}, s32[32,32,3]{1,2,0:T(4,128)S(1)}) fusion(s32[64]{0:T(128)S(1)} %and_select_fusion, s32[32,32,64]{2,1,0:T(8,128)S(1)} %bitcast.96, pred[32,32,64]{2,1,0:T(8,128)(4,1)S(1)} %fusion.4, s32[32,32,64]{2,1,0:T(8,128)S(1)} %fusion.5), kind=kLoop, calls=%fused_computation.7 | loop fusion | flops 1173504 | bytes 614656 | tf_op jit(solution)/shard_map/reduce_sum | solution.py:32
  197.0 12.5 %gather_fusion.1 = bf16[3072,240]{1,0:T(8,128)(2,1)S(1)} fusion(bf16[8192,240]{1,0:T(8,128)(2,1)} %bitcast.92, s32[3072]{0:T(1024)S(1)} %broadcast_clamp_fusion), kind=kCustom, calls=%fused_computation.1 | custom fusion | bytes 2961408 | tf_op jit(solution)/shard_map/jit(_take)/gather | solution.py:77
  209.5 0.7 copy.79
  210.8 2.8 %broadcast_select_fusion = bf16[3072,4,224]{0,2,1:T(8,128)(2,1)} fusion(pred[3072,4]{0,1:T(4,128)(4,1)S(1)} %iota_compare_fusion.1, bf16[3072,224]{0,1:T(8,128)(2,1)S(1)} %copy.79), kind=kLoop, calls=%fused_computation.5 | loop fusion | flops 2752512 | bytes 6893568 | tf_op jit(solution)/shard_map/jit(_where)/select_n | solution.py:79
  213.6 10.7 %fusion.2 = bf16[1024,896]{0,1:T(8,128)(2,1)} fusion(bf16[3072,896]{0,1:T(8,128)(2,1)} %bitcast.94, bf16[3072,1024]{1,0:T(8,128)(2,1)} %all-gather.2.cloned.1.call-done, f32[3072]{0:T(1024)S(1)} %mul.31), kind=kOutput, calls=%fused_computation.6 | convolution fusion | flops 5647499264 | bytes 13643776 | tf_op jit(solution)/shard_map/dot_general | solution.py:81
  (80 shorter events, 8.5 us)
Async XLA Ops:
  6.5 207.1 %all-gather.2.cloned.1.call-start = ((), (), s32[]{:S(2)}) async-start(), calls=%async_computation.1 | async-start | bytes 6488064 | tf_op jit(solution)/shard_map/all_gather | solution.py:45
  11.9 23.4 %all-to-all-start = ((bf16[32,8,240]{2,1,0:T(8,128)(2,1)}), bf16[32,8,240]{2,1,0:T(8,128)(2,1)S(1)}, u32[]{:S(2)}, u32[]{:S(2)}) async-start(bf16[32,8,240]{2,1,0:T(8,128)(2,1)} %pad_maximum_fusion), calls=%async_computation | async-start | bytes 262144 | tf_op jit(solution)/shard_map/all_to_all | solution.py:52
  35.4 12.5 %collective-permute-start = (bf16[32,8,240]{2,1,0:T(8,128)(2,1)S(1)}, bf16[32,8,240]{2,1,0:T(8,128)(2,1)S(1)}, u32[]{:S(2)}, u32[]{:S(2)}) collective-permute-start(bf16[32,8,240]{2,1,0:T(8,128)(2,1)S(1)} %all-to-all-done), channel_id=1, source_target_pairs={{0,992},{32,0},{64,32},{96,64},{128,96},{160,128},{192,160},{224,1... | collective-permute-start | bytes 368648 | tf_op jit(solution)/shard_map/ppermute | solution.py:65
  44.8 8.7 %collective-permute-start.15 = (bf16[32,8,240]{2,1,0:T(8,128)(2,1)S(1)}, bf16[32,8,240]{2,1,0:T(8,128)(2,1)S(1)}, u32[]{:S(2)}, u32[]{:S(2)}) collective-permute-start(bf16[32,8,240]{2,1,0:T(8,128)(2,1)S(1)} %all-to-all-done), channel_id=1, source_target_pairs={{0,32},{32,64},{64,96},{96,128},{128,160},{160,192},{192,224},{224... | collective-permute-start | bytes 368648 | tf_op jit(solution)/shard_map/ppermute | solution.py:62
  47.9 8.1 %collective-permute-start.1 = (bf16[32,8,240]{2,1,0:T(8,128)(2,1)S(1)}, bf16[32,8,240]{2,1,0:T(8,128)(2,1)S(1)}, u32[]{:S(2)}, u32[]{:S(2)}) collective-permute-start(bf16[32,8,240]{2,1,0:T(8,128)(2,1)S(1)} %collective-permute-done), channel_id=1, source_target_pairs={{0,992},{32,0},{64,32},{96,64},{128,96},{160,128},{192,160},{224,1... | collective-permute-start | bytes 368648 | tf_op jit(solution)/shard_map/ppermute | solution.py:65
  53.5 8.1 %collective-permute-start.16 = (bf16[32,8,240]{2,1,0:T(8,128)(2,1)S(1)}, bf16[32,8,240]{2,1,0:T(8,128)(2,1)S(1)}, u32[]{:S(2)}, u32[]{:S(2)}) collective-permute-start(bf16[32,8,240]{2,1,0:T(8,128)(2,1)S(1)} %collective-permute-done.15), channel_id=1, source_target_pairs={{0,32},{32,64},{64,96},{96,128},{128,160},{160,192},{192,224},{224... | collective-permute-start | bytes 368648 | tf_op jit(solution)/shard_map/ppermute | solution.py:62
  56.0 8.1 %collective-permute-start.2 = (bf16[32,8,240]{2,1,0:T(8,128)(2,1)S(1)}, bf16[32,8,240]{2,1,0:T(8,128)(2,1)S(1)}, u32[]{:S(2)}, u32[]{:S(2)}) collective-permute-start(bf16[32,8,240]{2,1,0:T(8,128)(2,1)S(1)} %collective-permute-done.1), channel_id=1, source_target_pairs={{0,992},{32,0},{64,32},{96,64},{128,96},{160,128},{192,160},{224,1... | collective-permute-start | bytes 368648 | tf_op jit(solution)/shard_map/ppermute | solution.py:65
  61.6 8.1 %collective-permute-start.17 = (bf16[32,8,240]{2,1,0:T(8,128)(2,1)S(1)}, bf16[32,8,240]{2,1,0:T(8,128)(2,1)S(1)}, u32[]{:S(2)}, u32[]{:S(2)}) collective-permute-start(bf16[32,8,240]{2,1,0:T(8,128)(2,1)S(1)} %collective-permute-done.16), channel_id=1, source_target_pairs={{0,32},{32,64},{64,96},{96,128},{128,160},{160,192},{192,224},{224... | collective-permute-start | bytes 368648 | tf_op jit(solution)/shard_map/ppermute | solution.py:62
  64.1 8.1 %collective-permute-start.3 = (bf16[32,8,240]{2,1,0:T(8,128)(2,1)S(1)}, bf16[32,8,240]{2,1,0:T(8,128)(2,1)S(1)}, u32[]{:S(2)}, u32[]{:S(2)}) collective-permute-start(bf16[32,8,240]{2,1,0:T(8,128)(2,1)S(1)} %collective-permute-done.2), channel_id=1, source_target_pairs={{0,992},{32,0},{64,32},{96,64},{128,96},{160,128},{192,160},{224,1... | collective-permute-start | bytes 368648 | tf_op jit(solution)/shard_map/ppermute | solution.py:65
  69.6 8.1 %collective-permute-start.18 = (bf16[32,8,240]{2,1,0:T(8,128)(2,1)S(1)}, bf16[32,8,240]{2,1,0:T(8,128)(2,1)S(1)}, u32[]{:S(2)}, u32[]{:S(2)}) collective-permute-start(bf16[32,8,240]{2,1,0:T(8,128)(2,1)S(1)} %collective-permute-done.17), channel_id=1, source_target_pairs={{0,32},{32,64},{64,96},{96,128},{128,160},{160,192},{192,224},{224... | collective-permute-start | bytes 368648 | tf_op jit(solution)/shard_map/ppermute | solution.py:62
  72.1 8.1 %collective-permute-start.4 = (bf16[32,8,240]{2,1,0:T(8,128)(2,1)S(1)}, bf16[32,8,240]{2,1,0:T(8,128)(2,1)S(1)}, u32[]{:S(2)}, u32[]{:S(2)}) collective-permute-start(bf16[32,8,240]{2,1,0:T(8,128)(2,1)S(1)} %collective-permute-done.3), channel_id=1, source_target_pairs={{0,992},{32,0},{64,32},{96,64},{128,96},{160,128},{192,160},{224,1... | collective-permute-start | bytes 368648 | tf_op jit(solution)/shard_map/ppermute | solution.py:65
  77.7 8.1 %collective-permute-start.19 = (bf16[32,8,240]{2,1,0:T(8,128)(2,1)S(1)}, bf16[32,8,240]{2,1,0:T(8,128)(2,1)S(1)}, u32[]{:S(2)}, u32[]{:S(2)}) collective-permute-start(bf16[32,8,240]{2,1,0:T(8,128)(2,1)S(1)} %collective-permute-done.18), channel_id=1, source_target_pairs={{0,32},{32,64},{64,96},{96,128},{128,160},{160,192},{192,224},{224... | collective-permute-start | bytes 368648 | tf_op jit(solution)/shard_map/ppermute | solution.py:62
  80.2 8.4 %collective-permute-start.5 = (bf16[32,8,240]{2,1,0:T(8,128)(2,1)S(1)}, bf16[32,8,240]{2,1,0:T(8,128)(2,1)S(1)}, u32[]{:S(2)}, u32[]{:S(2)}) collective-permute-start(bf16[32,8,240]{2,1,0:T(8,128)(2,1)S(1)} %collective-permute-done.4), channel_id=1, source_target_pairs={{0,992},{32,0},{64,32},{96,64},{128,96},{160,128},{192,160},{224,1... | collective-permute-start | bytes 368648 | tf_op jit(solution)/shard_map/ppermute | solution.py:65
  85.8 8.8 %collective-permute-start.20 = (bf16[32,8,240]{2,1,0:T(8,128)(2,1)S(1)}, bf16[32,8,240]{2,1,0:T(8,128)(2,1)S(1)}, u32[]{:S(2)}, u32[]{:S(2)}) collective-permute-start(bf16[32,8,240]{2,1,0:T(8,128)(2,1)S(1)} %collective-permute-done.19), channel_id=1, source_target_pairs={{0,32},{32,64},{64,96},{96,128},{128,160},{160,192},{192,224},{224... | collective-permute-start | bytes 368648 | tf_op jit(solution)/shard_map/ppermute | solution.py:62
  88.6 9.3 %collective-permute-start.6 = (bf16[32,8,240]{2,1,0:T(8,128)(2,1)S(1)}, bf16[32,8,240]{2,1,0:T(8,128)(2,1)S(1)}, u32[]{:S(2)}, u32[]{:S(2)}) collective-permute-start(bf16[32,8,240]{2,1,0:T(8,128)(2,1)S(1)} %collective-permute-done.5), channel_id=1, source_target_pairs={{0,992},{32,0},{64,32},{96,64},{128,96},{160,128},{192,160},{224,1... | collective-permute-start | bytes 368648 | tf_op jit(solution)/shard_map/ppermute | solution.py:65
  94.5 9.4 %collective-permute-start.21 = (bf16[32,8,240]{2,1,0:T(8,128)(2,1)S(1)}, bf16[32,8,240]{2,1,0:T(8,128)(2,1)S(1)}, u32[]{:S(2)}, u32[]{:S(2)}) collective-permute-start(bf16[32,8,240]{2,1,0:T(8,128)(2,1)S(1)} %collective-permute-done.20), channel_id=1, source_target_pairs={{0,32},{32,64},{64,96},{96,128},{128,160},{160,192},{192,224},{224... | collective-permute-start | bytes 368648 | tf_op jit(solution)/shard_map/ppermute | solution.py:62
  97.9 8.6 %collective-permute-start.7 = (bf16[32,8,240]{2,1,0:T(8,128)(2,1)S(1)}, bf16[32,8,240]{2,1,0:T(8,128)(2,1)S(1)}, u32[]{:S(2)}, u32[]{:S(2)}) collective-permute-start(bf16[32,8,240]{2,1,0:T(8,128)(2,1)S(1)} %collective-permute-done.6), channel_id=1, source_target_pairs={{0,992},{32,0},{64,32},{96,64},{128,96},{160,128},{192,160},{224,1... | collective-permute-start | bytes 368648 | tf_op jit(solution)/shard_map/ppermute | solution.py:65
  103.9 8.6 %collective-permute-start.22 = (bf16[32,8,240]{2,1,0:T(8,128)(2,1)S(1)}, bf16[32,8,240]{2,1,0:T(8,128)(2,1)S(1)}, u32[]{:S(2)}, u32[]{:S(2)}) collective-permute-start(bf16[32,8,240]{2,1,0:T(8,128)(2,1)S(1)} %collective-permute-done.21), channel_id=1, source_target_pairs={{0,32},{32,64},{64,96},{96,128},{128,160},{160,192},{192,224},{224... | collective-permute-start | bytes 368648 | tf_op jit(solution)/shard_map/ppermute | solution.py:62
  106.5 8.1 %collective-permute-start.8 = (bf16[32,8,240]{2,1,0:T(8,128)(2,1)S(1)}, bf16[32,8,240]{2,1,0:T(8,128)(2,1)S(1)}, u32[]{:S(2)}, u32[]{:S(2)}) collective-permute-start(bf16[32,8,240]{2,1,0:T(8,128)(2,1)S(1)} %collective-permute-done.7), channel_id=1, source_target_pairs={{0,992},{32,0},{64,32},{96,64},{128,96},{160,128},{192,160},{224,1... | collective-permute-start | bytes 368648 | tf_op jit(solution)/shard_map/ppermute | solution.py:65
  112.5 8.1 %collective-permute-start.23 = (bf16[32,8,240]{2,1,0:T(8,128)(2,1)S(1)}, bf16[32,8,240]{2,1,0:T(8,128)(2,1)S(1)}, u32[]{:S(2)}, u32[]{:S(2)}) collective-permute-start(bf16[32,8,240]{2,1,0:T(8,128)(2,1)S(1)} %collective-permute-done.22), channel_id=1, source_target_pairs={{0,32},{32,64},{64,96},{96,128},{128,160},{160,192},{192,224},{224... | collective-permute-start | bytes 368648 | tf_op jit(solution)/shard_map/ppermute | solution.py:62
  114.6 8.1 %collective-permute-start.9 = (bf16[32,8,240]{2,1,0:T(8,128)(2,1)S(1)}, bf16[32,8,240]{2,1,0:T(8,128)(2,1)S(1)}, u32[]{:S(2)}, u32[]{:S(2)}) collective-permute-start(bf16[32,8,240]{2,1,0:T(8,128)(2,1)S(1)} %collective-permute-done.8), channel_id=1, source_target_pairs={{0,992},{32,0},{64,32},{96,64},{128,96},{160,128},{192,160},{224,1... | collective-permute-start | bytes 368648 | tf_op jit(solution)/shard_map/ppermute | solution.py:65
  120.6 8.1 %collective-permute-start.24 = (bf16[32,8,240]{2,1,0:T(8,128)(2,1)S(1)}, bf16[32,8,240]{2,1,0:T(8,128)(2,1)S(1)}, u32[]{:S(2)}, u32[]{:S(2)}) collective-permute-start(bf16[32,8,240]{2,1,0:T(8,128)(2,1)S(1)} %collective-permute-done.23), channel_id=1, source_target_pairs={{0,32},{32,64},{64,96},{96,128},{128,160},{160,192},{192,224},{224... | collective-permute-start | bytes 368648 | tf_op jit(solution)/shard_map/ppermute | solution.py:62
  122.7 8.1 %collective-permute-start.10 = (bf16[32,8,240]{2,1,0:T(8,128)(2,1)S(1)}, bf16[32,8,240]{2,1,0:T(8,128)(2,1)S(1)}, u32[]{:S(2)}, u32[]{:S(2)}) collective-permute-start(bf16[32,8,240]{2,1,0:T(8,128)(2,1)S(1)} %collective-permute-done.9), channel_id=1, source_target_pairs={{0,992},{32,0},{64,32},{96,64},{128,96},{160,128},{192,160},{224,1... | collective-permute-start | bytes 368648 | tf_op jit(solution)/shard_map/ppermute | solution.py:65
  128.6 8.1 %collective-permute-start.25 = (bf16[32,8,240]{2,1,0:T(8,128)(2,1)S(1)}, bf16[32,8,240]{2,1,0:T(8,128)(2,1)S(1)}, u32[]{:S(2)}, u32[]{:S(2)}) collective-permute-start(bf16[32,8,240]{2,1,0:T(8,128)(2,1)S(1)} %collective-permute-done.24), channel_id=1, source_target_pairs={{0,32},{32,64},{64,96},{96,128},{128,160},{160,192},{192,224},{224... | collective-permute-start | bytes 368648 | tf_op jit(solution)/shard_map/ppermute | solution.py:62
  130.7 8.1 %collective-permute-start.11 = (bf16[32,8,240]{2,1,0:T(8,128)(2,1)S(1)}, bf16[32,8,240]{2,1,0:T(8,128)(2,1)S(1)}, u32[]{:S(2)}, u32[]{:S(2)}) collective-permute-start(bf16[32,8,240]{2,1,0:T(8,128)(2,1)S(1)} %collective-permute-done.10), channel_id=1, source_target_pairs={{0,992},{32,0},{64,32},{96,64},{128,96},{160,128},{192,160},{224,1... | collective-permute-start | bytes 368648 | tf_op jit(solution)/shard_map/ppermute | solution.py:65
  136.7 8.1 %collective-permute-start.26 = (bf16[32,8,240]{2,1,0:T(8,128)(2,1)S(1)}, bf16[32,8,240]{2,1,0:T(8,128)(2,1)S(1)}, u32[]{:S(2)}, u32[]{:S(2)}) collective-permute-start(bf16[32,8,240]{2,1,0:T(8,128)(2,1)S(1)} %collective-permute-done.25), channel_id=1, source_target_pairs={{0,32},{32,64},{64,96},{96,128},{128,160},{160,192},{192,224},{224... | collective-permute-start | bytes 368648 | tf_op jit(solution)/shard_map/ppermute | solution.py:62
  138.8 8.6 %collective-permute-start.12 = (bf16[32,8,240]{2,1,0:T(8,128)(2,1)S(1)}, bf16[32,8,240]{2,1,0:T(8,128)(2,1)S(1)}, u32[]{:S(2)}, u32[]{:S(2)}) collective-permute-start(bf16[32,8,240]{2,1,0:T(8,128)(2,1)S(1)} %collective-permute-done.11), channel_id=1, source_target_pairs={{0,992},{32,0},{64,32},{96,64},{128,96},{160,128},{192,160},{224,1... | collective-permute-start | bytes 368648 | tf_op jit(solution)/shard_map/ppermute | solution.py:65
  144.7 9.0 %collective-permute-start.27 = (bf16[32,8,240]{2,1,0:T(8,128)(2,1)S(1)}, bf16[32,8,240]{2,1,0:T(8,128)(2,1)S(1)}, u32[]{:S(2)}, u32[]{:S(2)}) collective-permute-start(bf16[32,8,240]{2,1,0:T(8,128)(2,1)S(1)} %collective-permute-done.26), channel_id=1, source_target_pairs={{0,32},{32,64},{64,96},{96,128},{128,160},{160,192},{192,224},{224... | collective-permute-start | bytes 368648 | tf_op jit(solution)/shard_map/ppermute | solution.py:62
  147.4 8.3 %collective-permute-start.13 = (bf16[32,8,240]{2,1,0:T(8,128)(2,1)S(1)}, bf16[32,8,240]{2,1,0:T(8,128)(2,1)S(1)}, u32[]{:S(2)}, u32[]{:S(2)}) collective-permute-start(bf16[32,8,240]{2,1,0:T(8,128)(2,1)S(1)} %collective-permute-done.12), channel_id=1, source_target_pairs={{0,992},{32,0},{64,32},{96,64},{128,96},{160,128},{192,160},{224,1... | collective-permute-start | bytes 368648 | tf_op jit(solution)/shard_map/ppermute | solution.py:65
  153.7 8.8 %collective-permute-start.28 = (bf16[32,8,240]{2,1,0:T(8,128)(2,1)S(1)}, bf16[32,8,240]{2,1,0:T(8,128)(2,1)S(1)}, u32[]{:S(2)}, u32[]{:S(2)}) collective-permute-start(bf16[32,8,240]{2,1,0:T(8,128)(2,1)S(1)} %collective-permute-done.27), channel_id=1, source_target_pairs={{0,32},{32,64},{64,96},{96,128},{128,160},{160,192},{192,224},{224... | collective-permute-start | bytes 368648 | tf_op jit(solution)/shard_map/ppermute | solution.py:62
  155.6 17.0 %collective-permute-start.14 = (bf16[32,8,240]{2,1,0:T(8,128)(2,1)S(1)}, bf16[32,8,240]{2,1,0:T(8,128)(2,1)S(1)}, u32[]{:S(2)}, u32[]{:S(2)}) collective-permute-start(bf16[32,8,240]{2,1,0:T(8,128)(2,1)S(1)} %collective-permute-done.13), channel_id=1, source_target_pairs={{0,992},{32,0},{64,32},{96,64},{128,96},{160,128},{192,160},{224,1... | collective-permute-start | bytes 368648 | tf_op jit(solution)/shard_map/ppermute | solution.py:65
  162.5 8.1 %collective-permute-start.29 = (bf16[32,8,240]{2,1,0:T(8,128)(2,1)S(1)}, bf16[32,8,240]{2,1,0:T(8,128)(2,1)S(1)}, u32[]{:S(2)}, u32[]{:S(2)}) collective-permute-start(bf16[32,8,240]{2,1,0:T(8,128)(2,1)S(1)} %collective-permute-done.28), channel_id=1, source_target_pairs={{0,32},{32,64},{64,96},{96,128},{128,160},{160,192},{192,224},{224... | collective-permute-start | bytes 368648 | tf_op jit(solution)/shard_map/ppermute | solution.py:62
  170.6 8.1 %collective-permute-start.30 = (bf16[32,8,240]{2,1,0:T(8,128)(2,1)S(1)}, bf16[32,8,240]{2,1,0:T(8,128)(2,1)S(1)}, u32[]{:S(2)}, u32[]{:S(2)}) collective-permute-start(bf16[32,8,240]{2,1,0:T(8,128)(2,1)S(1)} %collective-permute-done.29), channel_id=1, source_target_pairs={{0,32},{32,64},{64,96},{96,128},{128,160},{160,192},{192,224},{224... | collective-permute-start | bytes 368648 | tf_op jit(solution)/shard_map/ppermute | solution.py:62
  178.9 2.1 copy-start
Sparse Core Ops, SparseCore 0:
  11.6 91.7 all-gather.1

commit v6 on v5

--- a/solution.py
+++ b/solution.py
@@ -10,7 +10,7 @@
 TOK_DEV = 8
 
 
-def slot_tables(meta_gs, me_exp, relative, capacity):
+def slot_tables(meta_gs, me_exp, block, capacity):
     n_grp, n_src = meta_gs.shape[:2]
     per_block = TOK_DEV * TOP
     ids = meta_gs[..., :TOP].astype(jnp.int32).reshape(n_grp, n_src, per_block)
@@ -30,7 +30,6 @@
     weight = jnp.sum(jnp.where(select, wts[:, :, None, :], 0.0), axis=-1)
     label = jnp.sum(jnp.where(select, local[:, :, None, :] + 1, 0), axis=-1) - 1
     token_in_block = jnp.sum(jnp.where(select, (entry // TOP)[None, None, None, :], 0), axis=-1)
-    block = relative[None, :] * n_grp + jnp.arange(n_grp, dtype=jnp.int32)[:, None]
     token = token_in_block + block[:, :, None] * TOK_DEV
     return weight.reshape(-1), label.reshape(-1), token.reshape(-1)
 
@@ -42,8 +41,6 @@
     width = D // n_grp
     me_exp = lax.axis_index("expert")
 
-    hidden = lax.all_gather(saved_hidden.reshape(-1, FF), "dp", axis=0, tiled=True)
-
     meta = jnp.concatenate([expert_ids.astype(jnp.bfloat16), combine], axis=1)
     cols = jnp.transpose(grad_out.reshape(TOK_DEV, n_grp, width), (1, 0, 2))
     cols = jnp.concatenate(
@@ -51,13 +48,19 @@
     )
     cols = lax.all_to_all(cols, "dp", 0, 0, tiled=True)
 
+    split = n_grp // 2
+    gathered = lax.all_gather(cols[split:], "expert", axis=0, tiled=False)
+    hidden_src, cols = lax.optimization_barrier((saved_hidden.reshape(-1, FF), cols))
+    hidden = lax.all_gather(hidden_src, "dp", axis=0, tiled=True)
+
+    part = cols[:split]
     half = n_exp // 2
     fwd_perm = [(i, (i + 1) % n_exp) for i in range(n_exp)]
     bwd_perm = [(i, (i - 1) % n_exp) for i in range(n_exp)]
-    ahead = [cols]
+    ahead = [part]
     behind = []
-    fwd = cols
-    bwd = cols
+    fwd = part
+    bwd = part
     for step in range(1, half + 1):
         fwd = lax.ppermute(fwd, "expert", fwd_perm)
         behind.append(fwd)
@@ -65,12 +68,23 @@
             bwd = lax.ppermute(bwd, "expert", bwd_perm)
             ahead.append(bwd)
     ring = jnp.stack(ahead + behind[::-1], axis=0)
-    tokens = ring.reshape(-1, ring.shape[-1])
+    ring_rows = ring.shape[0] * ring.shape[1] * ring.shape[2]
+    tokens = jnp.concatenate(
+        [ring.reshape(-1, ring.shape[-1]), gathered.reshape(-1, gathered.shape[-1])], axis=0
+    )
 
     relative = (jnp.arange(n_exp, dtype=jnp.int32) - me_exp) % n_exp
-    meta_src = jnp.take(ring[:, :, :, width:], relative, axis=0)
+    ring_meta = jnp.take(ring[:, :, :, width:], relative, axis=0)
+    meta_src = jnp.concatenate([ring_meta, gathered[:, :, :, width:]], axis=1)
     meta_gs = jnp.transpose(meta_src, (1, 0, 2, 3))
-    weight, label, token = slot_tables(meta_gs, me_exp, relative, capacity)
+    groups = jnp.arange(n_grp, dtype=jnp.int32)[:, None]
+    sources = jnp.arange(n_exp, dtype=jnp.int32)[None, :]
+    block = jnp.where(
+        groups < split,
+        relative[None, :] * split + groups,
+        ring_rows // TOK_DEV + sources * (n_grp - split) + (groups - split),
+    )
+    weight, label, token = slot_tables(meta_gs, me_exp, block, capacity)
 
     hidden_t = jnp.transpose(hidden)
     rows_t = (weight[None, :] * hidden_t.astype(jnp.float32)).astype(jnp.bfloat16)

time: 232 us -> 269 us (1.16)
  the two profiles are of different devices: /device:TPU:2 before, /device:TPU:1 now
where the time goes in v6:
time: 269 us; the launch traced here: 268 us
  starting transfers between devices  107 us (40%)
  waiting for transfers between devices  57.2 us (21%)
  local copies, waits for them, and re-layouts  34.9 us (13%)
  blocking collectives  24.5 us (9%)
  other arithmetic  19.2 us (7%)
  between operations  14.2 us (5%)
  matrix products  11.1 us (4%)
    ppermute x15, starting transfers between devices, per_device(): bwd = lax.ppermute(bwd, 'expert', bwd_perm)  75.7 us
    all_gather x1, waiting for transfers between devices, per_device(): hidden = lax.all_gather(hidden_src, 'dp', axis=0, tiled=True)  46.8 us
    ppermute x16, starting transfers between devices, per_device(): fwd = lax.ppermute(fwd, 'expert', fwd_perm)  30.9 us
    all_to_all x1, blocking collectives, per_device(): cols = lax.all_to_all(cols, 'dp', 0, 0, tiled=True)  24.5 us
    gather x1, local copies, waits for them, and re-layouts, per_device(): grad_rows = jnp.take(tokens, token, axis=0, mode='clip')[:, :width]  12.8 us
    dot_general x1, matrix products, per_device(): gradient = jnp.dot(rows_t, spread, preferred_element_type=jnp.float32)  10.7 us
    ppermute x16, waiting for transfers between devices, per_device(): fwd = lax.ppermute(fwd, 'expert', fwd_perm)  10.2 us
  transfers between devices with their start and end apart: 33, of which 6 were waited for; matrix products, arithmetic and copies ran while one was open for 19% of the time, Pallas kernels for 0%

profile of v6, /device:TPU:1, one launch (start us, length us, event | category | flops | bytes accessed | tf_op | source)
XLA Modules:
  0.0 267.7 jit_solution(8543648895141036923)
XLA Ops:
  6.5 1.1 reshape.299
  7.7 0.7 convert_element_type.23
  8.4 0.8 pad_maximum_fusion.2
  9.3 24.5 %all_to_all.5 = bf16[32,8,240]{2,1,0:T(8,128)(2,1)S(1)} all-to-all(bf16[32,8,240]{2,1,0:T(8,128)(2,1)S(1)} %pad_maximum_fusion.1), channel_id=1, replica_groups=mesh['expert'=32,'dp'=32] {'dp'}, dimensions={0} | all-to-all | bytes 245760 | tf_op jit(solution)/shard_map/all_to_all | solution.py:49
  33.8 0.6 slice.33
  34.5 1.1 copy.60
  35.6 0.9 reshape.298
  36.6 9.9 %collective-permute-start = (bf16[16,8,240]{2,1,0:T(8,128)(2,1)S(1)}, bf16[16,8,240]{2,1,0:T(8,128)(2,1)S(1)}, u32[]{:S(2)}, u32[]{:S(2)}) collective-permute-start(bf16[16,8,240]{2,1,0:T(8,128)(2,1)S(1)} %slice.21), channel_id=1, source_target_pairs={{0,992},{32,0},{64,32},{96,64},{128,96},{160,128},{192,160},{224,1... | collective-permute-start | bytes 184328 | tf_op jit(solution)/shard_map/ppermute | solution.py:68
  46.5 1.9 collective-permute-start.15
  48.5 4.6 %collective-permute-start.1 = (bf16[16,8,240]{2,1,0:T(8,128)(2,1)S(1)}, bf16[16,8,240]{2,1,0:T(8,128)(2,1)S(1)}, u32[]{:S(2)}, u32[]{:S(2)}) collective-permute-start(bf16[16,8,240]{2,1,0:T(8,128)(2,1)S(1)} %collective-permute-done), channel_id=1, source_target_pairs={{0,992},{32,0},{64,32},{96,64},{128,96},{160,128},{192,160},{224,1... | collective-permute-start | bytes 184328 | tf_op jit(solution)/shard_map/ppermute | solution.py:68
  53.1 1.9 collective-permute-start.16
  55.1 4.6 %collective-permute-start.2 = (bf16[16,8,240]{2,1,0:T(8,128)(2,1)S(1)}, bf16[16,8,240]{2,1,0:T(8,128)(2,1)S(1)}, u32[]{:S(2)}, u32[]{:S(2)}) collective-permute-start(bf16[16,8,240]{2,1,0:T(8,128)(2,1)S(1)} %collective-permute-done.1), channel_id=1, source_target_pairs={{0,992},{32,0},{64,32},{96,64},{128,96},{160,128},{192,160},{224,1... | collective-permute-start | bytes 184328 | tf_op jit(solution)/shard_map/ppermute | solution.py:68
  59.7 1.9 collective-permute-start.17
  61.6 4.6 %collective-permute-start.3 = (bf16[16,8,240]{2,1,0:T(8,128)(2,1)S(1)}, bf16[16,8,240]{2,1,0:T(8,128)(2,1)S(1)}, u32[]{:S(2)}, u32[]{:S(2)}) collective-permute-start(bf16[16,8,240]{2,1,0:T(8,128)(2,1)S(1)} %collective-permute-done.2), channel_id=1, source_target_pairs={{0,992},{32,0},{64,32},{96,64},{128,96},{160,128},{192,160},{224,1... | collective-permute-start | bytes 184328 | tf_op jit(solution)/shard_map/ppermute | solution.py:68
  66.5 1.9 collective-permute-start.18
  68.5 4.6 %collective-permute-start.4 = (bf16[16,8,240]{2,1,0:T(8,128)(2,1)S(1)}, bf16[16,8,240]{2,1,0:T(8,128)(2,1)S(1)}, u32[]{:S(2)}, u32[]{:S(2)}) collective-permute-start(bf16[16,8,240]{2,1,0:T(8,128)(2,1)S(1)} %collective-permute-done.3), channel_id=1, source_target_pairs={{0,992},{32,0},{64,32},{96,64},{128,96},{160,128},{192,160},{224,1... | collective-permute-start | bytes 184328 | tf_op jit(solution)/shard_map/ppermute | solution.py:68
  73.0 1.9 collective-permute-start.19
  75.0 4.6 %collective-permute-start.5 = (bf16[16,8,240]{2,1,0:T(8,128)(2,1)S(1)}, bf16[16,8,240]{2,1,0:T(8,128)(2,1)S(1)}, u32[]{:S(2)}, u32[]{:S(2)}) collective-permute-start(bf16[16,8,240]{2,1,0:T(8,128)(2,1)S(1)} %collective-permute-done.4), channel_id=1, source_target_pairs={{0,992},{32,0},{64,32},{96,64},{128,96},{160,128},{192,160},{224,1... | collective-permute-start | bytes 184328 | tf_op jit(solution)/shard_map/ppermute | solution.py:68
  79.6 1.9 collective-permute-start.20
  81.5 4.6 %collective-permute-start.6 = (bf16[16,8,240]{2,1,0:T(8,128)(2,1)S(1)}, bf16[16,8,240]{2,1,0:T(8,128)(2,1)S(1)}, u32[]{:S(2)}, u32[]{:S(2)}) collective-permute-start(bf16[16,8,240]{2,1,0:T(8,128)(2,1)S(1)} %collective-permute-done.5), channel_id=1, source_target_pairs={{0,992},{32,0},{64,32},{96,64},{128,96},{160,128},{192,160},{224,1... | collective-permute-start | bytes 184328 | tf_op jit(solution)/shard_map/ppermute | solution.py:68
  86.1 1.9 collective-permute-start.21
  88.1 4.6 %collective-permute-start.7 = (bf16[16,8,240]{2,1,0:T(8,128)(2,1)S(1)}, bf16[16,8,240]{2,1,0:T(8,128)(2,1)S(1)}, u32[]{:S(2)}, u32[]{:S(2)}) collective-permute-start(bf16[16,8,240]{2,1,0:T(8,128)(2,1)S(1)} %collective-permute-done.6), channel_id=1, source_target_pairs={{0,992},{32,0},{64,32},{96,64},{128,96},{160,128},{192,160},{224,1... | collective-permute-start | bytes 184328 | tf_op jit(solution)/shard_map/ppermute | solution.py:68
  92.7 0.4 collective-permute-done.21
  93.1 1.9 collective-permute-start.22
  95.1 5.2 %collective-permute-start.8 = (bf16[16,8,240]{2,1,0:T(8,128)(2,1)S(1)}, bf16[16,8,240]{2,1,0:T(8,128)(2,1)S(1)}, u32[]{:S(2)}, u32[]{:S(2)}) collective-permute-start(bf16[16,8,240]{2,1,0:T(8,128)(2,1)S(1)} %collective-permute-done.7), channel_id=1, source_target_pairs={{0,992},{32,0},{64,32},{96,64},{128,96},{160,128},{192,160},{224,1... | collective-permute-start | bytes 184328 | tf_op jit(solution)/shard_map/ppermute | solution.py:68
  100.3 1.9 collective-permute-start.23
  102.3 5.2 %collective-permute-start.9 = (bf16[16,8,240]{2,1,0:T(8,128)(2,1)S(1)}, bf16[16,8,240]{2,1,0:T(8,128)(2,1)S(1)}, u32[]{:S(2)}, u32[]{:S(2)}) collective-permute-start(bf16[16,8,240]{2,1,0:T(8,128)(2,1)S(1)} %collective-permute-done.8), channel_id=1, source_target_pairs={{0,992},{32,0},{64,32},{96,64},{128,96},{160,128},{192,160},{224,1... | collective-permute-start | bytes 184328 | tf_op jit(solution)/shard_map/ppermute | solution.py:68
  107.5 1.9 collective-permute-start.24
  109.4 5.0 %collective-permute-start.10 = (bf16[16,8,240]{2,1,0:T(8,128)(2,1)S(1)}, bf16[16,8,240]{2,1,0:T(8,128)(2,1)S(1)}, u32[]{:S(2)}, u32[]{:S(2)}) collective-permute-start(bf16[16,8,240]{2,1,0:T(8,128)(2,1)S(1)} %collective-permute-done.9), channel_id=1, source_target_pairs={{0,992},{32,0},{64,32},{96,64},{128,96},{160,128},{192,160},{224,1... | collective-permute-start | bytes 184328 | tf_op jit(solution)/shard_map/ppermute | solution.py:68
  114.4 1.9 collective-permute-start.25
  116.4 4.7 %collective-permute-start.11 = (bf16[16,8,240]{2,1,0:T(8,128)(2,1)S(1)}, bf16[16,8,240]{2,1,0:T(8,128)(2,1)S(1)}, u32[]{:S(2)}, u32[]{:S(2)}) collective-permute-start(bf16[16,8,240]{2,1,0:T(8,128)(2,1)S(1)} %collective-permute-done.10), channel_id=1, source_target_pairs={{0,992},{32,0},{64,32},{96,64},{128,96},{160,128},{192,160},{224,1... | collective-permute-start | bytes 184328 | tf_op jit(solution)/shard_map/ppermute | solution.py:68
  121.0 1.9 collective-permute-start.26
  123.0 4.6 %collective-permute-start.12 = (bf16[16,8,240]{2,1,0:T(8,128)(2,1)S(1)}, bf16[16,8,240]{2,1,0:T(8,128)(2,1)S(1)}, u32[]{:S(2)}, u32[]{:S(2)}) collective-permute-start(bf16[16,8,240]{2,1,0:T(8,128)(2,1)S(1)} %collective-permute-done.11), channel_id=1, source_target_pairs={{0,992},{32,0},{64,32},{96,64},{128,96},{160,128},{192,160},{224,1... | collective-permute-start | bytes 184328 | tf_op jit(solution)/shard_map/ppermute | solution.py:68
  127.6 1.9 collective-permute-start.27
  129.5 4.6 %collective-permute-start.13 = (bf16[16,8,240]{2,1,0:T(8,128)(2,1)S(1)}, bf16[16,8,240]{2,1,0:T(8,128)(2,1)S(1)}, u32[]{:S(2)}, u32[]{:S(2)}) collective-permute-start(bf16[16,8,240]{2,1,0:T(8,128)(2,1)S(1)} %collective-permute-done.12), channel_id=1, source_target_pairs={{0,992},{32,0},{64,32},{96,64},{128,96},{160,128},{192,160},{224,1... | collective-permute-start | bytes 184328 | tf_op jit(solution)/shard_map/ppermute | solution.py:68
  134.3 1.9 collective-permute-start.28
  136.3 4.6 %collective-permute-start.14 = (bf16[16,8,240]{2,1,0:T(8,128)(2,1)S(1)}, bf16[16,8,240]{2,1,0:T(8,128)(2,1)S(1)}, u32[]{:S(2)}, u32[]{:S(2)}) collective-permute-start(bf16[16,8,240]{2,1,0:T(8,128)(2,1)S(1)} %collective-permute-done.13), channel_id=1, source_target_pairs={{0,992},{32,0},{64,32},{96,64},{128,96},{160,128},{192,160},{224,1... | collective-permute-start | bytes 184328 | tf_op jit(solution)/shard_map/ppermute | solution.py:68
  140.8 1.9 collective-permute-start.29
  142.8 4.9 %collective-permute-done.29 = bf16[16,8,240]{2,1,0:T(8,128)(2,1)S(1)} collective-permute-done((bf16[16,8,240]{2,1,0:T(8,128)(2,1)S(1)}, bf16[16,8,240]{2,1,0:T(8,128)(2,1)S(1)}, u32[]{:S(2)}, u32[]{:S(2)}) %collective-permute-start.29) | collective-permute-done | bytes 61472 | tf_op jit(solution)/shard_map/ppermute | solution.py:65
  147.7 2.1 collective-permute-start.30
  149.8 4.3 %collective-permute-done.30 = bf16[16,8,240]{2,1,0:T(8,128)(2,1)S(1)} collective-permute-done((bf16[16,8,240]{2,1,0:T(8,128)(2,1)S(1)}, bf16[16,8,240]{2,1,0:T(8,128)(2,1)S(1)}, u32[]{:S(2)}, u32[]{:S(2)}) %collective-permute-start.30) | collective-permute-done | bytes 61472 | tf_op jit(solution)/shard_map/ppermute | solution.py:65
  154.4 1.4 slice.32
  155.8 2.0 gather_fusion
  157.7 1.9 copy.62
  159.7 1.9 broadcast_select_fusion.1
  161.6 1.6 slice.34
  163.2 1.9 copy.76
  165.1 1.4 maximum_bitcast_fusion
  166.5 1.5 fusion.6
  168.0 0.6 copy.68
  168.6 0.5 reshape.301
  169.7 1.5 copy.64
  171.2 2.4 copy.70
  173.6 0.4 fusion.4
  174.0 1.5 select_reduce_fusion.2
  175.5 1.1 copy.71
  176.6 1.3 mul.38
  178.1 3.4 %select_reduce_fusion = (s32[32,32,3]{1,2,0:T(4,128)S(1)}, s32[32,32,3]{1,2,0:T(4,128)S(1)}) fusion(s32[64]{0:T(128)S(1)} %and_select_fusion, s32[32,32,64]{2,1,0:T(8,128)S(1)} %bitcast.96, pred[32,32,64]{2,1,0:T(8,128)(4,1)S(1)} %fusion.4, s32[32,32,64]{2,1,0:T(8,128)S(1)} %fusion.5), kind=kLoop, calls=%fused_computation.8 | loop fusion | flops 1173504 | bytes 614656 | tf_op jit(solution)/shard_map/reduce_sum | solution.py:32
  182.1 4.3 %pad_maximum_fusion = bf16[8192,240]{1,0:T(8,128)(2,1)} fusion(bf16[4096,240]{1,0:T(8,128)(2,1)} %bitcast.98, bf16[4096,240]{1,0:T(8,128)(2,1)S(1)} %bitcast.94), kind=kLoop, calls=%fused_computation.6 | loop fusion | flops 7864320 | bytes 7864320 | tf_op jit(solution)/shard_map/concatenate | solution.py:72
  186.5 12.8 %gather_fusion.1 = bf16[3072,240]{1,0:T(8,128)(2,1)S(1)} fusion(bf16[8192,240]{1,0:T(8,128)(2,1)} %pad_maximum_fusion, s32[3072]{0:T(1024)S(1)} %broadcast_clamp_fusion), kind=kCustom, calls=%fused_computation.1 | custom fusion | bytes 2961408 | tf_op jit(solution)/shard_map/jit(_take)/gather | solution.py:91
  199.2 0.7 copy.75
  200.5 2.8 %broadcast_select_fusion = bf16[3072,4,224]{0,2,1:T(8,128)(2,1)} fusion(pred[3072,4]{0,1:T(4,128)(4,1)S(1)} %iota_compare_fusion.1, bf16[3072,224]{0,1:T(8,128)(2,1)S(1)} %copy.75), kind=kLoop, calls=%fused_computation.5 | loop fusion | flops 2752512 | bytes 6893568 | tf_op jit(solution)/shard_map/jit(_where)/select_n | solution.py:93
  203.3 46.8 %all-gather.4.cloned.1.call-done = bf16[3072,1024]{1,0:T(8,128)(2,1)} async-done(((bf16[96,1024]{1,0:T(8,128)(2,1)}), bf16[3072,1024]{1,0:T(8,128)(2,1)}) %all-gather.4.cloned.1.call-update) | async-done | bytes 6291472 | tf_op jit(solution)/shard_map/all_gather | solution.py:54
  250.1 10.7 %fusion.2 = bf16[1024,896]{0,1:T(8,128)(2,1)} fusion(bf16[3072,896]{0,1:T(8,128)(2,1)} %bitcast.93, bf16[3072,1024]{1,0:T(8,128)(2,1)} %all-gather.4.cloned.1.call-done, f32[3072]{0:T(1024)S(1)} %mul.38), kind=kOutput, calls=%fused_computation.7 | convolution fusion | flops 5647499264 | bytes 13643776 | tf_op jit(solution)/shard_map/dot_general | solution.py:95
  (88 shorter events, 3.1 us)
Async XLA Ops:
  6.5 155.0 %all-gather.6.cloned.1.call-start = ((), (), s32[]{:S(2)}) async-start(), calls=%async_computation.2 | async-start | bytes 2162688 | tf_op jit(solution)/shard_map/all_gather | solution.py:52
  34.5 215.7 %all-gather.4.cloned.1.call-start = ((), (), s32[]{:S(2)}) async-start(), calls=%async_computation.1 | async-start | bytes 6488064 | tf_op jit(solution)/shard_map/all_gather | solution.py:54
  36.6 11.9 %collective-permute-start = (bf16[16,8,240]{2,1,0:T(8,128)(2,1)S(1)}, bf16[16,8,240]{2,1,0:T(8,128)(2,1)S(1)}, u32[]{:S(2)}, u32[]{:S(2)}) collective-permute-start(bf16[16,8,240]{2,1,0:T(8,128)(2,1)S(1)} %slice.21), channel_id=1, source_target_pairs={{0,992},{32,0},{64,32},{96,64},{128,96},{160,128},{192,160},{224,1... | collective-permute-start | bytes 184328 | tf_op jit(solution)/shard_map/ppermute | solution.py:68
  46.5 6.6 %collective-permute-start.15 = (bf16[16,8,240]{2,1,0:T(8,128)(2,1)S(1)}, bf16[16,8,240]{2,1,0:T(8,128)(2,1)S(1)}, u32[]{:S(2)}, u32[]{:S(2)}) collective-permute-start(bf16[16,8,240]{2,1,0:T(8,128)(2,1)S(1)} %slice.21), channel_id=1, source_target_pairs={{0,32},{32,64},{64,96},{96,128},{128,160},{160,192},{192,224},{224... | collective-permute-start | bytes 184328 | tf_op jit(solution)/shard_map/ppermute | solution.py:65
  48.5 6.5 %collective-permute-start.1 = (bf16[16,8,240]{2,1,0:T(8,128)(2,1)S(1)}, bf16[16,8,240]{2,1,0:T(8,128)(2,1)S(1)}, u32[]{:S(2)}, u32[]{:S(2)}) collective-permute-start(bf16[16,8,240]{2,1,0:T(8,128)(2,1)S(1)} %collective-permute-done), channel_id=1, source_target_pairs={{0,992},{32,0},{64,32},{96,64},{128,96},{160,128},{192,160},{224,1... | collective-permute-start | bytes 184328 | tf_op jit(solution)/shard_map/ppermute | solution.py:68
  53.1 6.5 %collective-permute-start.16 = (bf16[16,8,240]{2,1,0:T(8,128)(2,1)S(1)}, bf16[16,8,240]{2,1,0:T(8,128)(2,1)S(1)}, u32[]{:S(2)}, u32[]{:S(2)}) collective-permute-start(bf16[16,8,240]{2,1,0:T(8,128)(2,1)S(1)} %collective-permute-done.15), channel_id=1, source_target_pairs={{0,32},{32,64},{64,96},{96,128},{128,160},{160,192},{192,224},{224... | collective-permute-start | bytes 184328 | tf_op jit(solution)/shard_map/ppermute | solution.py:65
  55.1 6.5 %collective-permute-start.2 = (bf16[16,8,240]{2,1,0:T(8,128)(2,1)S(1)}, bf16[16,8,240]{2,1,0:T(8,128)(2,1)S(1)}, u32[]{:S(2)}, u32[]{:S(2)}) collective-permute-start(bf16[16,8,240]{2,1,0:T(8,128)(2,1)S(1)} %collective-permute-done.1), channel_id=1, source_target_pairs={{0,992},{32,0},{64,32},{96,64},{128,96},{160,128},{192,160},{224,1... | collective-permute-start | bytes 184328 | tf_op jit(solution)/shard_map/ppermute | solution.py:68
  59.7 6.8 %collective-permute-start.17 = (bf16[16,8,240]{2,1,0:T(8,128)(2,1)S(1)}, bf16[16,8,240]{2,1,0:T(8,128)(2,1)S(1)}, u32[]{:S(2)}, u32[]{:S(2)}) collective-permute-start(bf16[16,8,240]{2,1,0:T(8,128)(2,1)S(1)} %collective-permute-done.16), channel_id=1, source_target_pairs={{0,32},{32,64},{64,96},{96,128},{128,160},{160,192},{192,224},{224... | collective-permute-start | bytes 184328 | tf_op jit(solution)/shard_map/ppermute | solution.py:65
  61.6 6.8 %collective-permute-start.3 = (bf16[16,8,240]{2,1,0:T(8,128)(2,1)S(1)}, bf16[16,8,240]{2,1,0:T(8,128)(2,1)S(1)}, u32[]{:S(2)}, u32[]{:S(2)}) collective-permute-start(bf16[16,8,240]{2,1,0:T(8,128)(2,1)S(1)} %collective-permute-done.2), channel_id=1, source_target_pairs={{0,992},{32,0},{64,32},{96,64},{128,96},{160,128},{192,160},{224,1... | collective-permute-start | bytes 184328 | tf_op jit(solution)/shard_map/ppermute | solution.py:68
  66.5 6.5 %collective-permute-start.18 = (bf16[16,8,240]{2,1,0:T(8,128)(2,1)S(1)}, bf16[16,8,240]{2,1,0:T(8,128)(2,1)S(1)}, u32[]{:S(2)}, u32[]{:S(2)}) collective-permute-start(bf16[16,8,240]{2,1,0:T(8,128)(2,1)S(1)} %collective-permute-done.17), channel_id=1, source_target_pairs={{0,32},{32,64},{64,96},{96,128},{128,160},{160,192},{192,224},{224... | collective-permute-start | bytes 184328 | tf_op jit(solution)/shard_map/ppermute | solution.py:65
  68.5 6.5 %collective-permute-start.4 = (bf16[16,8,240]{2,1,0:T(8,128)(2,1)S(1)}, bf16[16,8,240]{2,1,0:T(8,128)(2,1)S(1)}, u32[]{:S(2)}, u32[]{:S(2)}) collective-permute-start(bf16[16,8,240]{2,1,0:T(8,128)(2,1)S(1)} %collective-permute-done.3), channel_id=1, source_target_pairs={{0,992},{32,0},{64,32},{96,64},{128,96},{160,128},{192,160},{224,1... | collective-permute-start | bytes 184328 | tf_op jit(solution)/shard_map/ppermute | solution.py:68
  73.0 6.5 %collective-permute-start.19 = (bf16[16,8,240]{2,1,0:T(8,128)(2,1)S(1)}, bf16[16,8,240]{2,1,0:T(8,128)(2,1)S(1)}, u32[]{:S(2)}, u32[]{:S(2)}) collective-permute-start(bf16[16,8,240]{2,1,0:T(8,128)(2,1)S(1)} %collective-permute-done.18), channel_id=1, source_target_pairs={{0,32},{32,64},{64,96},{96,128},{128,160},{160,192},{192,224},{224... | collective-permute-start | bytes 184328 | tf_op jit(solution)/shard_map/ppermute | solution.py:65
  75.0 6.5 %collective-permute-start.5 = (bf16[16,8,240]{2,1,0:T(8,128)(2,1)S(1)}, bf16[16,8,240]{2,1,0:T(8,128)(2,1)S(1)}, u32[]{:S(2)}, u32[]{:S(2)}) collective-permute-start(bf16[16,8,240]{2,1,0:T(8,128)(2,1)S(1)} %collective-permute-done.4), channel_id=1, source_target_pairs={{0,992},{32,0},{64,32},{96,64},{128,96},{160,128},{192,160},{224,1... | collective-permute-start | bytes 184328 | tf_op jit(solution)/shard_map/ppermute | solution.py:68
  79.6 6.5 %collective-permute-start.20 = (bf16[16,8,240]{2,1,0:T(8,128)(2,1)S(1)}, bf16[16,8,240]{2,1,0:T(8,128)(2,1)S(1)}, u32[]{:S(2)}, u32[]{:S(2)}) collective-permute-start(bf16[16,8,240]{2,1,0:T(8,128)(2,1)S(1)} %collective-permute-done.19), channel_id=1, source_target_pairs={{0,32},{32,64},{64,96},{96,128},{128,160},{160,192},{192,224},{224... | collective-permute-start | bytes 184328 | tf_op jit(solution)/shard_map/ppermute | solution.py:65
  81.5 6.5 %collective-permute-start.6 = (bf16[16,8,240]{2,1,0:T(8,128)(2,1)S(1)}, bf16[16,8,240]{2,1,0:T(8,128)(2,1)S(1)}, u32[]{:S(2)}, u32[]{:S(2)}) collective-permute-start(bf16[16,8,240]{2,1,0:T(8,128)(2,1)S(1)} %collective-permute-done.5), channel_id=1, source_target_pairs={{0,992},{32,0},{64,32},{96,64},{128,96},{160,128},{192,160},{224,1... | collective-permute-start | bytes 184328 | tf_op jit(solution)/shard_map/ppermute | solution.py:68
  86.1 7.0 %collective-permute-start.21 = (bf16[16,8,240]{2,1,0:T(8,128)(2,1)S(1)}, bf16[16,8,240]{2,1,0:T(8,128)(2,1)S(1)}, u32[]{:S(2)}, u32[]{:S(2)}) collective-permute-start(bf16[16,8,240]{2,1,0:T(8,128)(2,1)S(1)} %collective-permute-done.20), channel_id=1, source_target_pairs={{0,32},{32,64},{64,96},{96,128},{128,160},{160,192},{192,224},{224... | collective-permute-start | bytes 184328 | tf_op jit(solution)/shard_map/ppermute | solution.py:65
  88.1 7.0 %collective-permute-start.7 = (bf16[16,8,240]{2,1,0:T(8,128)(2,1)S(1)}, bf16[16,8,240]{2,1,0:T(8,128)(2,1)S(1)}, u32[]{:S(2)}, u32[]{:S(2)}) collective-permute-start(bf16[16,8,240]{2,1,0:T(8,128)(2,1)S(1)} %collective-permute-done.6), channel_id=1, source_target_pairs={{0,992},{32,0},{64,32},{96,64},{128,96},{160,128},{192,160},{224,1... | collective-permute-start | bytes 184328 | tf_op jit(solution)/shard_map/ppermute | solution.py:68
  93.1 7.2 %collective-permute-start.22 = (bf16[16,8,240]{2,1,0:T(8,128)(2,1)S(1)}, bf16[16,8,240]{2,1,0:T(8,128)(2,1)S(1)}, u32[]{:S(2)}, u32[]{:S(2)}) collective-permute-start(bf16[16,8,240]{2,1,0:T(8,128)(2,1)S(1)} %collective-permute-done.21), channel_id=1, source_target_pairs={{0,32},{32,64},{64,96},{96,128},{128,160},{160,192},{192,224},{224... | collective-permute-start | bytes 184328 | tf_op jit(solution)/shard_map/ppermute | solution.py:65
  95.1 7.2 %collective-permute-start.8 = (bf16[16,8,240]{2,1,0:T(8,128)(2,1)S(1)}, bf16[16,8,240]{2,1,0:T(8,128)(2,1)S(1)}, u32[]{:S(2)}, u32[]{:S(2)}) collective-permute-start(bf16[16,8,240]{2,1,0:T(8,128)(2,1)S(1)} %collective-permute-done.7), channel_id=1, source_target_pairs={{0,992},{32,0},{64,32},{96,64},{128,96},{160,128},{192,160},{224,1... | collective-permute-start | bytes 184328 | tf_op jit(solution)/shard_map/ppermute | solution.py:68
  100.3 7.2 %collective-permute-start.23 = (bf16[16,8,240]{2,1,0:T(8,128)(2,1)S(1)}, bf16[16,8,240]{2,1,0:T(8,128)(2,1)S(1)}, u32[]{:S(2)}, u32[]{:S(2)}) collective-permute-start(bf16[16,8,240]{2,1,0:T(8,128)(2,1)S(1)} %collective-permute-done.22), channel_id=1, source_target_pairs={{0,32},{32,64},{64,96},{96,128},{128,160},{160,192},{192,224},{224... | collective-permute-start | bytes 184328 | tf_op jit(solution)/shard_map/ppermute | solution.py:65
  102.3 7.2 %collective-permute-start.9 = (bf16[16,8,240]{2,1,0:T(8,128)(2,1)S(1)}, bf16[16,8,240]{2,1,0:T(8,128)(2,1)S(1)}, u32[]{:S(2)}, u32[]{:S(2)}) collective-permute-start(bf16[16,8,240]{2,1,0:T(8,128)(2,1)S(1)} %collective-permute-done.8), channel_id=1, source_target_pairs={{0,992},{32,0},{64,32},{96,64},{128,96},{160,128},{192,160},{224,1... | collective-permute-start | bytes 184328 | tf_op jit(solution)/shard_map/ppermute | solution.py:68
  107.5 7.0 %collective-permute-start.24 = (bf16[16,8,240]{2,1,0:T(8,128)(2,1)S(1)}, bf16[16,8,240]{2,1,0:T(8,128)(2,1)S(1)}, u32[]{:S(2)}, u32[]{:S(2)}) collective-permute-start(bf16[16,8,240]{2,1,0:T(8,128)(2,1)S(1)} %collective-permute-done.23), channel_id=1, source_target_pairs={{0,32},{32,64},{64,96},{96,128},{128,160},{160,192},{192,224},{224... | collective-permute-start | bytes 184328 | tf_op jit(solution)/shard_map/ppermute | solution.py:65
  109.4 7.0 %collective-permute-start.10 = (bf16[16,8,240]{2,1,0:T(8,128)(2,1)S(1)}, bf16[16,8,240]{2,1,0:T(8,128)(2,1)S(1)}, u32[]{:S(2)}, u32[]{:S(2)}) collective-permute-start(bf16[16,8,240]{2,1,0:T(8,128)(2,1)S(1)} %collective-permute-done.9), channel_id=1, source_target_pairs={{0,992},{32,0},{64,32},{96,64},{128,96},{160,128},{192,160},{224,1... | collective-permute-start | bytes 184328 | tf_op jit(solution)/shard_map/ppermute | solution.py:68
  114.4 6.6 %collective-permute-start.25 = (bf16[16,8,240]{2,1,0:T(8,128)(2,1)S(1)}, bf16[16,8,240]{2,1,0:T(8,128)(2,1)S(1)}, u32[]{:S(2)}, u32[]{:S(2)}) collective-permute-start(bf16[16,8,240]{2,1,0:T(8,128)(2,1)S(1)} %collective-permute-done.24), channel_id=1, source_target_pairs={{0,32},{32,64},{64,96},{96,128},{128,160},{160,192},{192,224},{224... | collective-permute-start | bytes 184328 | tf_op jit(solution)/shard_map/ppermute | solution.py:65
  116.4 6.6 %collective-permute-start.11 = (bf16[16,8,240]{2,1,0:T(8,128)(2,1)S(1)}, bf16[16,8,240]{2,1,0:T(8,128)(2,1)S(1)}, u32[]{:S(2)}, u32[]{:S(2)}) collective-permute-start(bf16[16,8,240]{2,1,0:T(8,128)(2,1)S(1)} %collective-permute-done.10), channel_id=1, source_target_pairs={{0,992},{32,0},{64,32},{96,64},{128,96},{160,128},{192,160},{224,1... | collective-permute-start | bytes 184328 | tf_op jit(solution)/shard_map/ppermute | solution.py:68
  121.0 6.5 %collective-permute-start.26 = (bf16[16,8,240]{2,1,0:T(8,128)(2,1)S(1)}, bf16[16,8,240]{2,1,0:T(8,128)(2,1)S(1)}, u32[]{:S(2)}, u32[]{:S(2)}) collective-permute-start(bf16[16,8,240]{2,1,0:T(8,128)(2,1)S(1)} %collective-permute-done.25), channel_id=1, source_target_pairs={{0,32},{32,64},{64,96},{96,128},{128,160},{160,192},{192,224},{224... | collective-permute-start | bytes 184328 | tf_op jit(solution)/shard_map/ppermute | solution.py:65
  123.0 6.5 %collective-permute-start.12 = (bf16[16,8,240]{2,1,0:T(8,128)(2,1)S(1)}, bf16[16,8,240]{2,1,0:T(8,128)(2,1)S(1)}, u32[]{:S(2)}, u32[]{:S(2)}) collective-permute-start(bf16[16,8,240]{2,1,0:T(8,128)(2,1)S(1)} %collective-permute-done.11), channel_id=1, source_target_pairs={{0,992},{32,0},{64,32},{96,64},{128,96},{160,128},{192,160},{224,1... | collective-permute-start | bytes 184328 | tf_op jit(solution)/shard_map/ppermute | solution.py:68
  127.6 6.7 %collective-permute-start.27 = (bf16[16,8,240]{2,1,0:T(8,128)(2,1)S(1)}, bf16[16,8,240]{2,1,0:T(8,128)(2,1)S(1)}, u32[]{:S(2)}, u32[]{:S(2)}) collective-permute-start(bf16[16,8,240]{2,1,0:T(8,128)(2,1)S(1)} %collective-permute-done.26), channel_id=1, source_target_pairs={{0,32},{32,64},{64,96},{96,128},{128,160},{160,192},{192,224},{224... | collective-permute-start | bytes 184328 | tf_op jit(solution)/shard_map/ppermute | solution.py:65
  129.5 6.7 %collective-permute-start.13 = (bf16[16,8,240]{2,1,0:T(8,128)(2,1)S(1)}, bf16[16,8,240]{2,1,0:T(8,128)(2,1)S(1)}, u32[]{:S(2)}, u32[]{:S(2)}) collective-permute-start(bf16[16,8,240]{2,1,0:T(8,128)(2,1)S(1)} %collective-permute-done.12), channel_id=1, source_target_pairs={{0,992},{32,0},{64,32},{96,64},{128,96},{160,128},{192,160},{224,1... | collective-permute-start | bytes 184328 | tf_op jit(solution)/shard_map/ppermute | solution.py:68
  134.3 6.5 %collective-permute-start.28 = (bf16[16,8,240]{2,1,0:T(8,128)(2,1)S(1)}, bf16[16,8,240]{2,1,0:T(8,128)(2,1)S(1)}, u32[]{:S(2)}, u32[]{:S(2)}) collective-permute-start(bf16[16,8,240]{2,1,0:T(8,128)(2,1)S(1)} %collective-permute-done.27), channel_id=1, source_target_pairs={{0,32},{32,64},{64,96},{96,128},{128,160},{160,192},{192,224},{224... | collective-permute-start | bytes 184328 | tf_op jit(solution)/shard_map/ppermute | solution.py:65
  136.3 13.6 %collective-permute-start.14 = (bf16[16,8,240]{2,1,0:T(8,128)(2,1)S(1)}, bf16[16,8,240]{2,1,0:T(8,128)(2,1)S(1)}, u32[]{:S(2)}, u32[]{:S(2)}) collective-permute-start(bf16[16,8,240]{2,1,0:T(8,128)(2,1)S(1)} %collective-permute-done.13), channel_id=1, source_target_pairs={{0,992},{32,0},{64,32},{96,64},{128,96},{160,128},{192,160},{224,1... | collective-permute-start | bytes 184328 | tf_op jit(solution)/shard_map/ppermute | solution.py:68
  140.8 6.9 %collective-permute-start.29 = (bf16[16,8,240]{2,1,0:T(8,128)(2,1)S(1)}, bf16[16,8,240]{2,1,0:T(8,128)(2,1)S(1)}, u32[]{:S(2)}, u32[]{:S(2)}) collective-permute-start(bf16[16,8,240]{2,1,0:T(8,128)(2,1)S(1)} %collective-permute-done.28), channel_id=1, source_target_pairs={{0,32},{32,64},{64,96},{96,128},{128,160},{160,192},{192,224},{224... | collective-permute-start | bytes 184328 | tf_op jit(solution)/shard_map/ppermute | solution.py:65
  147.7 6.5 %collective-permute-start.30 = (bf16[16,8,240]{2,1,0:T(8,128)(2,1)S(1)}, bf16[16,8,240]{2,1,0:T(8,128)(2,1)S(1)}, u32[]{:S(2)}, u32[]{:S(2)}) collective-permute-start(bf16[16,8,240]{2,1,0:T(8,128)(2,1)S(1)} %collective-permute-done.29), channel_id=1, source_target_pairs={{0,32},{32,64},{64,96},{96,128},{128,160},{160,192},{192,224},{224... | collective-permute-start | bytes 184328 | tf_op jit(solution)/shard_map/ppermute | solution.py:65
Sparse Core Ops, SparseCore 0:
  34.6 115.2 all-gather.5
  154.2 95.9 all-gather.3

commit v7 on v5

--- a/solution.py
+++ b/solution.py
@@ -64,11 +64,13 @@
         if step < n_exp - half:
             bwd = lax.ppermute(bwd, "expert", bwd_perm)
             ahead.append(bwd)
-    ring = jnp.stack(ahead + behind[::-1], axis=0)
+    pieces = ahead + behind[::-1]
+    ring = jnp.stack(pieces, axis=0)
     tokens = ring.reshape(-1, ring.shape[-1])
 
     relative = (jnp.arange(n_exp, dtype=jnp.int32) - me_exp) % n_exp
-    meta_src = jnp.take(ring[:, :, :, width:], relative, axis=0)
+    meta_ring = jnp.stack([piece[:, :, width:] for piece in pieces], axis=0)
+    meta_src = jnp.take(meta_ring, relative, axis=0)
     meta_gs = jnp.transpose(meta_src, (1, 0, 2, 3))
     weight, label, token = slot_tables(meta_gs, me_exp, relative, capacity)
 

time: 232 us -> 360 us (1.55)
  local copies, waits for them, and re-layouts: 28.9 us -> 116 us
  waiting for transfers between devices: 31.4 us -> 66.5 us
    another operation x1 -> x33, local copies, waits for them, and re-layouts: 0.01 us -> 45.4 us  [the longest x32 45.4 us: per_device(): ring = jnp.stack(pieces, axis=0)]
    unnamed x35 -> x83, local copies, waits for them, and re-layouts: 5.79 us -> 48.7 us
    ppermute x15, waiting for transfers between devices: 7.61 us -> 41.1 us  [per_device(): bwd = lax.ppermute(bwd, 'expert', bwd_perm)]
    ppermute x16, waiting for transfers between devices: 17.1 us -> 21.3 us  [per_device(): fwd = lax.ppermute(fwd, 'expert', fwd_perm)]
  transfers between devices with their start and end apart: 33 -> 33, of which waited for: 25 -> 25; matrix products, arithmetic and copies ran while one was open for 16% -> 35% of each run, Pallas kernels for 0% -> 0%
where the time goes in v7:
time: 360 us; the launch traced here: 356 us
  starting transfers between devices  135 us (38%)
  local copies, waits for them, and re-layouts  116 us (32%)
  waiting for transfers between devices  66.5 us (18%)
  between operations  14.1 us (4%)
  other arithmetic  12.9 us (4%)
  matrix products  11.1 us (3%)
    ppermute x15, starting transfers between devices, per_device(): bwd = lax.ppermute(bwd, 'expert', bwd_perm)  87.8 us
    unnamed x83, local copies, waits for them, and re-layouts  48.7 us
    another operation x32, local copies, waits for them, and re-layouts, per_device(): ring = jnp.stack(pieces, axis=0)  45.4 us
    ppermute x15, waiting for transfers between devices, per_device(): bwd = lax.ppermute(bwd, 'expert', bwd_perm)  41.1 us
    ppermute x16, starting transfers between devices, per_device(): fwd = lax.ppermute(fwd, 'expert', fwd_perm)  30.8 us
    ppermute x16, waiting for transfers between devices, per_device(): fwd = lax.ppermute(fwd, 'expert', fwd_perm)  21.3 us
    all_to_all x1, starting transfers between devices, per_device(): cols = lax.all_to_all(cols, 'dp', 0, 0, tiled=True)  16.7 us
    gather x1, local copies, waits for them, and re-layouts, per_device(): grad_rows = jnp.take(tokens, token, axis=0, mode='clip')[:, :width]  12.8 us
  transfers between devices with their start and end apart: 33, of which 25 were waited for; matrix products, arithmetic and copies ran while one was open for 35% of the time, Pallas kernels for 0%

profile of v7, /device:TPU:2, one launch (start us, length us, event | category | flops | bytes accessed | tf_op | source)
XLA Modules:
  0.0 355.7 jit_solution(17494223887282551231)
XLA Ops:
  9.9 16.7 %all-to-all-start = ((bf16[32,8,240]{2,1,0:T(8,128)(2,1)}), bf16[32,8,240]{2,1,0:T(8,128)(2,1)S(1)}, u32[]{:S(2)}, u32[]{:S(2)}) async-start(bf16[32,8,240]{2,1,0:T(8,128)(2,1)} %pad_maximum_fusion), calls=%async_computation | async-start | bytes 262144 | tf_op jit(solution)/shard_map/all_to_all | solution.py:52
  29.2 4.1 %all-to-all-done = bf16[32,8,240]{2,1,0:T(8,128)(2,1)S(1)} async-done(((bf16[32,8,240]{2,1,0:T(8,128)(2,1)}), bf16[32,8,240]{2,1,0:T(8,128)(2,1)S(1)}, u32[]{:S(2)}, u32[]{:S(2)}) %all-to-all-start) | async-done | bytes 122912 | tf_op jit(solution)/shard_map/all_to_all | solution.py:52
  33.6 9.5 %collective-permute-start = (bf16[32,8,240]{0,2,1:T(8,128)(2,1)S(1)}, bf16[32,8,240]{0,2,1:T(8,128)(2,1)S(1)}, u32[]{:S(2)}, u32[]{:S(2)}) collective-permute-start(bf16[32,8,240]{0,2,1:T(8,128)(2,1)S(1)} %copy.130), channel_id=1, source_target_pairs={{0,992},{32,0},{64,32},{96,64},{128,96},{160,128},{192,160},{224,1... | collective-permute-start | bytes 368648 | tf_op jit(solution)/shard_map/ppermute | solution.py:65
  43.1 1.9 collective-permute-start.15
  45.7 8.2 %collective-permute-done = bf16[32,8,240]{0,2,1:T(8,128)(2,1)S(1)} collective-permute-done((bf16[32,8,240]{0,2,1:T(8,128)(2,1)S(1)}, bf16[32,8,240]{0,2,1:T(8,128)(2,1)S(1)}, u32[]{:S(2)}, u32[]{:S(2)}) %collective-permute-start) | collective-permute-done | bytes 122912 | tf_op jit(solution)/shard_map/ppermute | solution.py:65
  53.9 5.6 %collective-permute-start.1 = (bf16[32,8,240]{0,2,1:T(8,128)(2,1)S(1)}, bf16[32,8,240]{0,2,1:T(8,128)(2,1)}, u32[]{:S(2)}, u32[]{:S(2)}) collective-permute-start(bf16[32,8,240]{0,2,1:T(8,128)(2,1)S(1)} %collective-permute-done), channel_id=1, source_target_pairs={{0,992},{32,0},{64,32},{96,64},{128,96},{160,128},{192,160},{224,1... | collective-permute-start | bytes 368648 | tf_op jit(solution)/shard_map/ppermute | solution.py:65
  59.5 1.9 collective-permute-start.16
  63.2 6.2 %collective-permute-done.1 = bf16[32,8,240]{0,2,1:T(8,128)(2,1)} collective-permute-done((bf16[32,8,240]{0,2,1:T(8,128)(2,1)S(1)}, bf16[32,8,240]{0,2,1:T(8,128)(2,1)}, u32[]{:S(2)}, u32[]{:S(2)}) %collective-permute-start.1) | collective-permute-done | bytes 122912 | tf_op jit(solution)/shard_map/ppermute | solution.py:65
  69.5 5.7 %collective-permute-start.2 = (bf16[32,8,240]{0,2,1:T(8,128)(2,1)}, bf16[32,8,240]{0,2,1:T(8,128)(2,1)}, u32[]{:S(2)}, u32[]{:S(2)}) collective-permute-start(bf16[32,8,240]{0,2,1:T(8,128)(2,1)} %collective-permute-done.1), channel_id=1, source_target_pairs={{0,992},{32,0},{64,32},{96,64},{128,96},{160,128},{192,160},{224,1... | collective-permute-start | bytes 368648 | tf_op jit(solution)/shard_map/ppermute | solution.py:65
  75.2 1.9 collective-permute-start.17
  80.7 3.9 %collective-permute-done.2 = bf16[32,8,240]{0,2,1:T(8,128)(2,1)} collective-permute-done((bf16[32,8,240]{0,2,1:T(8,128)(2,1)}, bf16[32,8,240]{0,2,1:T(8,128)(2,1)}, u32[]{:S(2)}, u32[]{:S(2)}) %collective-permute-start.2) | collective-permute-done | bytes 122912 | tf_op jit(solution)/shard_map/ppermute | solution.py:65
  84.5 5.6 %collective-permute-start.3 = (bf16[32,8,240]{0,2,1:T(8,128)(2,1)}, bf16[32,8,240]{0,2,1:T(8,128)(2,1)}, u32[]{:S(2)}, u32[]{:S(2)}) collective-permute-start(bf16[32,8,240]{0,2,1:T(8,128)(2,1)} %collective-permute-done.2), channel_id=1, source_target_pairs={{0,992},{32,0},{64,32},{96,64},{128,96},{160,128},{192,160},{224,1... | collective-permute-start | bytes 368648 | tf_op jit(solution)/shard_map/ppermute | solution.py:65
  90.1 1.9 collective-permute-start.18
  95.6 2.9 collective-permute-done.3
  98.5 5.6 %collective-permute-start.4 = (bf16[32,8,240]{0,2,1:T(8,128)(2,1)}, bf16[32,8,240]{0,2,1:T(8,128)(2,1)}, u32[]{:S(2)}, u32[]{:S(2)}) collective-permute-start(bf16[32,8,240]{0,2,1:T(8,128)(2,1)} %collective-permute-done.3), channel_id=1, source_target_pairs={{0,992},{32,0},{64,32},{96,64},{128,96},{160,128},{192,160},{224,1... | collective-permute-start | bytes 368648 | tf_op jit(solution)/shard_map/ppermute | solution.py:65
  104.1 1.9 collective-permute-start.19
  108.1 1.9 copy.173
  111.6 5.6 %collective-permute-start.5 = (bf16[32,8,240]{0,2,1:T(8,128)(2,1)}, bf16[32,8,240]{0,2,1:T(8,128)(2,1)}, u32[]{:S(2)}, u32[]{:S(2)}) collective-permute-start(bf16[32,8,240]{0,2,1:T(8,128)(2,1)} %collective-permute-done.4), channel_id=1, source_target_pairs={{0,992},{32,0},{64,32},{96,64},{128,96},{160,128},{192,160},{224,1... | collective-permute-start | bytes 368648 | tf_op jit(solution)/shard_map/ppermute | solution.py:65
  117.2 1.9 collective-permute-start.20
  121.2 1.9 copy.172
  123.9 5.6 %collective-permute-start.6 = (bf16[32,8,240]{0,2,1:T(8,128)(2,1)}, bf16[32,8,240]{0,2,1:T(8,128)(2,1)}, u32[]{:S(2)}, u32[]{:S(2)}) collective-permute-start(bf16[32,8,240]{0,2,1:T(8,128)(2,1)} %collective-permute-done.5), channel_id=1, source_target_pairs={{0,992},{32,0},{64,32},{96,64},{128,96},{160,128},{192,160},{224,1... | collective-permute-start | bytes 368648 | tf_op jit(solution)/shard_map/ppermute | solution.py:65
  129.5 1.9 collective-permute-start.21
  133.4 1.9 copy.171
  136.7 5.6 %collective-permute-start.7 = (bf16[32,8,240]{0,2,1:T(8,128)(2,1)}, bf16[32,8,240]{0,2,1:T(8,128)(2,1)}, u32[]{:S(2)}, u32[]{:S(2)}) collective-permute-start(bf16[32,8,240]{0,2,1:T(8,128)(2,1)} %collective-permute-done.6), channel_id=1, source_target_pairs={{0,992},{32,0},{64,32},{96,64},{128,96},{160,128},{192,160},{224,1... | collective-permute-start | bytes 368648 | tf_op jit(solution)/shard_map/ppermute | solution.py:65
  142.6 1.9 collective-permute-start.22
  146.5 1.9 copy.170
  150.6 5.6 %collective-permute-start.8 = (bf16[32,8,240]{0,2,1:T(8,128)(2,1)}, bf16[32,8,240]{0,2,1:T(8,128)(2,1)}, u32[]{:S(2)}, u32[]{:S(2)}) collective-permute-start(bf16[32,8,240]{0,2,1:T(8,128)(2,1)} %collective-permute-done.7), channel_id=1, source_target_pairs={{0,992},{32,0},{64,32},{96,64},{128,96},{160,128},{192,160},{224,1... | collective-permute-start | bytes 368648 | tf_op jit(solution)/shard_map/ppermute | solution.py:65
  156.8 1.9 collective-permute-start.23
  160.7 1.9 copy.169
  163.3 2.3 collective-permute-done.8
  165.6 5.6 %collective-permute-start.9 = (bf16[32,8,240]{0,2,1:T(8,128)(2,1)}, bf16[32,8,240]{0,2,1:T(8,128)(2,1)}, u32[]{:S(2)}, u32[]{:S(2)}) collective-permute-start(bf16[32,8,240]{0,2,1:T(8,128)(2,1)} %collective-permute-done.8), channel_id=1, source_target_pairs={{0,992},{32,0},{64,32},{96,64},{128,96},{160,128},{192,160},{224,1... | collective-permute-start | bytes 368648 | tf_op jit(solution)/shard_map/ppermute | solution.py:65
  172.1 1.9 collective-permute-start.24
  176.0 1.9 copy.168
  178.5 3.1 collective-permute-done.9
  181.7 5.6 %collective-permute-start.10 = (bf16[32,8,240]{0,2,1:T(8,128)(2,1)}, bf16[32,8,240]{0,2,1:T(8,128)(2,1)}, u32[]{:S(2)}, u32[]{:S(2)}) collective-permute-start(bf16[32,8,240]{0,2,1:T(8,128)(2,1)} %collective-permute-done.9), channel_id=1, source_target_pairs={{0,992},{32,0},{64,32},{96,64},{128,96},{160,128},{192,160},{224,1... | collective-permute-start | bytes 368648 | tf_op jit(solution)/shard_map/ppermute | solution.py:65
  188.5 1.9 collective-permute-start.25
  192.4 1.9 copy.167
  195.0 3.9 %collective-permute-done.10 = bf16[32,8,240]{0,2,1:T(8,128)(2,1)} collective-permute-done((bf16[32,8,240]{0,2,1:T(8,128)(2,1)}, bf16[32,8,240]{0,2,1:T(8,128)(2,1)}, u32[]{:S(2)}, u32[]{:S(2)}) %collective-permute-start.10) | collective-permute-done | bytes 122912 | tf_op jit(solution)/shard_map/ppermute | solution.py:65
  198.9 5.6 %collective-permute-start.11 = (bf16[32,8,240]{0,2,1:T(8,128)(2,1)}, bf16[32,8,240]{0,2,1:T(8,128)(2,1)}, u32[]{:S(2)}, u32[]{:S(2)}) collective-permute-start(bf16[32,8,240]{0,2,1:T(8,128)(2,1)} %collective-permute-done.10), channel_id=1, source_target_pairs={{0,992},{32,0},{64,32},{96,64},{128,96},{160,128},{192,160},{224,1... | collective-permute-start | bytes 368648 | tf_op jit(solution)/shard_map/ppermute | solution.py:65
  205.9 1.9 collective-permute-start.26
  209.9 1.9 copy.166
  212.4 3.2 collective-permute-done.11
  215.6 5.6 %collective-permute-start.12 = (bf16[32,8,240]{0,2,1:T(8,128)(2,1)}, bf16[32,8,240]{0,2,1:T(8,128)(2,1)}, u32[]{:S(2)}, u32[]{:S(2)}) collective-permute-start(bf16[32,8,240]{0,2,1:T(8,128)(2,1)} %collective-permute-done.11), channel_id=1, source_target_pairs={{0,992},{32,0},{64,32},{96,64},{128,96},{160,128},{192,160},{224,1... | collective-permute-start | bytes 368648 | tf_op jit(solution)/shard_map/ppermute | solution.py:65
  222.5 1.9 collective-permute-start.27
  226.5 1.9 copy.165
  229.0 2.4 collective-permute-done.12
  231.4 5.6 %collective-permute-start.13 = (bf16[32,8,240]{0,2,1:T(8,128)(2,1)}, bf16[32,8,240]{0,2,1:T(8,128)(2,1)}, u32[]{:S(2)}, u32[]{:S(2)}) collective-permute-start(bf16[32,8,240]{0,2,1:T(8,128)(2,1)} %collective-permute-done.12), channel_id=1, source_target_pairs={{0,992},{32,0},{64,32},{96,64},{128,96},{160,128},{192,160},{224,1... | collective-permute-start | bytes 368648 | tf_op jit(solution)/shard_map/ppermute | solution.py:65
  238.3 1.9 collective-permute-start.28
  242.2 1.9 copy.164
  246.3 5.6 %collective-permute-start.14 = (bf16[32,8,240]{0,2,1:T(8,128)(2,1)}, bf16[32,8,240]{0,2,1:T(8,128)(2,1)}, u32[]{:S(2)}, u32[]{:S(2)}) collective-permute-start(bf16[32,8,240]{0,2,1:T(8,128)(2,1)} %collective-permute-done.13), channel_id=1, source_target_pairs={{0,992},{32,0},{64,32},{96,64},{128,96},{160,128},{192,160},{224,1... | collective-permute-start | bytes 368648 | tf_op jit(solution)/shard_map/ppermute | solution.py:65
  253.1 1.9 collective-permute-start.29
  257.1 1.9 copy.163
  259.6 7.5 %collective-permute-done.29 = bf16[32,8,240]{0,2,1:T(8,128)(2,1)} collective-permute-done((bf16[32,8,240]{0,2,1:T(8,128)(2,1)}, bf16[32,8,240]{0,2,1:T(8,128)(2,1)}, u32[]{:S(2)}, u32[]{:S(2)}) %collective-permute-start.29) | collective-permute-done | bytes 122912 | tf_op jit(solution)/shard_map/ppermute | solution.py:62
  267.0 2.1 collective-permute-start.30
  271.2 1.9 copy.162
  273.7 5.6 %collective-permute-done.30 = bf16[32,8,240]{0,2,1:T(8,128)(2,1)} collective-permute-done((bf16[32,8,240]{0,2,1:T(8,128)(2,1)}, bf16[32,8,240]{0,2,1:T(8,128)(2,1)}, u32[]{:S(2)}, u32[]{:S(2)}) %collective-permute-start.30) | collective-permute-done | bytes 122912 | tf_op jit(solution)/shard_map/ppermute | solution.py:62
  279.3 1.9 copy.161
  296.1 4.0 %select_reduce_fusion = (s32[32,32,3]{1,2,0:T(4,128)S(1)}, s32[32,32,3]{1,2,0:T(4,128)S(1)}) fusion(s32[64]{0:T(128)} %and_select_fusion, s32[32,32,64]{2,1,0:T(8,128)S(1)} %bitcast.192, pred[32,32,64]{2,1,0:T(8,128)(4,1)S(1)} %fusion.4, s32[32,32,64]{2,1,0:T(8,128)S(1)} %fusion.5), kind=kLoop, calls=%fused_computation.7 | loop fusion | flops 1173504 | bytes 614656 | tf_op jit(solution)/shard_map/reduce_sum | solution.py:32
  300.6 1.6 constant_dynamic-update-slice_fusion.47
  302.2 1.6 constant_dynamic-update-slice_fusion.46
  317.5 12.8 %gather_fusion.1 = bf16[3072,240]{1,0:T(8,128)(2,1)S(1)} fusion(bf16[8192,240]{1,0:T(8,128)(2,1)} %bitcast.189, s32[3072]{0:T(1024)S(1)} %broadcast_clamp_fusion), kind=kCustom, calls=%fused_computation.1 | custom fusion | bytes 2961408 | tf_op jit(solution)/shard_map/jit(_take)/gather | solution.py:79
  331.6 1.7 copy.141
  335.3 2.8 broadcast_select_fusion
  338.1 10.7 %fusion.2 = bf16[1024,896]{0,1:T(8,128)(2,1)} fusion(bf16[3072,896]{0,1:T(8,128)(2,1)} %bitcast.191, bf16[3072,1024]{1,0:T(8,128)(2,1)} %all-gather.2.cloned.1.call-done, f32[3072]{0:T(1024)S(1)} %mul.31), kind=kOutput, calls=%fused_computation.6 | convolution fusion | flops 5647499264 | bytes 13643776 | tf_op jit(solution)/shard_map/dot_general | solution.py:83
  (160 shorter events, 93.2 us)
Async XLA Ops:
  9.9 23.4 %all-to-all-start = ((bf16[32,8,240]{2,1,0:T(8,128)(2,1)}), bf16[32,8,240]{2,1,0:T(8,128)(2,1)S(1)}, u32[]{:S(2)}, u32[]{:S(2)}) async-start(bf16[32,8,240]{2,1,0:T(8,128)(2,1)} %pad_maximum_fusion), calls=%async_computation | async-start | bytes 262144 | tf_op jit(solution)/shard_map/all_to_all | solution.py:52
  26.6 311.4 %all-gather.2.cloned.1.call-start = ((), (), s32[]{:S(2)}) async-start(), calls=%async_computation.1 | async-start | bytes 6488064 | tf_op jit(solution)/shard_map/all_gather | solution.py:45
  33.6 20.3 %collective-permute-start = (bf16[32,8,240]{0,2,1:T(8,128)(2,1)S(1)}, bf16[32,8,240]{0,2,1:T(8,128)(2,1)S(1)}, u32[]{:S(2)}, u32[]{:S(2)}) collective-permute-start(bf16[32,8,240]{0,2,1:T(8,128)(2,1)S(1)} %copy.130), channel_id=1, source_target_pairs={{0,992},{32,0},{64,32},{96,64},{128,96},{160,128},{192,160},{224,1... | collective-permute-start | bytes 368648 | tf_op jit(solution)/shard_map/ppermute | solution.py:65
  43.1 16.4 %collective-permute-start.15 = (bf16[32,8,240]{0,2,1:T(8,128)(2,1)S(1)}, bf16[32,8,240]{0,2,1:T(8,128)(2,1)S(1)}, u32[]{:S(2)}, u32[]{:S(2)}) collective-permute-start(bf16[32,8,240]{0,2,1:T(8,128)(2,1)S(1)} %copy.130), channel_id=1, source_target_pairs={{0,32},{32,64},{64,96},{96,128},{128,160},{160,192},{192,224},{224... | collective-permute-start | bytes 368648 | tf_op jit(solution)/shard_map/ppermute | solution.py:62
  53.9 15.5 %collective-permute-start.1 = (bf16[32,8,240]{0,2,1:T(8,128)(2,1)S(1)}, bf16[32,8,240]{0,2,1:T(8,128)(2,1)}, u32[]{:S(2)}, u32[]{:S(2)}) collective-permute-start(bf16[32,8,240]{0,2,1:T(8,128)(2,1)S(1)} %collective-permute-done), channel_id=1, source_target_pairs={{0,992},{32,0},{64,32},{96,64},{128,96},{160,128},{192,160},{224,1... | collective-permute-start | bytes 368648 | tf_op jit(solution)/shard_map/ppermute | solution.py:65
  59.5 15.6 %collective-permute-start.16 = (bf16[32,8,240]{0,2,1:T(8,128)(2,1)S(1)}, bf16[32,8,240]{0,2,1:T(8,128)(2,1)S(1)}, u32[]{:S(2)}, u32[]{:S(2)}) collective-permute-start(bf16[32,8,240]{0,2,1:T(8,128)(2,1)S(1)} %collective-permute-done.15), channel_id=1, source_target_pairs={{0,32},{32,64},{64,96},{96,128},{128,160},{160,192},{192,224},{224... | collective-permute-start | bytes 368648 | tf_op jit(solution)/shard_map/ppermute | solution.py:62
  69.5 15.0 %collective-permute-start.2 = (bf16[32,8,240]{0,2,1:T(8,128)(2,1)}, bf16[32,8,240]{0,2,1:T(8,128)(2,1)}, u32[]{:S(2)}, u32[]{:S(2)}) collective-permute-start(bf16[32,8,240]{0,2,1:T(8,128)(2,1)} %collective-permute-done.1), channel_id=1, source_target_pairs={{0,992},{32,0},{64,32},{96,64},{128,96},{160,128},{192,160},{224,1... | collective-permute-start | bytes 368648 | tf_op jit(solution)/shard_map/ppermute | solution.py:65
  75.2 14.9 %collective-permute-start.17 = (bf16[32,8,240]{0,2,1:T(8,128)(2,1)S(1)}, bf16[32,8,240]{0,2,1:T(8,128)(2,1)S(1)}, u32[]{:S(2)}, u32[]{:S(2)}) collective-permute-start(bf16[32,8,240]{0,2,1:T(8,128)(2,1)S(1)} %collective-permute-done.16), channel_id=1, source_target_pairs={{0,32},{32,64},{64,96},{96,128},{128,160},{160,192},{192,224},{224... | collective-permute-start | bytes 368648 | tf_op jit(solution)/shard_map/ppermute | solution.py:62
  84.5 14.0 %collective-permute-start.3 = (bf16[32,8,240]{0,2,1:T(8,128)(2,1)}, bf16[32,8,240]{0,2,1:T(8,128)(2,1)}, u32[]{:S(2)}, u32[]{:S(2)}) collective-permute-start(bf16[32,8,240]{0,2,1:T(8,128)(2,1)} %collective-permute-done.2), channel_id=1, source_target_pairs={{0,992},{32,0},{64,32},{96,64},{128,96},{160,128},{192,160},{224,1... | collective-permute-start | bytes 368648 | tf_op jit(solution)/shard_map/ppermute | solution.py:65
  90.1 14.0 %collective-permute-start.18 = (bf16[32,8,240]{0,2,1:T(8,128)(2,1)S(1)}, bf16[32,8,240]{0,2,1:T(8,128)(2,1)}, u32[]{:S(2)}, u32[]{:S(2)}) collective-permute-start(bf16[32,8,240]{0,2,1:T(8,128)(2,1)S(1)} %collective-permute-done.17), channel_id=1, source_target_pairs={{0,32},{32,64},{64,96},{96,128},{128,160},{160,192},{192,224},{224... | collective-permute-start | bytes 368648 | tf_op jit(solution)/shard_map/ppermute | solution.py:62
  98.5 13.1 %collective-permute-start.4 = (bf16[32,8,240]{0,2,1:T(8,128)(2,1)}, bf16[32,8,240]{0,2,1:T(8,128)(2,1)}, u32[]{:S(2)}, u32[]{:S(2)}) collective-permute-start(bf16[32,8,240]{0,2,1:T(8,128)(2,1)} %collective-permute-done.3), channel_id=1, source_target_pairs={{0,992},{32,0},{64,32},{96,64},{128,96},{160,128},{192,160},{224,1... | collective-permute-start | bytes 368648 | tf_op jit(solution)/shard_map/ppermute | solution.py:65
  104.1 13.1 %collective-permute-start.19 = (bf16[32,8,240]{0,2,1:T(8,128)(2,1)}, bf16[32,8,240]{0,2,1:T(8,128)(2,1)}, u32[]{:S(2)}, u32[]{:S(2)}) collective-permute-start(bf16[32,8,240]{0,2,1:T(8,128)(2,1)} %collective-permute-done.18), channel_id=1, source_target_pairs={{0,32},{32,64},{64,96},{96,128},{128,160},{160,192},{192,224},{224... | collective-permute-start | bytes 368648 | tf_op jit(solution)/shard_map/ppermute | solution.py:62
  111.6 12.2 %collective-permute-start.5 = (bf16[32,8,240]{0,2,1:T(8,128)(2,1)}, bf16[32,8,240]{0,2,1:T(8,128)(2,1)}, u32[]{:S(2)}, u32[]{:S(2)}) collective-permute-start(bf16[32,8,240]{0,2,1:T(8,128)(2,1)} %collective-permute-done.4), channel_id=1, source_target_pairs={{0,992},{32,0},{64,32},{96,64},{128,96},{160,128},{192,160},{224,1... | collective-permute-start | bytes 368648 | tf_op jit(solution)/shard_map/ppermute | solution.py:65
  117.2 12.3 %collective-permute-start.20 = (bf16[32,8,240]{0,2,1:T(8,128)(2,1)}, bf16[32,8,240]{0,2,1:T(8,128)(2,1)}, u32[]{:S(2)}, u32[]{:S(2)}) collective-permute-start(bf16[32,8,240]{0,2,1:T(8,128)(2,1)} %collective-permute-done.19), channel_id=1, source_target_pairs={{0,32},{32,64},{64,96},{96,128},{128,160},{160,192},{192,224},{224... | collective-permute-start | bytes 368648 | tf_op jit(solution)/shard_map/ppermute | solution.py:62
  123.9 12.8 %collective-permute-start.6 = (bf16[32,8,240]{0,2,1:T(8,128)(2,1)}, bf16[32,8,240]{0,2,1:T(8,128)(2,1)}, u32[]{:S(2)}, u32[]{:S(2)}) collective-permute-start(bf16[32,8,240]{0,2,1:T(8,128)(2,1)} %collective-permute-done.5), channel_id=1, source_target_pairs={{0,992},{32,0},{64,32},{96,64},{128,96},{160,128},{192,160},{224,1... | collective-permute-start | bytes 368648 | tf_op jit(solution)/shard_map/ppermute | solution.py:65
  129.5 13.1 %collective-permute-start.21 = (bf16[32,8,240]{0,2,1:T(8,128)(2,1)}, bf16[32,8,240]{0,2,1:T(8,128)(2,1)}, u32[]{:S(2)}, u32[]{:S(2)}) collective-permute-start(bf16[32,8,240]{0,2,1:T(8,128)(2,1)} %collective-permute-done.20), channel_id=1, source_target_pairs={{0,32},{32,64},{64,96},{96,128},{128,160},{160,192},{192,224},{224... | collective-permute-start | bytes 368648 | tf_op jit(solution)/shard_map/ppermute | solution.py:62
  136.7 13.9 %collective-permute-start.7 = (bf16[32,8,240]{0,2,1:T(8,128)(2,1)}, bf16[32,8,240]{0,2,1:T(8,128)(2,1)}, u32[]{:S(2)}, u32[]{:S(2)}) collective-permute-start(bf16[32,8,240]{0,2,1:T(8,128)(2,1)} %collective-permute-done.6), channel_id=1, source_target_pairs={{0,992},{32,0},{64,32},{96,64},{128,96},{160,128},{192,160},{224,1... | collective-permute-start | bytes 368648 | tf_op jit(solution)/shard_map/ppermute | solution.py:65
  142.6 14.2 %collective-permute-start.22 = (bf16[32,8,240]{0,2,1:T(8,128)(2,1)}, bf16[32,8,240]{0,2,1:T(8,128)(2,1)}, u32[]{:S(2)}, u32[]{:S(2)}) collective-permute-start(bf16[32,8,240]{0,2,1:T(8,128)(2,1)} %collective-permute-done.21), channel_id=1, source_target_pairs={{0,32},{32,64},{64,96},{96,128},{128,160},{160,192},{192,224},{224... | collective-permute-start | bytes 368648 | tf_op jit(solution)/shard_map/ppermute | solution.py:62
  150.6 15.0 %collective-permute-start.8 = (bf16[32,8,240]{0,2,1:T(8,128)(2,1)}, bf16[32,8,240]{0,2,1:T(8,128)(2,1)}, u32[]{:S(2)}, u32[]{:S(2)}) collective-permute-start(bf16[32,8,240]{0,2,1:T(8,128)(2,1)} %collective-permute-done.7), channel_id=1, source_target_pairs={{0,992},{32,0},{64,32},{96,64},{128,96},{160,128},{192,160},{224,1... | collective-permute-start | bytes 368648 | tf_op jit(solution)/shard_map/ppermute | solution.py:65
  156.8 15.3 %collective-permute-start.23 = (bf16[32,8,240]{0,2,1:T(8,128)(2,1)}, bf16[32,8,240]{0,2,1:T(8,128)(2,1)}, u32[]{:S(2)}, u32[]{:S(2)}) collective-permute-start(bf16[32,8,240]{0,2,1:T(8,128)(2,1)} %collective-permute-done.22), channel_id=1, source_target_pairs={{0,32},{32,64},{64,96},{96,128},{128,160},{160,192},{192,224},{224... | collective-permute-start | bytes 368648 | tf_op jit(solution)/shard_map/ppermute | solution.py:62
  165.6 16.1 %collective-permute-start.9 = (bf16[32,8,240]{0,2,1:T(8,128)(2,1)}, bf16[32,8,240]{0,2,1:T(8,128)(2,1)}, u32[]{:S(2)}, u32[]{:S(2)}) collective-permute-start(bf16[32,8,240]{0,2,1:T(8,128)(2,1)} %collective-permute-done.8), channel_id=1, source_target_pairs={{0,992},{32,0},{64,32},{96,64},{128,96},{160,128},{192,160},{224,1... | collective-permute-start | bytes 368648 | tf_op jit(solution)/shard_map/ppermute | solution.py:65
  172.1 16.4 %collective-permute-start.24 = (bf16[32,8,240]{0,2,1:T(8,128)(2,1)}, bf16[32,8,240]{0,2,1:T(8,128)(2,1)}, u32[]{:S(2)}, u32[]{:S(2)}) collective-permute-start(bf16[32,8,240]{0,2,1:T(8,128)(2,1)} %collective-permute-done.23), channel_id=1, source_target_pairs={{0,32},{32,64},{64,96},{96,128},{128,160},{160,192},{192,224},{224... | collective-permute-start | bytes 368648 | tf_op jit(solution)/shard_map/ppermute | solution.py:62
  181.7 17.2 %collective-permute-start.10 = (bf16[32,8,240]{0,2,1:T(8,128)(2,1)}, bf16[32,8,240]{0,2,1:T(8,128)(2,1)}, u32[]{:S(2)}, u32[]{:S(2)}) collective-permute-start(bf16[32,8,240]{0,2,1:T(8,128)(2,1)} %collective-permute-done.9), channel_id=1, source_target_pairs={{0,992},{32,0},{64,32},{96,64},{128,96},{160,128},{192,160},{224,1... | collective-permute-start | bytes 368648 | tf_op jit(solution)/shard_map/ppermute | solution.py:65
  188.5 17.5 %collective-permute-start.25 = (bf16[32,8,240]{0,2,1:T(8,128)(2,1)}, bf16[32,8,240]{0,2,1:T(8,128)(2,1)}, u32[]{:S(2)}, u32[]{:S(2)}) collective-permute-start(bf16[32,8,240]{0,2,1:T(8,128)(2,1)} %collective-permute-done.24), channel_id=1, source_target_pairs={{0,32},{32,64},{64,96},{96,128},{128,160},{160,192},{192,224},{224... | collective-permute-start | bytes 368648 | tf_op jit(solution)/shard_map/ppermute | solution.py:62
  198.9 16.7 %collective-permute-start.11 = (bf16[32,8,240]{0,2,1:T(8,128)(2,1)}, bf16[32,8,240]{0,2,1:T(8,128)(2,1)}, u32[]{:S(2)}, u32[]{:S(2)}) collective-permute-start(bf16[32,8,240]{0,2,1:T(8,128)(2,1)} %collective-permute-done.10), channel_id=1, source_target_pairs={{0,992},{32,0},{64,32},{96,64},{128,96},{160,128},{192,160},{224,1... | collective-permute-start | bytes 368648 | tf_op jit(solution)/shard_map/ppermute | solution.py:65
  205.9 16.6 %collective-permute-start.26 = (bf16[32,8,240]{0,2,1:T(8,128)(2,1)}, bf16[32,8,240]{0,2,1:T(8,128)(2,1)}, u32[]{:S(2)}, u32[]{:S(2)}) collective-permute-start(bf16[32,8,240]{0,2,1:T(8,128)(2,1)} %collective-permute-done.25), channel_id=1, source_target_pairs={{0,32},{32,64},{64,96},{96,128},{128,160},{160,192},{192,224},{224... | collective-permute-start | bytes 368648 | tf_op jit(solution)/shard_map/ppermute | solution.py:62
  215.6 15.8 %collective-permute-start.12 = (bf16[32,8,240]{0,2,1:T(8,128)(2,1)}, bf16[32,8,240]{0,2,1:T(8,128)(2,1)}, u32[]{:S(2)}, u32[]{:S(2)}) collective-permute-start(bf16[32,8,240]{0,2,1:T(8,128)(2,1)} %collective-permute-done.11), channel_id=1, source_target_pairs={{0,992},{32,0},{64,32},{96,64},{128,96},{160,128},{192,160},{224,1... | collective-permute-start | bytes 368648 | tf_op jit(solution)/shard_map/ppermute | solution.py:65
  222.5 15.8 %collective-permute-start.27 = (bf16[32,8,240]{0,2,1:T(8,128)(2,1)}, bf16[32,8,240]{0,2,1:T(8,128)(2,1)}, u32[]{:S(2)}, u32[]{:S(2)}) collective-permute-start(bf16[32,8,240]{0,2,1:T(8,128)(2,1)} %collective-permute-done.26), channel_id=1, source_target_pairs={{0,32},{32,64},{64,96},{96,128},{128,160},{160,192},{192,224},{224... | collective-permute-start | bytes 368648 | tf_op jit(solution)/shard_map/ppermute | solution.py:62
  231.4 14.9 %collective-permute-start.13 = (bf16[32,8,240]{0,2,1:T(8,128)(2,1)}, bf16[32,8,240]{0,2,1:T(8,128)(2,1)}, u32[]{:S(2)}, u32[]{:S(2)}) collective-permute-start(bf16[32,8,240]{0,2,1:T(8,128)(2,1)} %collective-permute-done.12), channel_id=1, source_target_pairs={{0,992},{32,0},{64,32},{96,64},{128,96},{160,128},{192,160},{224,1... | collective-permute-start | bytes 368648 | tf_op jit(solution)/shard_map/ppermute | solution.py:65
  238.3 14.8 %collective-permute-start.28 = (bf16[32,8,240]{0,2,1:T(8,128)(2,1)}, bf16[32,8,240]{0,2,1:T(8,128)(2,1)}, u32[]{:S(2)}, u32[]{:S(2)}) collective-permute-start(bf16[32,8,240]{0,2,1:T(8,128)(2,1)} %collective-permute-done.27), channel_id=1, source_target_pairs={{0,32},{32,64},{64,96},{96,128},{128,160},{160,192},{192,224},{224... | collective-permute-start | bytes 368648 | tf_op jit(solution)/shard_map/ppermute | solution.py:62
  246.3 22.9 %collective-permute-start.14 = (bf16[32,8,240]{0,2,1:T(8,128)(2,1)}, bf16[32,8,240]{0,2,1:T(8,128)(2,1)}, u32[]{:S(2)}, u32[]{:S(2)}) collective-permute-start(bf16[32,8,240]{0,2,1:T(8,128)(2,1)} %collective-permute-done.13), channel_id=1, source_target_pairs={{0,992},{32,0},{64,32},{96,64},{128,96},{160,128},{192,160},{224,1... | collective-permute-start | bytes 368648 | tf_op jit(solution)/shard_map/ppermute | solution.py:65
  253.1 13.9 %collective-permute-start.29 = (bf16[32,8,240]{0,2,1:T(8,128)(2,1)}, bf16[32,8,240]{0,2,1:T(8,128)(2,1)}, u32[]{:S(2)}, u32[]{:S(2)}) collective-permute-start(bf16[32,8,240]{0,2,1:T(8,128)(2,1)} %collective-permute-done.28), channel_id=1, source_target_pairs={{0,32},{32,64},{64,96},{96,128},{128,160},{160,192},{192,224},{224... | collective-permute-start | bytes 368648 | tf_op jit(solution)/shard_map/ppermute | solution.py:62
  267.0 12.2 %collective-permute-start.30 = (bf16[32,8,240]{0,2,1:T(8,128)(2,1)}, bf16[32,8,240]{0,2,1:T(8,128)(2,1)}, u32[]{:S(2)}, u32[]{:S(2)}) collective-permute-start(bf16[32,8,240]{0,2,1:T(8,128)(2,1)} %collective-permute-done.29), channel_id=1, source_target_pairs={{0,32},{32,64},{64,96},{96,128},{128,160},{160,192},{192,224},{224... | collective-permute-start | bytes 368648 | tf_op jit(solution)/shard_map/ppermute | solution.py:62
  294.7 16.9 %copy-start.9 = (bf16[1,32,8,240]{3,2,1,0:T(8,128)(2,1)S(1)}, bf16[1,32,8,240]{3,2,1,0:T(8,128)(2,1)}, u32[]{:S(2)}) copy-start(bf16[1,32,8,240]{3,2,1,0:T(8,128)(2,1)} %copy.168) | copy-start | bytes 368644
  294.7 17.5 %copy-start.8 = (bf16[1,32,8,240]{3,2,1,0:T(8,128)(2,1)S(1)}, bf16[1,32,8,240]{3,2,1,0:T(8,128)(2,1)}, u32[]{:S(2)}) copy-start(bf16[1,32,8,240]{3,2,1,0:T(8,128)(2,1)} %copy.169) | copy-start | bytes 368644
  294.9 18.0 %copy-start.7 = (bf16[1,32,8,240]{3,2,1,0:T(8,128)(2,1)S(1)}, bf16[1,32,8,240]{3,2,1,0:T(8,128)(2,1)}, u32[]{:S(2)}) copy-start(bf16[1,32,8,240]{3,2,1,0:T(8,128)(2,1)} %copy.170) | copy-start | bytes 368644
  294.9 18.6 %copy-start.6 = (bf16[1,32,8,240]{3,2,1,0:T(8,128)(2,1)S(1)}, bf16[1,32,8,240]{3,2,1,0:T(8,128)(2,1)}, u32[]{:S(2)}) copy-start(bf16[1,32,8,240]{3,2,1,0:T(8,128)(2,1)} %copy.171) | copy-start | bytes 368644
  294.9 19.3 %copy-start.5 = (bf16[1,32,8,240]{3,2,1,0:T(8,128)(2,1)S(1)}, bf16[1,32,8,240]{3,2,1,0:T(8,128)(2,1)}, u32[]{:S(2)}) copy-start(bf16[1,32,8,240]{3,2,1,0:T(8,128)(2,1)} %copy.172) | copy-start | bytes 368644
  295.0 19.9 %copy-start.4 = (bf16[1,32,8,240]{3,2,1,0:T(8,128)(2,1)S(1)}, bf16[1,32,8,240]{3,2,1,0:T(8,128)(2,1)}, u32[]{:S(2)}) copy-start(bf16[1,32,8,240]{3,2,1,0:T(8,128)(2,1)} %copy.173) | copy-start | bytes 368644
  295.4 20.1 %copy-start.3 = (bf16[1,32,8,240]{3,2,1,0:T(8,128)(2,1)S(1)}, bf16[1,32,8,240]{3,2,1,0:T(8,128)(2,1)}, u32[]{:S(2)}) copy-start(bf16[1,32,8,240]{3,2,1,0:T(8,128)(2,1)} %copy.174) | copy-start | bytes 368644
  295.5 20.7 %copy-start.2 = (bf16[1,32,8,240]{3,2,1,0:T(8,128)(2,1)S(1)}, bf16[1,32,8,240]{3,2,1,0:T(8,128)(2,1)}, u32[]{:S(2)}) copy-start(bf16[1,32,8,240]{3,2,1,0:T(8,128)(2,1)} %copy.175) | copy-start | bytes 368644
  295.5 21.4 %copy-start.1 = (bf16[1,32,8,240]{3,2,1,0:T(8,128)(2,1)S(1)}, bf16[1,32,8,240]{3,2,1,0:T(8,128)(2,1)}, u32[]{:S(2)}) copy-start(bf16[1,32,8,240]{3,2,1,0:T(8,128)(2,1)} %copy.176) | copy-start | bytes 368644
  295.8 21.7 %copy-start = (pred[32,32,64]{2,1,0:T(8,128)(4,1)}, pred[32,32,64]{2,1,0:T(8,128)(4,1)S(1)}, u32[]{:S(2)}) copy-start(pred[32,32,64]{2,1,0:T(8,128)(4,1)S(1)} %fusion.4) | copy-start | bytes 196612
Sparse Core Ops, SparseCore 0:
  31.8 82.4 all-gather.1

commit v8 on v5

--- a/solution.py
+++ b/solution.py
@@ -74,7 +74,13 @@
 
     hidden_t = jnp.transpose(hidden)
     rows_t = (weight[None, :] * hidden_t.astype(jnp.float32)).astype(jnp.bfloat16)
-    grad_rows = jnp.take(tokens, token, axis=0, mode="clip")[:, :width]
+    back = (jnp.arange(n_exp, dtype=jnp.int32) - me_exp) % n_exp
+    ring_src = jnp.take(ring[..., :width], back, axis=0)
+    pick_t = (token % TOK_DEV).reshape(n_grp, n_exp, capacity)
+    onehot = (pick_t[..., None] == jnp.arange(TOK_DEV, dtype=jnp.int32)).astype(jnp.bfloat16)
+    grad_rows = jnp.einsum(
+        "gsrt,sgtc->gsrc", onehot, ring_src, preferred_element_type=jnp.float32
+    ).astype(jnp.bfloat16).reshape(-1, width)
     mask = label[:, None] == jnp.arange(EXP_DEV, dtype=jnp.int32)[None, :]
     spread = jnp.where(mask[:, :, None], grad_rows[:, None, :], jnp.zeros_like(grad_rows)[:, None, :])
     spread = spread.reshape(grad_rows.shape[0], EXP_DEV * width)

time: 232 us -> 229 us (0.987)
  matrix products: 11.1 us -> 16.4 us
  local copies, waits for them, and re-layouts: 28.9 us -> 23.6 us
  waiting for transfers between devices: 31.4 us -> 28.5 us
    gather x1, local copies, waits for them, and re-layouts: 12.5 us -> 5.07 us  [per_device(): ring_src = jnp.take(ring[..., :width], back, axis=0)]
    dot_general x0 -> x1, matrix products: none -> 5.37 us  [per_device(): jnp.einsum('gsrt,sgtc->gsrc', onehot, ring_src, preferred_element_type=jn...]
    broadcast_in_dim x0 -> x2, local copies, waits for them, and re-layouts: none -> 4.6 us  [per_device(): jnp.where(mask[:, :, None], grad_rows[:, None, :], jnp.zeros_like(grad_ro...]
    ppermute x16, waiting for transfers between devices: 17.1 us -> 13.8 us  [per_device(): fwd = lax.ppermute(fwd, 'expert', fwd_perm)]
    ppermute x15, waiting for transfers between devices: 7.61 us -> 10.1 us  [per_device(): bwd = lax.ppermute(bwd, 'expert', bwd_perm)]
  transfers between devices with their start and end apart: 33 -> 33, of which waited for: 25 -> 20; matrix products, arithmetic and copies ran while one was open for 16% -> 15% of each run, Pallas kernels for 0% -> 0%
where the time goes in v8:
time: 229 us; the launch traced here: 227 us
  starting transfers between devices  135 us (59%)
  waiting for transfers between devices  28.5 us (12%)
  local copies, waits for them, and re-layouts  23.6 us (10%)
  matrix products  16.4 us (7%)
  between operations  14.1 us (6%)
  other arithmetic  10.1 us (4%)
    ppermute x15, starting transfers between devices, per_device(): bwd = lax.ppermute(bwd, 'expert', bwd_perm)  87.4 us
    ppermute x16, starting transfers between devices, per_device(): fwd = lax.ppermute(fwd, 'expert', fwd_perm)  30.6 us
    all_to_all x1, starting transfers between devices, per_device(): cols = lax.all_to_all(cols, 'dp', 0, 0, tiled=True)  16.7 us
    ppermute x16, waiting for transfers between devices, per_device(): fwd = lax.ppermute(fwd, 'expert', fwd_perm)  13.8 us
    dot_general x1, matrix products, per_device(): gradient = jnp.dot(rows_t, spread, preferred_element_type=jnp.float32)  10.7 us
    ppermute x15, waiting for transfers between devices, per_device(): bwd = lax.ppermute(bwd, 'expert', bwd_perm)  10.1 us
    dot_general x1, matrix products, per_device(): jnp.einsum('gsrt,sgtc->gsrc', onehot, ring_src, preferred_element_type=jn...  5.37 us
    gather x1, local copies, waits for them, and re-layouts, per_device(): ring_src = jnp.take(ring[..., :width], back, axis=0)  5.07 us
  transfers between devices with their start and end apart: 33, of which 20 were waited for; matrix products, arithmetic and copies ran while one was open for 15% of the time, Pallas kernels for 0%

profile of v8, /device:TPU:2, one launch (start us, length us, event | category | flops | bytes accessed | tf_op | source)
XLA Modules:
  0.0 227.5 jit_solution(9448434018259106780)
XLA Ops:
  6.5 1.1 reshape.229
  7.7 0.7 convert_element_type.27
  8.4 0.8 pad_maximum_fusion.1
  9.2 0.8 pad_maximum_fusion
  9.9 16.7 %all-to-all-start = ((bf16[32,8,240]{2,1,0:T(8,128)(2,1)}), bf16[32,8,240]{2,1,0:T(8,128)(2,1)S(1)}, u32[]{:S(2)}, u32[]{:S(2)}) async-start(bf16[32,8,240]{2,1,0:T(8,128)(2,1)} %pad_maximum_fusion), calls=%async_computation | async-start | bytes 262144 | tf_op jit(solution)/shard_map/all_to_all | solution.py:52
  26.7 1.1 copy.84
  27.8 0.8 reshape.232
  28.7 4.6 %all-to-all-done = bf16[32,8,240]{2,1,0:T(8,128)(2,1)S(1)} async-done(((bf16[32,8,240]{2,1,0:T(8,128)(2,1)}), bf16[32,8,240]{2,1,0:T(8,128)(2,1)S(1)}, u32[]{:S(2)}, u32[]{:S(2)}) %all-to-all-start) | async-done | bytes 122912 | tf_op jit(solution)/shard_map/all_to_all | solution.py:52
  33.4 9.5 %collective-permute-start = (bf16[32,8,240]{2,1,0:T(8,128)(2,1)S(1)}, bf16[32,8,240]{2,1,0:T(8,128)(2,1)S(1)}, u32[]{:S(2)}, u32[]{:S(2)}) collective-permute-start(bf16[32,8,240]{2,1,0:T(8,128)(2,1)S(1)} %all-to-all-done), channel_id=1, source_target_pairs={{0,992},{32,0},{64,32},{96,64},{128,96},{160,128},{192,160},{224,1... | collective-permute-start | bytes 368648 | tf_op jit(solution)/shard_map/ppermute | solution.py:65
  42.9 1.9 collective-permute-start.15
  44.8 1.1 collective-permute-done
  45.9 5.6 %collective-permute-start.1 = (bf16[32,8,240]{2,1,0:T(8,128)(2,1)S(1)}, bf16[32,8,240]{2,1,0:T(8,128)(2,1)S(1)}, u32[]{:S(2)}, u32[]{:S(2)}) collective-permute-start(bf16[32,8,240]{2,1,0:T(8,128)(2,1)S(1)} %collective-permute-done), channel_id=1, source_target_pairs={{0,992},{32,0},{64,32},{96,64},{128,96},{160,128},{192,160},{224,1... | collective-permute-start | bytes 368648 | tf_op jit(solution)/shard_map/ppermute | solution.py:65
  51.5 1.9 collective-permute-start.16
  53.5 0.5 collective-permute-done.1
  54.0 5.6 %collective-permute-start.2 = (bf16[32,8,240]{2,1,0:T(8,128)(2,1)S(1)}, bf16[32,8,240]{2,1,0:T(8,128)(2,1)S(1)}, u32[]{:S(2)}, u32[]{:S(2)}) collective-permute-start(bf16[32,8,240]{2,1,0:T(8,128)(2,1)S(1)} %collective-permute-done.1), channel_id=1, source_target_pairs={{0,992},{32,0},{64,32},{96,64},{128,96},{160,128},{192,160},{224,1... | collective-permute-start | bytes 368648 | tf_op jit(solution)/shard_map/ppermute | solution.py:65
  59.6 1.9 collective-permute-start.17
  61.5 0.5 collective-permute-done.2
  62.1 5.6 %collective-permute-start.3 = (bf16[32,8,240]{2,1,0:T(8,128)(2,1)S(1)}, bf16[32,8,240]{2,1,0:T(8,128)(2,1)S(1)}, u32[]{:S(2)}, u32[]{:S(2)}) collective-permute-start(bf16[32,8,240]{2,1,0:T(8,128)(2,1)S(1)} %collective-permute-done.2), channel_id=1, source_target_pairs={{0,992},{32,0},{64,32},{96,64},{128,96},{160,128},{192,160},{224,1... | collective-permute-start | bytes 368648 | tf_op jit(solution)/shard_map/ppermute | solution.py:65
  67.7 1.9 collective-permute-start.18
  69.6 0.5 collective-permute-done.3
  70.1 5.6 %collective-permute-start.4 = (bf16[32,8,240]{2,1,0:T(8,128)(2,1)S(1)}, bf16[32,8,240]{2,1,0:T(8,128)(2,1)S(1)}, u32[]{:S(2)}, u32[]{:S(2)}) collective-permute-start(bf16[32,8,240]{2,1,0:T(8,128)(2,1)S(1)} %collective-permute-done.3), channel_id=1, source_target_pairs={{0,992},{32,0},{64,32},{96,64},{128,96},{160,128},{192,160},{224,1... | collective-permute-start | bytes 368648 | tf_op jit(solution)/shard_map/ppermute | solution.py:65
  75.7 1.9 collective-permute-start.19
  78.2 5.6 %collective-permute-start.5 = (bf16[32,8,240]{2,1,0:T(8,128)(2,1)S(1)}, bf16[32,8,240]{2,1,0:T(8,128)(2,1)S(1)}, u32[]{:S(2)}, u32[]{:S(2)}) collective-permute-start(bf16[32,8,240]{2,1,0:T(8,128)(2,1)S(1)} %collective-permute-done.4), channel_id=1, source_target_pairs={{0,992},{32,0},{64,32},{96,64},{128,96},{160,128},{192,160},{224,1... | collective-permute-start | bytes 368648 | tf_op jit(solution)/shard_map/ppermute | solution.py:65
  83.8 1.9 collective-permute-start.20
  85.7 1.3 collective-permute-done.5
  87.0 5.6 %collective-permute-start.6 = (bf16[32,8,240]{2,1,0:T(8,128)(2,1)S(1)}, bf16[32,8,240]{2,1,0:T(8,128)(2,1)S(1)}, u32[]{:S(2)}, u32[]{:S(2)}) collective-permute-start(bf16[32,8,240]{2,1,0:T(8,128)(2,1)S(1)} %collective-permute-done.5), channel_id=1, source_target_pairs={{0,992},{32,0},{64,32},{96,64},{128,96},{160,128},{192,160},{224,1... | collective-permute-start | bytes 368648 | tf_op jit(solution)/shard_map/ppermute | solution.py:65
  92.9 1.9 collective-permute-start.21
  94.9 1.1 collective-permute-done.6
  95.9 5.6 %collective-permute-start.7 = (bf16[32,8,240]{2,1,0:T(8,128)(2,1)S(1)}, bf16[32,8,240]{2,1,0:T(8,128)(2,1)S(1)}, u32[]{:S(2)}, u32[]{:S(2)}) collective-permute-start(bf16[32,8,240]{2,1,0:T(8,128)(2,1)S(1)} %collective-permute-done.6), channel_id=1, source_target_pairs={{0,992},{32,0},{64,32},{96,64},{128,96},{160,128},{192,160},{224,1... | collective-permute-start | bytes 368648 | tf_op jit(solution)/shard_map/ppermute | solution.py:65
  101.6 1.9 collective-permute-start.22
  103.5 0.6 collective-permute-done.7
  104.1 5.6 %collective-permute-start.8 = (bf16[32,8,240]{2,1,0:T(8,128)(2,1)S(1)}, bf16[32,8,240]{2,1,0:T(8,128)(2,1)S(1)}, u32[]{:S(2)}, u32[]{:S(2)}) collective-permute-start(bf16[32,8,240]{2,1,0:T(8,128)(2,1)S(1)} %collective-permute-done.7), channel_id=1, source_target_pairs={{0,992},{32,0},{64,32},{96,64},{128,96},{160,128},{192,160},{224,1... | collective-permute-start | bytes 368648 | tf_op jit(solution)/shard_map/ppermute | solution.py:65
  109.7 1.9 collective-permute-start.23
  112.2 5.6 %collective-permute-start.9 = (bf16[32,8,240]{2,1,0:T(8,128)(2,1)S(1)}, bf16[32,8,240]{2,1,0:T(8,128)(2,1)S(1)}, u32[]{:S(2)}, u32[]{:S(2)}) collective-permute-start(bf16[32,8,240]{2,1,0:T(8,128)(2,1)S(1)} %collective-permute-done.8), channel_id=1, source_target_pairs={{0,992},{32,0},{64,32},{96,64},{128,96},{160,128},{192,160},{224,1... | collective-permute-start | bytes 368648 | tf_op jit(solution)/shard_map/ppermute | solution.py:65
  117.8 1.9 collective-permute-start.24
  120.2 5.6 %collective-permute-start.10 = (bf16[32,8,240]{2,1,0:T(8,128)(2,1)S(1)}, bf16[32,8,240]{2,1,0:T(8,128)(2,1)S(1)}, u32[]{:S(2)}, u32[]{:S(2)}) collective-permute-start(bf16[32,8,240]{2,1,0:T(8,128)(2,1)S(1)} %collective-permute-done.9), channel_id=1, source_target_pairs={{0,992},{32,0},{64,32},{96,64},{128,96},{160,128},{192,160},{224,1... | collective-permute-start | bytes 368648 | tf_op jit(solution)/shard_map/ppermute | solution.py:65
  125.8 1.9 collective-permute-start.25
  128.3 5.6 %collective-permute-start.11 = (bf16[32,8,240]{2,1,0:T(8,128)(2,1)S(1)}, bf16[32,8,240]{2,1,0:T(8,128)(2,1)S(1)}, u32[]{:S(2)}, u32[]{:S(2)}) collective-permute-start(bf16[32,8,240]{2,1,0:T(8,128)(2,1)S(1)} %collective-permute-done.10), channel_id=1, source_target_pairs={{0,992},{32,0},{64,32},{96,64},{128,96},{160,128},{192,160},{224,1... | collective-permute-start | bytes 368648 | tf_op jit(solution)/shard_map/ppermute | solution.py:65
  133.9 1.9 collective-permute-start.26
  136.4 5.6 %collective-permute-start.12 = (bf16[32,8,240]{2,1,0:T(8,128)(2,1)S(1)}, bf16[32,8,240]{2,1,0:T(8,128)(2,1)S(1)}, u32[]{:S(2)}, u32[]{:S(2)}) collective-permute-start(bf16[32,8,240]{2,1,0:T(8,128)(2,1)S(1)} %collective-permute-done.11), channel_id=1, source_target_pairs={{0,992},{32,0},{64,32},{96,64},{128,96},{160,128},{192,160},{224,1... | collective-permute-start | bytes 368648 | tf_op jit(solution)/shard_map/ppermute | solution.py:65
  141.9 1.9 collective-permute-start.27
  143.9 1.4 collective-permute-done.12
  145.3 5.6 %collective-permute-start.13 = (bf16[32,8,240]{2,1,0:T(8,128)(2,1)S(1)}, bf16[32,8,240]{2,1,0:T(8,128)(2,1)S(1)}, u32[]{:S(2)}, u32[]{:S(2)}) collective-permute-start(bf16[32,8,240]{2,1,0:T(8,128)(2,1)S(1)} %collective-permute-done.12), channel_id=1, source_target_pairs={{0,992},{32,0},{64,32},{96,64},{128,96},{160,128},{192,160},{224,1... | collective-permute-start | bytes 368648 | tf_op jit(solution)/shard_map/ppermute | solution.py:65
  151.1 1.9 collective-permute-start.28
  153.3 5.6 %collective-permute-start.14 = (bf16[32,8,240]{2,1,0:T(8,128)(2,1)S(1)}, bf16[32,8,240]{2,1,0:T(8,128)(2,1)S(1)}, u32[]{:S(2)}, u32[]{:S(2)}) collective-permute-start(bf16[32,8,240]{2,1,0:T(8,128)(2,1)S(1)} %collective-permute-done.13), channel_id=1, source_target_pairs={{0,992},{32,0},{64,32},{96,64},{128,96},{160,128},{192,160},{224,1... | collective-permute-start | bytes 368648 | tf_op jit(solution)/shard_map/ppermute | solution.py:65
  158.9 0.8 collective-permute-done.28
  159.7 1.9 collective-permute-start.29
  161.7 6.1 %collective-permute-done.29 = bf16[32,8,240]{2,1,0:T(8,128)(2,1)S(1)} collective-permute-done((bf16[32,8,240]{2,1,0:T(8,128)(2,1)S(1)}, bf16[32,8,240]{2,1,0:T(8,128)(2,1)S(1)}, u32[]{:S(2)}, u32[]{:S(2)}) %collective-permute-start.29) | collective-permute-done | bytes 122912 | tf_op jit(solution)/shard_map/ppermute | solution.py:62
  167.8 1.9 collective-permute-start.30
  169.7 6.1 %collective-permute-done.30 = bf16[32,8,240]{2,1,0:T(8,128)(2,1)S(1)} collective-permute-done((bf16[32,8,240]{2,1,0:T(8,128)(2,1)S(1)}, bf16[32,8,240]{2,1,0:T(8,128)(2,1)S(1)}, u32[]{:S(2)}, u32[]{:S(2)}) %collective-permute-start.30) | collective-permute-done | bytes 122912 | tf_op jit(solution)/shard_map/ppermute | solution.py:62
  176.2 2.0 copy-done
  178.2 0.7 slice.20
  178.9 1.4 copy.90
  180.3 0.7 gather_fusion
  181.1 2.2 copy.75
  183.6 0.6 copy.80
  186.3 0.6 select_reduce_fusion.2
  187.7 3.4 %select_reduce_fusion = (s32[32,32,3]{1,2,0:T(4,128)S(1)}, s32[32,32,3]{1,2,0:T(4,128)S(1)}) fusion(s32[64]{0:T(128)S(1)} %and_select_fusion, s32[32,32,64]{2,1,0:T(8,128)S(1)} %bitcast.90, pred[32,32,64]{2,1,0:T(8,128)(4,1)S(1)} %fusion.10, s32[32,32,64]{2,1,0:T(8,128)S(1)} %fusion.11), kind=kLoop, calls=%fused_computation.12 | loop fusion | flops 1173504 | bytes 614656 | tf_op jit(solution)/shard_map/reduce_sum | solution.py:32
  191.4 5.1 %gather_fusion.1 = bf16[32,32,8,224]{3,2,1,0:T(8,128)(2,1)} fusion(bf16[32,32,8,224]{3,2,1,0:T(8,128)(2,1)} %bitcast.87, s32[1024]{0:T(1024)S(1)} %pad_clamp_fusion), kind=kCustom, calls=%fused_computation.1 | custom fusion | bytes 7340160 | tf_op jit(solution)/shard_map/jit(_take)/gather | solution.py:78
  196.5 5.4 %fusion.4 = bf16[32,32,3,224]{3,2,1,0:T(4,128)(2,1)} fusion(s32[32,32,3]{2,1,0:T(8,128)S(1)} %copy.87, bf16[32,32,8,224]{3,2,1,0:T(8,128)(2,1)} %gather_fusion.1, pred[32]{0:T(512)(128)(4,1)S(1)} %compare_and_fusion), kind=kOutput, calls=%fused_computation.10 | convolution fusion | flops 13557760 | bytes 5058592 | tf_op jit(solution)/shard_map/gsrt,sgtc->gsrc/dot_general | solution.py:81
  201.9 3.9 %broadcast_in_dim.116 = bf16[3072,224]{1,0:T(8,128)(2,1)S(1)} reshape(bf16[32,32,3,224]{3,2,1,0:T(4,128)(2,1)} %fusion.4) | data formatting | bytes 2752512 | tf_op jit(solution)/shard_map/jit(_where)/broadcast_in_dim | solution.py:85
  205.8 0.7 copy.89
  207.1 2.8 %broadcast_select_fusion = bf16[3072,4,224]{0,2,1:T(8,128)(2,1)} fusion(pred[3072,4]{0,1:T(4,128)(4,1)S(1)} %iota_compare_fusion.5, bf16[3072,224]{0,1:T(8,128)(2,1)S(1)} %copy.89), kind=kLoop, calls=%fused_computation.5 | loop fusion | flops 2752512 | bytes 6893568 | tf_op jit(solution)/shard_map/jit(_where)/select_n | solution.py:85
  209.9 10.7 %fusion.7 = bf16[1024,896]{0,1:T(8,128)(2,1)} fusion(bf16[3072,896]{0,1:T(8,128)(2,1)} %bitcast.88, bf16[3072,1024]{1,0:T(8,128)(2,1)} %all-gather.2.cloned.1.call-done, f32[3072]{0:T(1024)S(1)} %mul.31), kind=kOutput, calls=%fused_computation.11 | convolution fusion | flops 5647499264 | bytes 13643776 | tf_op jit(solution)/shard_map/dot_general | solution.py:87
  (81 shorter events, 8.4 us)
Async XLA Ops:
  9.9 23.4 %all-to-all-start = ((bf16[32,8,240]{2,1,0:T(8,128)(2,1)}), bf16[32,8,240]{2,1,0:T(8,128)(2,1)S(1)}, u32[]{:S(2)}, u32[]{:S(2)}) async-start(bf16[32,8,240]{2,1,0:T(8,128)(2,1)} %pad_maximum_fusion), calls=%async_computation | async-start | bytes 262144 | tf_op jit(solution)/shard_map/all_to_all | solution.py:52
  26.6 183.2 %all-gather.2.cloned.1.call-start = ((), (), s32[]{:S(2)}) async-start(), calls=%async_computation.1 | async-start | bytes 6488064 | tf_op jit(solution)/shard_map/all_gather | solution.py:45
  33.4 12.6 %collective-permute-start = (bf16[32,8,240]{2,1,0:T(8,128)(2,1)S(1)}, bf16[32,8,240]{2,1,0:T(8,128)(2,1)S(1)}, u32[]{:S(2)}, u32[]{:S(2)}) collective-permute-start(bf16[32,8,240]{2,1,0:T(8,128)(2,1)S(1)} %all-to-all-done), channel_id=1, source_target_pairs={{0,992},{32,0},{64,32},{96,64},{128,96},{160,128},{192,160},{224,1... | collective-permute-start | bytes 368648 | tf_op jit(solution)/shard_map/ppermute | solution.py:65
  42.9 8.7 %collective-permute-start.15 = (bf16[32,8,240]{2,1,0:T(8,128)(2,1)S(1)}, bf16[32,8,240]{2,1,0:T(8,128)(2,1)S(1)}, u32[]{:S(2)}, u32[]{:S(2)}) collective-permute-start(bf16[32,8,240]{2,1,0:T(8,128)(2,1)S(1)} %all-to-all-done), channel_id=1, source_target_pairs={{0,32},{32,64},{64,96},{96,128},{128,160},{160,192},{192,224},{224... | collective-permute-start | bytes 368648 | tf_op jit(solution)/shard_map/ppermute | solution.py:62
  45.9 8.1 %collective-permute-start.1 = (bf16[32,8,240]{2,1,0:T(8,128)(2,1)S(1)}, bf16[32,8,240]{2,1,0:T(8,128)(2,1)S(1)}, u32[]{:S(2)}, u32[]{:S(2)}) collective-permute-start(bf16[32,8,240]{2,1,0:T(8,128)(2,1)S(1)} %collective-permute-done), channel_id=1, source_target_pairs={{0,992},{32,0},{64,32},{96,64},{128,96},{160,128},{192,160},{224,1... | collective-permute-start | bytes 368648 | tf_op jit(solution)/shard_map/ppermute | solution.py:65
  51.5 8.1 %collective-permute-start.16 = (bf16[32,8,240]{2,1,0:T(8,128)(2,1)S(1)}, bf16[32,8,240]{2,1,0:T(8,128)(2,1)S(1)}, u32[]{:S(2)}, u32[]{:S(2)}) collective-permute-start(bf16[32,8,240]{2,1,0:T(8,128)(2,1)S(1)} %collective-permute-done.15), channel_id=1, source_target_pairs={{0,32},{32,64},{64,96},{96,128},{128,160},{160,192},{192,224},{224... | collective-permute-start | bytes 368648 | tf_op jit(solution)/shard_map/ppermute | solution.py:62
  54.0 8.1 %collective-permute-start.2 = (bf16[32,8,240]{2,1,0:T(8,128)(2,1)S(1)}, bf16[32,8,240]{2,1,0:T(8,128)(2,1)S(1)}, u32[]{:S(2)}, u32[]{:S(2)}) collective-permute-start(bf16[32,8,240]{2,1,0:T(8,128)(2,1)S(1)} %collective-permute-done.1), channel_id=1, source_target_pairs={{0,992},{32,0},{64,32},{96,64},{128,96},{160,128},{192,160},{224,1... | collective-permute-start | bytes 368648 | tf_op jit(solution)/shard_map/ppermute | solution.py:65
  59.6 8.1 %collective-permute-start.17 = (bf16[32,8,240]{2,1,0:T(8,128)(2,1)S(1)}, bf16[32,8,240]{2,1,0:T(8,128)(2,1)S(1)}, u32[]{:S(2)}, u32[]{:S(2)}) collective-permute-start(bf16[32,8,240]{2,1,0:T(8,128)(2,1)S(1)} %collective-permute-done.16), channel_id=1, source_target_pairs={{0,32},{32,64},{64,96},{96,128},{128,160},{160,192},{192,224},{224... | collective-permute-start | bytes 368648 | tf_op jit(solution)/shard_map/ppermute | solution.py:62
  62.1 8.1 %collective-permute-start.3 = (bf16[32,8,240]{2,1,0:T(8,128)(2,1)S(1)}, bf16[32,8,240]{2,1,0:T(8,128)(2,1)S(1)}, u32[]{:S(2)}, u32[]{:S(2)}) collective-permute-start(bf16[32,8,240]{2,1,0:T(8,128)(2,1)S(1)} %collective-permute-done.2), channel_id=1, source_target_pairs={{0,992},{32,0},{64,32},{96,64},{128,96},{160,128},{192,160},{224,1... | collective-permute-start | bytes 368648 | tf_op jit(solution)/shard_map/ppermute | solution.py:65
  67.7 8.1 %collective-permute-start.18 = (bf16[32,8,240]{2,1,0:T(8,128)(2,1)S(1)}, bf16[32,8,240]{2,1,0:T(8,128)(2,1)S(1)}, u32[]{:S(2)}, u32[]{:S(2)}) collective-permute-start(bf16[32,8,240]{2,1,0:T(8,128)(2,1)S(1)} %collective-permute-done.17), channel_id=1, source_target_pairs={{0,32},{32,64},{64,96},{96,128},{128,160},{160,192},{192,224},{224... | collective-permute-start | bytes 368648 | tf_op jit(solution)/shard_map/ppermute | solution.py:62
  70.1 8.1 %collective-permute-start.4 = (bf16[32,8,240]{2,1,0:T(8,128)(2,1)S(1)}, bf16[32,8,240]{2,1,0:T(8,128)(2,1)S(1)}, u32[]{:S(2)}, u32[]{:S(2)}) collective-permute-start(bf16[32,8,240]{2,1,0:T(8,128)(2,1)S(1)} %collective-permute-done.3), channel_id=1, source_target_pairs={{0,992},{32,0},{64,32},{96,64},{128,96},{160,128},{192,160},{224,1... | collective-permute-start | bytes 368648 | tf_op jit(solution)/shard_map/ppermute | solution.py:65
  75.7 8.1 %collective-permute-start.19 = (bf16[32,8,240]{2,1,0:T(8,128)(2,1)S(1)}, bf16[32,8,240]{2,1,0:T(8,128)(2,1)S(1)}, u32[]{:S(2)}, u32[]{:S(2)}) collective-permute-start(bf16[32,8,240]{2,1,0:T(8,128)(2,1)S(1)} %collective-permute-done.18), channel_id=1, source_target_pairs={{0,32},{32,64},{64,96},{96,128},{128,160},{160,192},{192,224},{224... | collective-permute-start | bytes 368648 | tf_op jit(solution)/shard_map/ppermute | solution.py:62
  78.2 8.8 %collective-permute-start.5 = (bf16[32,8,240]{2,1,0:T(8,128)(2,1)S(1)}, bf16[32,8,240]{2,1,0:T(8,128)(2,1)S(1)}, u32[]{:S(2)}, u32[]{:S(2)}) collective-permute-start(bf16[32,8,240]{2,1,0:T(8,128)(2,1)S(1)} %collective-permute-done.4), channel_id=1, source_target_pairs={{0,992},{32,0},{64,32},{96,64},{128,96},{160,128},{192,160},{224,1... | collective-permute-start | bytes 368648 | tf_op jit(solution)/shard_map/ppermute | solution.py:65
  83.8 9.2 %collective-permute-start.20 = (bf16[32,8,240]{2,1,0:T(8,128)(2,1)S(1)}, bf16[32,8,240]{2,1,0:T(8,128)(2,1)S(1)}, u32[]{:S(2)}, u32[]{:S(2)}) collective-permute-start(bf16[32,8,240]{2,1,0:T(8,128)(2,1)S(1)} %collective-permute-done.19), channel_id=1, source_target_pairs={{0,32},{32,64},{64,96},{96,128},{128,160},{160,192},{192,224},{224... | collective-permute-start | bytes 368648 | tf_op jit(solution)/shard_map/ppermute | solution.py:62
  87.0 8.9 %collective-permute-start.6 = (bf16[32,8,240]{2,1,0:T(8,128)(2,1)S(1)}, bf16[32,8,240]{2,1,0:T(8,128)(2,1)S(1)}, u32[]{:S(2)}, u32[]{:S(2)}) collective-permute-start(bf16[32,8,240]{2,1,0:T(8,128)(2,1)S(1)} %collective-permute-done.5), channel_id=1, source_target_pairs={{0,992},{32,0},{64,32},{96,64},{128,96},{160,128},{192,160},{224,1... | collective-permute-start | bytes 368648 | tf_op jit(solution)/shard_map/ppermute | solution.py:65
  92.9 8.6 %collective-permute-start.21 = (bf16[32,8,240]{2,1,0:T(8,128)(2,1)S(1)}, bf16[32,8,240]{2,1,0:T(8,128)(2,1)S(1)}, u32[]{:S(2)}, u32[]{:S(2)}) collective-permute-start(bf16[32,8,240]{2,1,0:T(8,128)(2,1)S(1)} %collective-permute-done.20), channel_id=1, source_target_pairs={{0,32},{32,64},{64,96},{96,128},{128,160},{160,192},{192,224},{224... | collective-permute-start | bytes 368648 | tf_op jit(solution)/shard_map/ppermute | solution.py:62
  95.9 8.1 %collective-permute-start.7 = (bf16[32,8,240]{2,1,0:T(8,128)(2,1)S(1)}, bf16[32,8,240]{2,1,0:T(8,128)(2,1)S(1)}, u32[]{:S(2)}, u32[]{:S(2)}) collective-permute-start(bf16[32,8,240]{2,1,0:T(8,128)(2,1)S(1)} %collective-permute-done.6), channel_id=1, source_target_pairs={{0,992},{32,0},{64,32},{96,64},{128,96},{160,128},{192,160},{224,1... | collective-permute-start | bytes 368648 | tf_op jit(solution)/shard_map/ppermute | solution.py:65
  101.6 8.1 %collective-permute-start.22 = (bf16[32,8,240]{2,1,0:T(8,128)(2,1)S(1)}, bf16[32,8,240]{2,1,0:T(8,128)(2,1)S(1)}, u32[]{:S(2)}, u32[]{:S(2)}) collective-permute-start(bf16[32,8,240]{2,1,0:T(8,128)(2,1)S(1)} %collective-permute-done.21), channel_id=1, source_target_pairs={{0,32},{32,64},{64,96},{96,128},{128,160},{160,192},{192,224},{224... | collective-permute-start | bytes 368648 | tf_op jit(solution)/shard_map/ppermute | solution.py:62
  104.1 8.1 %collective-permute-start.8 = (bf16[32,8,240]{2,1,0:T(8,128)(2,1)S(1)}, bf16[32,8,240]{2,1,0:T(8,128)(2,1)S(1)}, u32[]{:S(2)}, u32[]{:S(2)}) collective-permute-start(bf16[32,8,240]{2,1,0:T(8,128)(2,1)S(1)} %collective-permute-done.7), channel_id=1, source_target_pairs={{0,992},{32,0},{64,32},{96,64},{128,96},{160,128},{192,160},{224,1... | collective-permute-start | bytes 368648 | tf_op jit(solution)/shard_map/ppermute | solution.py:65
  109.7 8.1 %collective-permute-start.23 = (bf16[32,8,240]{2,1,0:T(8,128)(2,1)S(1)}, bf16[32,8,240]{2,1,0:T(8,128)(2,1)S(1)}, u32[]{:S(2)}, u32[]{:S(2)}) collective-permute-start(bf16[32,8,240]{2,1,0:T(8,128)(2,1)S(1)} %collective-permute-done.22), channel_id=1, source_target_pairs={{0,32},{32,64},{64,96},{96,128},{128,160},{160,192},{192,224},{224... | collective-permute-start | bytes 368648 | tf_op jit(solution)/shard_map/ppermute | solution.py:62
  112.2 8.1 %collective-permute-start.9 = (bf16[32,8,240]{2,1,0:T(8,128)(2,1)S(1)}, bf16[32,8,240]{2,1,0:T(8,128)(2,1)S(1)}, u32[]{:S(2)}, u32[]{:S(2)}) collective-permute-start(bf16[32,8,240]{2,1,0:T(8,128)(2,1)S(1)} %collective-permute-done.8), channel_id=1, source_target_pairs={{0,992},{32,0},{64,32},{96,64},{128,96},{160,128},{192,160},{224,1... | collective-permute-start | bytes 368648 | tf_op jit(solution)/shard_map/ppermute | solution.py:65
  117.8 8.1 %collective-permute-start.24 = (bf16[32,8,240]{2,1,0:T(8,128)(2,1)S(1)}, bf16[32,8,240]{2,1,0:T(8,128)(2,1)S(1)}, u32[]{:S(2)}, u32[]{:S(2)}) collective-permute-start(bf16[32,8,240]{2,1,0:T(8,128)(2,1)S(1)} %collective-permute-done.23), channel_id=1, source_target_pairs={{0,32},{32,64},{64,96},{96,128},{128,160},{160,192},{192,224},{224... | collective-permute-start | bytes 368648 | tf_op jit(solution)/shard_map/ppermute | solution.py:62
  120.2 8.1 %collective-permute-start.10 = (bf16[32,8,240]{2,1,0:T(8,128)(2,1)S(1)}, bf16[32,8,240]{2,1,0:T(8,128)(2,1)S(1)}, u32[]{:S(2)}, u32[]{:S(2)}) collective-permute-start(bf16[32,8,240]{2,1,0:T(8,128)(2,1)S(1)} %collective-permute-done.9), channel_id=1, source_target_pairs={{0,992},{32,0},{64,32},{96,64},{128,96},{160,128},{192,160},{224,1... | collective-permute-start | bytes 368648 | tf_op jit(solution)/shard_map/ppermute | solution.py:65
  125.8 8.1 %collective-permute-start.25 = (bf16[32,8,240]{2,1,0:T(8,128)(2,1)S(1)}, bf16[32,8,240]{2,1,0:T(8,128)(2,1)S(1)}, u32[]{:S(2)}, u32[]{:S(2)}) collective-permute-start(bf16[32,8,240]{2,1,0:T(8,128)(2,1)S(1)} %collective-permute-done.24), channel_id=1, source_target_pairs={{0,32},{32,64},{64,96},{96,128},{128,160},{160,192},{192,224},{224... | collective-permute-start | bytes 368648 | tf_op jit(solution)/shard_map/ppermute | solution.py:62
  128.3 8.1 %collective-permute-start.11 = (bf16[32,8,240]{2,1,0:T(8,128)(2,1)S(1)}, bf16[32,8,240]{2,1,0:T(8,128)(2,1)S(1)}, u32[]{:S(2)}, u32[]{:S(2)}) collective-permute-start(bf16[32,8,240]{2,1,0:T(8,128)(2,1)S(1)} %collective-permute-done.10), channel_id=1, source_target_pairs={{0,992},{32,0},{64,32},{96,64},{128,96},{160,128},{192,160},{224,1... | collective-permute-start | bytes 368648 | tf_op jit(solution)/shard_map/ppermute | solution.py:65
  133.9 8.1 %collective-permute-start.26 = (bf16[32,8,240]{2,1,0:T(8,128)(2,1)S(1)}, bf16[32,8,240]{2,1,0:T(8,128)(2,1)S(1)}, u32[]{:S(2)}, u32[]{:S(2)}) collective-permute-start(bf16[32,8,240]{2,1,0:T(8,128)(2,1)S(1)} %collective-permute-done.25), channel_id=1, source_target_pairs={{0,32},{32,64},{64,96},{96,128},{128,160},{160,192},{192,224},{224... | collective-permute-start | bytes 368648 | tf_op jit(solution)/shard_map/ppermute | solution.py:62
  136.4 8.9 %collective-permute-start.12 = (bf16[32,8,240]{2,1,0:T(8,128)(2,1)S(1)}, bf16[32,8,240]{2,1,0:T(8,128)(2,1)S(1)}, u32[]{:S(2)}, u32[]{:S(2)}) collective-permute-start(bf16[32,8,240]{2,1,0:T(8,128)(2,1)S(1)} %collective-permute-done.11), channel_id=1, source_target_pairs={{0,992},{32,0},{64,32},{96,64},{128,96},{160,128},{192,160},{224,1... | collective-permute-start | bytes 368648 | tf_op jit(solution)/shard_map/ppermute | solution.py:65
  141.9 9.1 %collective-permute-start.27 = (bf16[32,8,240]{2,1,0:T(8,128)(2,1)S(1)}, bf16[32,8,240]{2,1,0:T(8,128)(2,1)S(1)}, u32[]{:S(2)}, u32[]{:S(2)}) collective-permute-start(bf16[32,8,240]{2,1,0:T(8,128)(2,1)S(1)} %collective-permute-done.26), channel_id=1, source_target_pairs={{0,32},{32,64},{64,96},{96,128},{128,160},{160,192},{192,224},{224... | collective-permute-start | bytes 368648 | tf_op jit(solution)/shard_map/ppermute | solution.py:62
  145.3 8.1 %collective-permute-start.13 = (bf16[32,8,240]{2,1,0:T(8,128)(2,1)S(1)}, bf16[32,8,240]{2,1,0:T(8,128)(2,1)S(1)}, u32[]{:S(2)}, u32[]{:S(2)}) collective-permute-start(bf16[32,8,240]{2,1,0:T(8,128)(2,1)S(1)} %collective-permute-done.12), channel_id=1, source_target_pairs={{0,992},{32,0},{64,32},{96,64},{128,96},{160,128},{192,160},{224,1... | collective-permute-start | bytes 368648 | tf_op jit(solution)/shard_map/ppermute | solution.py:65
  151.1 8.6 %collective-permute-start.28 = (bf16[32,8,240]{2,1,0:T(8,128)(2,1)S(1)}, bf16[32,8,240]{2,1,0:T(8,128)(2,1)S(1)}, u32[]{:S(2)}, u32[]{:S(2)}) collective-permute-start(bf16[32,8,240]{2,1,0:T(8,128)(2,1)S(1)} %collective-permute-done.27), channel_id=1, source_target_pairs={{0,32},{32,64},{64,96},{96,128},{128,160},{160,192},{192,224},{224... | collective-permute-start | bytes 368648 | tf_op jit(solution)/shard_map/ppermute | solution.py:62
  153.3 16.4 %collective-permute-start.14 = (bf16[32,8,240]{2,1,0:T(8,128)(2,1)S(1)}, bf16[32,8,240]{2,1,0:T(8,128)(2,1)S(1)}, u32[]{:S(2)}, u32[]{:S(2)}) collective-permute-start(bf16[32,8,240]{2,1,0:T(8,128)(2,1)S(1)} %collective-permute-done.13), channel_id=1, source_target_pairs={{0,992},{32,0},{64,32},{96,64},{128,96},{160,128},{192,160},{224,1... | collective-permute-start | bytes 368648 | tf_op jit(solution)/shard_map/ppermute | solution.py:65
  159.7 8.1 %collective-permute-start.29 = (bf16[32,8,240]{2,1,0:T(8,128)(2,1)S(1)}, bf16[32,8,240]{2,1,0:T(8,128)(2,1)S(1)}, u32[]{:S(2)}, u32[]{:S(2)}) collective-permute-start(bf16[32,8,240]{2,1,0:T(8,128)(2,1)S(1)} %collective-permute-done.28), channel_id=1, source_target_pairs={{0,32},{32,64},{64,96},{96,128},{128,160},{160,192},{192,224},{224... | collective-permute-start | bytes 368648 | tf_op jit(solution)/shard_map/ppermute | solution.py:62
  167.8 8.1 %collective-permute-start.30 = (bf16[32,8,240]{2,1,0:T(8,128)(2,1)S(1)}, bf16[32,8,240]{2,1,0:T(8,128)(2,1)S(1)}, u32[]{:S(2)}, u32[]{:S(2)}) collective-permute-start(bf16[32,8,240]{2,1,0:T(8,128)(2,1)S(1)} %collective-permute-done.29), channel_id=1, source_target_pairs={{0,32},{32,64},{64,96},{96,128},{128,160},{160,192},{192,224},{224... | collective-permute-start | bytes 368648 | tf_op jit(solution)/shard_map/ppermute | solution.py:62
  176.1 2.0 copy-start
Sparse Core Ops, SparseCore 0:
  31.8 82.4 all-gather.1

commit v9 on v5

--- a/solution.py
+++ b/solution.py
@@ -74,7 +74,13 @@
 
     hidden_t = jnp.transpose(hidden)
     rows_t = (weight[None, :] * hidden_t.astype(jnp.float32)).astype(jnp.bfloat16)
-    grad_rows = jnp.take(tokens, token, axis=0, mode="clip")[:, :width]
+    forward = (jnp.arange(n_exp, dtype=jnp.int32) + me_exp) % n_exp
+    pick_t = jnp.take((token % TOK_DEV).reshape(n_grp, n_exp, capacity), forward, axis=1)
+    onehot = (pick_t[..., None] == jnp.arange(TOK_DEV, dtype=jnp.int32)).astype(jnp.bfloat16)
+    grad_rows = jnp.einsum(
+        "gqrt,qgtc->gqrc", onehot, ring[..., :width], preferred_element_type=jnp.float32
+    ).astype(jnp.bfloat16)
+    grad_rows = jnp.take(grad_rows, relative, axis=1).reshape(-1, width)
     mask = label[:, None] == jnp.arange(EXP_DEV, dtype=jnp.int32)[None, :]
     spread = jnp.where(mask[:, :, None], grad_rows[:, None, :], jnp.zeros_like(grad_rows)[:, None, :])
     spread = spread.reshape(grad_rows.shape[0], EXP_DEV * width)

time: 232 us -> 242 us (1.043)
  local copies, waits for them, and re-layouts: 28.9 us -> 47.1 us
  waiting for transfers between devices: 31.4 us -> 18.6 us
  matrix products: 11.1 us -> 15.3 us
    unnamed x35 -> x32, local copies, waits for them, and re-layouts: 5.79 us -> 22.4 us
    ppermute x15, waiting for transfers between devices: 7.61 us -> 1.53 us  [per_device(): bwd = lax.ppermute(bwd, 'expert', bwd_perm)]
    dot_general x0 -> x1, matrix products: none -> 4.25 us  [per_device(): jnp.einsum('gqrt,qgtc->gqrc', onehot, ring[..., :width], preferred_elemen...]
    ppermute x16, waiting for transfers between devices: 17.1 us -> 12.9 us  [per_device(): fwd = lax.ppermute(fwd, 'expert', fwd_perm)]
    select_n x0 -> x4, other arithmetic: none -> 2.88 us  [the longest x1 2.71 us: per_device(): grad_rows = jnp.take(grad_rows, relative, axis=1).reshape(-1, width)]
    gather x1 -> x4, local copies, waits for them, and re-layouts: 12.5 us -> 9.8 us  [the longest x3 9.19 us: per_device(): grad_rows = jnp.take(grad_rows, relative, axis=1).reshape(-1, width)]
    all_to_all x1, waiting for transfers between devices: 6.63 us -> 4.1 us  [per_device(): cols = lax.all_to_all(cols, 'dp', 0, 0, tiled=True)]
  transfers between devices with their start and end apart: 33 -> 33, of which waited for: 25 -> 14; matrix products, arithmetic and copies ran while one was open for 16% -> 25% of each run, Pallas kernels for 0% -> 0%
where the time goes in v9:
time: 242 us; the launch traced here: 240 us
  starting transfers between devices  133 us (55%)
  local copies, waits for them, and re-layouts  47.1 us (19%)
  waiting for transfers between devices  18.6 us (8%)
  matrix products  15.3 us (6%)
  between operations  13.9 us (6%)
  other arithmetic  12.9 us (5%)
    ppermute x15, starting transfers between devices, per_device(): bwd = lax.ppermute(bwd, 'expert', bwd_perm)  85.1 us
    ppermute x16, starting transfers between devices, per_device(): fwd = lax.ppermute(fwd, 'expert', fwd_perm)  30.7 us
    unnamed x32, local copies, waits for them, and re-layouts  22.4 us
    all_to_all x1, starting transfers between devices, per_device(): cols = lax.all_to_all(cols, 'dp', 0, 0, tiled=True)  16.7 us
    ppermute x16, waiting for transfers between devices, per_device(): fwd = lax.ppermute(fwd, 'expert', fwd_perm)  12.9 us
    dot_general x1, matrix products, per_device(): gradient = jnp.dot(rows_t, spread, preferred_element_type=jnp.float32)  10.7 us
    gather x3, local copies, waits for them, and re-layouts, per_device(): grad_rows = jnp.take(grad_rows, relative, axis=1).reshape(-1, width)  9.19 us
  transfers between devices with their start and end apart: 33, of which 14 were waited for; matrix products, arithmetic and copies ran while one was open for 25% of the time, Pallas kernels for 0%

profile of v9, /device:TPU:2, one launch (start us, length us, event | category | flops | bytes accessed | tf_op | source)
XLA Modules:
  0.0 240.5 jit_solution(13105082337097205360)
XLA Ops:
  6.5 1.1 reshape.283
  7.7 0.7 convert_element_type.27
  8.4 0.8 pad_maximum_fusion.1
  9.2 0.7 pad_maximum_fusion
  9.9 16.7 %all-to-all-start = ((bf16[32,8,240]{2,1,0:T(8,128)(2,1)}), bf16[32,8,240]{2,1,0:T(8,128)(2,1)S(1)}, u32[]{:S(2)}, u32[]{:S(2)}) async-start(bf16[32,8,240]{2,1,0:T(8,128)(2,1)} %pad_maximum_fusion), calls=%async_computation | async-start | bytes 262144 | tf_op jit(solution)/shard_map/all_to_all | solution.py:52
  26.7 1.1 copy.218
  27.8 0.8 reshape.286
  29.3 4.1 %all-to-all-done = bf16[32,8,240]{2,1,0:T(8,128)(2,1)S(1)} async-done(((bf16[32,8,240]{2,1,0:T(8,128)(2,1)}), bf16[32,8,240]{2,1,0:T(8,128)(2,1)S(1)}, u32[]{:S(2)}, u32[]{:S(2)}) %all-to-all-start) | async-done | bytes 122912 | tf_op jit(solution)/shard_map/all_to_all | solution.py:52
  33.4 9.5 %collective-permute-start = (bf16[32,8,240]{2,1,0:T(8,128)(2,1)S(1)}, bf16[32,8,240]{2,1,0:T(8,128)(2,1)S(1)}, u32[]{:S(2)}, u32[]{:S(2)}) collective-permute-start(bf16[32,8,240]{2,1,0:T(8,128)(2,1)S(1)} %all-to-all-done), channel_id=1, source_target_pairs={{0,992},{32,0},{64,32},{96,64},{128,96},{160,128},{192,160},{224,1... | collective-permute-start | bytes 368648 | tf_op jit(solution)/shard_map/ppermute | solution.py:65
  42.9 1.9 collective-permute-start.15
  44.8 0.7 bitcast_dynamic-update-slice_fusion.30
  45.9 5.6 %collective-permute-start.1 = (bf16[32,8,240]{2,1,0:T(8,128)(2,1)S(1)}, bf16[32,8,240]{2,1,0:T(8,128)(2,1)S(1)}, u32[]{:S(2)}, u32[]{:S(2)}) collective-permute-start(bf16[32,8,240]{2,1,0:T(8,128)(2,1)S(1)} %collective-permute-done), channel_id=1, source_target_pairs={{0,992},{32,0},{64,32},{96,64},{128,96},{160,128},{192,160},{224,1... | collective-permute-start | bytes 368648 | tf_op jit(solution)/shard_map/ppermute | solution.py:65
  51.5 1.9 collective-permute-start.16
  54.1 5.4 %collective-permute-start.2 = (bf16[32,8,240]{2,1,0:T(8,128)(2,1)S(1)}, bf16[32,8,240]{2,1,0:T(8,128)(2,1)S(1)}, u32[]{:S(2)}, u32[]{:S(2)}) collective-permute-start(bf16[32,8,240]{2,1,0:T(8,128)(2,1)S(1)} %collective-permute-done.1), channel_id=1, source_target_pairs={{0,992},{32,0},{64,32},{96,64},{128,96},{160,128},{192,160},{224,1... | collective-permute-start | bytes 368648 | tf_op jit(solution)/shard_map/ppermute | solution.py:65
  59.6 1.9 collective-permute-start.17
  62.2 5.4 %collective-permute-start.3 = (bf16[32,8,240]{2,1,0:T(8,128)(2,1)S(1)}, bf16[32,8,240]{2,1,0:T(8,128)(2,1)S(1)}, u32[]{:S(2)}, u32[]{:S(2)}) collective-permute-start(bf16[32,8,240]{2,1,0:T(8,128)(2,1)S(1)} %collective-permute-done.2), channel_id=1, source_target_pairs={{0,992},{32,0},{64,32},{96,64},{128,96},{160,128},{192,160},{224,1... | collective-permute-start | bytes 368648 | tf_op jit(solution)/shard_map/ppermute | solution.py:65
  67.7 1.9 collective-permute-start.18
  69.6 0.7 bitcast_dynamic-update-slice_fusion.27
  70.3 5.4 %collective-permute-start.4 = (bf16[32,8,240]{2,1,0:T(8,128)(2,1)S(1)}, bf16[32,8,240]{2,1,0:T(8,128)(2,1)S(1)}, u32[]{:S(2)}, u32[]{:S(2)}) collective-permute-start(bf16[32,8,240]{2,1,0:T(8,128)(2,1)S(1)} %collective-permute-done.3), channel_id=1, source_target_pairs={{0,992},{32,0},{64,32},{96,64},{128,96},{160,128},{192,160},{224,1... | collective-permute-start | bytes 368648 | tf_op jit(solution)/shard_map/ppermute | solution.py:65
  75.7 1.9 collective-permute-start.19
  78.3 5.4 %collective-permute-start.5 = (bf16[32,8,240]{2,1,0:T(8,128)(2,1)S(1)}, bf16[32,8,240]{2,1,0:T(8,128)(2,1)S(1)}, u32[]{:S(2)}, u32[]{:S(2)}) collective-permute-start(bf16[32,8,240]{2,1,0:T(8,128)(2,1)S(1)} %collective-permute-done.4), channel_id=1, source_target_pairs={{0,992},{32,0},{64,32},{96,64},{128,96},{160,128},{192,160},{224,1... | collective-permute-start | bytes 368648 | tf_op jit(solution)/shard_map/ppermute | solution.py:65
  83.8 1.9 collective-permute-start.20
  85.7 0.7 bitcast_dynamic-update-slice_fusion.25
  86.4 5.4 %collective-permute-start.6 = (bf16[32,8,240]{2,1,0:T(8,128)(2,1)S(1)}, bf16[32,8,240]{2,1,0:T(8,128)(2,1)S(1)}, u32[]{:S(2)}, u32[]{:S(2)}) collective-permute-start(bf16[32,8,240]{2,1,0:T(8,128)(2,1)S(1)} %collective-permute-done.5), channel_id=1, source_target_pairs={{0,992},{32,0},{64,32},{96,64},{128,96},{160,128},{192,160},{224,1... | collective-permute-start | bytes 368648 | tf_op jit(solution)/shard_map/ppermute | solution.py:65
  91.8 1.9 collective-permute-start.21
  93.8 0.7 bitcast_dynamic-update-slice_fusion.24
  94.5 5.5 %collective-permute-start.7 = (bf16[32,8,240]{2,1,0:T(8,128)(2,1)S(1)}, bf16[32,8,240]{2,1,0:T(8,128)(2,1)S(1)}, u32[]{:S(2)}, u32[]{:S(2)}) collective-permute-start(bf16[32,8,240]{2,1,0:T(8,128)(2,1)S(1)} %collective-permute-done.6), channel_id=1, source_target_pairs={{0,992},{32,0},{64,32},{96,64},{128,96},{160,128},{192,160},{224,1... | collective-permute-start | bytes 368648 | tf_op jit(solution)/shard_map/ppermute | solution.py:65
  100.3 1.9 collective-permute-start.22
  102.2 0.7 bitcast_dynamic-update-slice_fusion.23
  103.5 5.6 %collective-permute-start.8 = (bf16[32,8,240]{2,1,0:T(8,128)(2,1)S(1)}, bf16[32,8,240]{2,1,0:T(8,128)(2,1)S(1)}, u32[]{:S(2)}, u32[]{:S(2)}) collective-permute-start(bf16[32,8,240]{2,1,0:T(8,128)(2,1)S(1)} %collective-permute-done.7), channel_id=1, source_target_pairs={{0,992},{32,0},{64,32},{96,64},{128,96},{160,128},{192,160},{224,1... | collective-permute-start | bytes 368648 | tf_op jit(solution)/shard_map/ppermute | solution.py:65
  109.5 1.9 collective-permute-start.23
  112.5 5.6 %collective-permute-start.9 = (bf16[32,8,240]{2,1,0:T(8,128)(2,1)S(1)}, bf16[32,8,240]{2,1,0:T(8,128)(2,1)S(1)}, u32[]{:S(2)}, u32[]{:S(2)}) collective-permute-start(bf16[32,8,240]{2,1,0:T(8,128)(2,1)S(1)} %collective-permute-done.8), channel_id=1, source_target_pairs={{0,992},{32,0},{64,32},{96,64},{128,96},{160,128},{192,160},{224,1... | collective-permute-start | bytes 368648 | tf_op jit(solution)/shard_map/ppermute | solution.py:65
  118.5 1.9 collective-permute-start.24
  120.4 0.7 bitcast_dynamic-update-slice_fusion.21
  121.1 5.4 %collective-permute-start.10 = (bf16[32,8,240]{2,1,0:T(8,128)(2,1)S(1)}, bf16[32,8,240]{2,1,0:T(8,128)(2,1)S(1)}, u32[]{:S(2)}, u32[]{:S(2)}) collective-permute-start(bf16[32,8,240]{2,1,0:T(8,128)(2,1)S(1)} %collective-permute-done.9), channel_id=1, source_target_pairs={{0,992},{32,0},{64,32},{96,64},{128,96},{160,128},{192,160},{224,1... | collective-permute-start | bytes 368648 | tf_op jit(solution)/shard_map/ppermute | solution.py:65
  126.7 1.9 collective-permute-start.25
  129.3 5.2 %collective-permute-start.11 = (bf16[32,8,240]{2,1,0:T(8,128)(2,1)S(1)}, bf16[32,8,240]{2,1,0:T(8,128)(2,1)S(1)}, u32[]{:S(2)}, u32[]{:S(2)}) collective-permute-start(bf16[32,8,240]{2,1,0:T(8,128)(2,1)S(1)} %collective-permute-done.10), channel_id=1, source_target_pairs={{0,992},{32,0},{64,32},{96,64},{128,96},{160,128},{192,160},{224,1... | collective-permute-start | bytes 368648 | tf_op jit(solution)/shard_map/ppermute | solution.py:65
  134.7 1.9 collective-permute-start.26
  137.3 5.2 %collective-permute-start.12 = (bf16[32,8,240]{2,1,0:T(8,128)(2,1)S(1)}, bf16[32,8,240]{2,1,0:T(8,128)(2,1)S(1)}, u32[]{:S(2)}, u32[]{:S(2)}) collective-permute-start(bf16[32,8,240]{2,1,0:T(8,128)(2,1)S(1)} %collective-permute-done.11), channel_id=1, source_target_pairs={{0,992},{32,0},{64,32},{96,64},{128,96},{160,128},{192,160},{224,1... | collective-permute-start | bytes 368648 | tf_op jit(solution)/shard_map/ppermute | solution.py:65
  142.8 1.9 collective-permute-start.27
  145.4 5.2 %collective-permute-start.13 = (bf16[32,8,240]{2,1,0:T(8,128)(2,1)S(1)}, bf16[32,8,240]{2,1,0:T(8,128)(2,1)S(1)}, u32[]{:S(2)}, u32[]{:S(2)}) collective-permute-start(bf16[32,8,240]{2,1,0:T(8,128)(2,1)S(1)} %collective-permute-done.12), channel_id=1, source_target_pairs={{0,992},{32,0},{64,32},{96,64},{128,96},{160,128},{192,160},{224,1... | collective-permute-start | bytes 368648 | tf_op jit(solution)/shard_map/ppermute | solution.py:65
  150.9 1.9 collective-permute-start.28
  153.5 5.2 %collective-permute-start.14 = (bf16[32,8,240]{2,1,0:T(8,128)(2,1)S(1)}, bf16[32,8,240]{2,1,0:T(8,128)(2,1)S(1)}, u32[]{:S(2)}, u32[]{:S(2)}) collective-permute-start(bf16[32,8,240]{2,1,0:T(8,128)(2,1)S(1)} %collective-permute-done.13), channel_id=1, source_target_pairs={{0,992},{32,0},{64,32},{96,64},{128,96},{160,128},{192,160},{224,1... | collective-permute-start | bytes 368648 | tf_op jit(solution)/shard_map/ppermute | solution.py:65
  158.9 1.9 collective-permute-start.29
  161.5 5.5 %collective-permute-done.29 = bf16[32,8,240]{2,1,0:T(8,128)(2,1)S(1)} collective-permute-done((bf16[32,8,240]{2,1,0:T(8,128)(2,1)S(1)}, bf16[32,8,240]{2,1,0:T(8,128)(2,1)S(1)}, u32[]{:S(2)}, u32[]{:S(2)}) %collective-permute-start.29) | collective-permute-done | bytes 122912 | tf_op jit(solution)/shard_map/ppermute | solution.py:62
  167.0 2.1 collective-permute-start.30
  169.8 5.3 %collective-permute-done.30 = bf16[32,8,240]{2,1,0:T(8,128)(2,1)S(1)} collective-permute-done((bf16[32,8,240]{2,1,0:T(8,128)(2,1)S(1)}, bf16[32,8,240]{2,1,0:T(8,128)(2,1)S(1)}, u32[]{:S(2)}, u32[]{:S(2)}) %collective-permute-start.30) | collective-permute-done | bytes 122912 | tf_op jit(solution)/shard_map/ppermute | solution.py:62
  175.7 0.7 bitcast_dynamic-update-slice_fusion.13
  176.4 0.7 bitcast_dynamic-update-slice_fusion.12
  177.1 0.7 bitcast_dynamic-update-slice_fusion.11
  183.9 0.7 bitcast_dynamic-update-slice_fusion.1
  185.3 0.7 bitcast_dynamic-update-slice_fusion.31
  186.0 2.2 slice.22
  188.3 2.1 copy.208
  190.4 0.7 gather_fusion
  191.2 2.2 copy.209
  197.8 3.4 %select_reduce_fusion = (s32[32,32,3]{1,2,0:T(4,128)S(1)}, s32[32,32,3]{1,2,0:T(4,128)S(1)}) fusion(s32[64]{0:T(128)S(1)} %and_select_fusion.1, s32[32,32,64]{2,1,0:T(8,128)S(1)} %bitcast.158, pred[32,32,64]{2,1,0:T(8,128)(4,1)S(1)} %fusion.10, s32[32,32,64]{2,1,0:T(8,128)S(1)} %fusion.11), kind=kLoop, calls=%fused_computation.12 | loop fusion | flops 1173504 | bytes 614656 | tf_op jit(solution)/shard_map/reduce_sum | solution.py:32
  202.6 4.2 %fusion.4 = bf16[32,32,3,224]{3,2,1,0:T(4,128)(2,1)S(1)} fusion(bf16[32,32,8,240]{3,2,0,1:T(8,128)(2,1)} %bitcast_dynamic-update-slice_fusion.31, s32[32,32,3]{2,1,0:T(8,128)S(1)} %copy.222), kind=kOutput, calls=%fused_computation.10 | convolution fusion | flops 11722752 | bytes 5320704 | tf_op jit(solution)/shard_map/gqrt,qgtc->gqrc/dot_general | solution.py:80
  206.9 4.0 %gather_fusion.2 = bf16[32,32,3,224]{3,2,1,0:T(4,128)(2,1)} fusion(bf16[32,32,3,224]{3,2,1,0:T(4,128)(2,1)S(1)} %fusion.4, s32[1024]{0:T(1024)S(1)} %get-tuple-element.13), kind=kCustom, calls=%fused_computation.2 | custom fusion | bytes 2752640 | tf_op jit(solution)/shard_map/jit(_take)/gather | solution.py:83
  210.9 2.7 %copy.223 = bf16[32,32,3,224]{3,2,1,0:T(4,128)(2,1)S(1)} copy(bf16[32,32,3,224]{3,2,0,1:T(4,128)(2,1)} %bitcast.155) | data formatting | bytes 2752512 | tf_op jit(solution)/shard_map/jit(_take)/gather | solution.py:83
  213.6 2.5 %gather.17 = bf16[3072,224]{1,0:T(8,128)(2,1)} reshape(bf16[32,32,3,224]{3,2,1,0:T(4,128)(2,1)S(1)} %copy.223) | data formatting | bytes 2752512 | tf_op jit(solution)/shard_map/jit(_take)/gather | solution.py:83
  216.1 2.7 %broadcast_select_fusion.1 = bf16[3072,224]{1,0:T(8,128)(2,1)S(1)} fusion(bf16[3072,224]{1,0:T(8,128)(2,1)} %gather.17, pred[3072]{0:T(1024)(128)(4,1)S(1)} %broadcast_in_dim.127), kind=kLoop, calls=%fused_computation.16 | loop fusion | flops 688128 | bytes 2755584 | tf_op jit(solution)/shard_map/jit(_take)/select_n | solution.py:83
  220.1 2.8 %broadcast_select_fusion = bf16[3072,4,224]{0,2,1:T(8,128)(2,1)} fusion(pred[3072,4]{0,1:T(4,128)(4,1)S(1)} %iota_compare_fusion.5, bf16[3072,224]{0,1:T(8,128)(2,1)S(1)} %copy.224), kind=kLoop, calls=%fused_computation.6 | loop fusion | flops 2752512 | bytes 6893568 | tf_op jit(solution)/shard_map/jit(_where)/select_n | solution.py:85
  222.9 10.7 %fusion.7 = bf16[1024,896]{0,1:T(8,128)(2,1)} fusion(bf16[3072,896]{0,1:T(8,128)(2,1)} %bitcast.156, bf16[3072,1024]{1,0:T(8,128)(2,1)} %all-gather.2.cloned.1.call-done, f32[3072]{0:T(1024)S(1)} %mul.31), kind=kOutput, calls=%fused_computation.11 | convolution fusion | flops 5647499264 | bytes 13643776 | tf_op jit(solution)/shard_map/dot_general | solution.py:87
  (87 shorter events, 25.8 us)
Async XLA Ops:
  9.9 23.4 %all-to-all-start = ((bf16[32,8,240]{2,1,0:T(8,128)(2,1)}), bf16[32,8,240]{2,1,0:T(8,128)(2,1)S(1)}, u32[]{:S(2)}, u32[]{:S(2)}) async-start(bf16[32,8,240]{2,1,0:T(8,128)(2,1)} %pad_maximum_fusion), calls=%async_computation | async-start | bytes 262144 | tf_op jit(solution)/shard_map/all_to_all | solution.py:52
  26.6 196.2 %all-gather.2.cloned.1.call-start = ((), (), s32[]{:S(2)}) async-start(), calls=%async_computation.1 | async-start | bytes 6488064 | tf_op jit(solution)/shard_map/all_gather | solution.py:45
  33.4 12.5 %collective-permute-start = (bf16[32,8,240]{2,1,0:T(8,128)(2,1)S(1)}, bf16[32,8,240]{2,1,0:T(8,128)(2,1)S(1)}, u32[]{:S(2)}, u32[]{:S(2)}) collective-permute-start(bf16[32,8,240]{2,1,0:T(8,128)(2,1)S(1)} %all-to-all-done), channel_id=1, source_target_pairs={{0,992},{32,0},{64,32},{96,64},{128,96},{160,128},{192,160},{224,1... | collective-permute-start | bytes 368648 | tf_op jit(solution)/shard_map/ppermute | solution.py:65
  42.9 8.7 %collective-permute-start.15 = (bf16[32,8,240]{2,1,0:T(8,128)(2,1)S(1)}, bf16[32,8,240]{2,1,0:T(8,128)(2,1)S(1)}, u32[]{:S(2)}, u32[]{:S(2)}) collective-permute-start(bf16[32,8,240]{2,1,0:T(8,128)(2,1)S(1)} %all-to-all-done), channel_id=1, source_target_pairs={{0,32},{32,64},{64,96},{96,128},{128,160},{160,192},{192,224},{224... | collective-permute-start | bytes 368648 | tf_op jit(solution)/shard_map/ppermute | solution.py:62
  45.9 8.2 %collective-permute-start.1 = (bf16[32,8,240]{2,1,0:T(8,128)(2,1)S(1)}, bf16[32,8,240]{2,1,0:T(8,128)(2,1)S(1)}, u32[]{:S(2)}, u32[]{:S(2)}) collective-permute-start(bf16[32,8,240]{2,1,0:T(8,128)(2,1)S(1)} %collective-permute-done), channel_id=1, source_target_pairs={{0,992},{32,0},{64,32},{96,64},{128,96},{160,128},{192,160},{224,1... | collective-permute-start | bytes 368648 | tf_op jit(solution)/shard_map/ppermute | solution.py:65
  51.5 8.1 %collective-permute-start.16 = (bf16[32,8,240]{2,1,0:T(8,128)(2,1)S(1)}, bf16[32,8,240]{2,1,0:T(8,128)(2,1)S(1)}, u32[]{:S(2)}, u32[]{:S(2)}) collective-permute-start(bf16[32,8,240]{2,1,0:T(8,128)(2,1)S(1)} %collective-permute-done.15), channel_id=1, source_target_pairs={{0,32},{32,64},{64,96},{96,128},{128,160},{160,192},{192,224},{224... | collective-permute-start | bytes 368648 | tf_op jit(solution)/shard_map/ppermute | solution.py:62
  54.1 8.0 %collective-permute-start.2 = (bf16[32,8,240]{2,1,0:T(8,128)(2,1)S(1)}, bf16[32,8,240]{2,1,0:T(8,128)(2,1)S(1)}, u32[]{:S(2)}, u32[]{:S(2)}) collective-permute-start(bf16[32,8,240]{2,1,0:T(8,128)(2,1)S(1)} %collective-permute-done.1), channel_id=1, source_target_pairs={{0,992},{32,0},{64,32},{96,64},{128,96},{160,128},{192,160},{224,1... | collective-permute-start | bytes 368648 | tf_op jit(solution)/shard_map/ppermute | solution.py:65
  59.6 8.1 %collective-permute-start.17 = (bf16[32,8,240]{2,1,0:T(8,128)(2,1)S(1)}, bf16[32,8,240]{2,1,0:T(8,128)(2,1)S(1)}, u32[]{:S(2)}, u32[]{:S(2)}) collective-permute-start(bf16[32,8,240]{2,1,0:T(8,128)(2,1)S(1)} %collective-permute-done.16), channel_id=1, source_target_pairs={{0,32},{32,64},{64,96},{96,128},{128,160},{160,192},{192,224},{224... | collective-permute-start | bytes 368648 | tf_op jit(solution)/shard_map/ppermute | solution.py:62
  62.2 8.1 %collective-permute-start.3 = (bf16[32,8,240]{2,1,0:T(8,128)(2,1)S(1)}, bf16[32,8,240]{2,1,0:T(8,128)(2,1)S(1)}, u32[]{:S(2)}, u32[]{:S(2)}) collective-permute-start(bf16[32,8,240]{2,1,0:T(8,128)(2,1)S(1)} %collective-permute-done.2), channel_id=1, source_target_pairs={{0,992},{32,0},{64,32},{96,64},{128,96},{160,128},{192,160},{224,1... | collective-permute-start | bytes 368648 | tf_op jit(solution)/shard_map/ppermute | solution.py:65
  67.7 8.1 %collective-permute-start.18 = (bf16[32,8,240]{2,1,0:T(8,128)(2,1)S(1)}, bf16[32,8,240]{2,1,0:T(8,128)(2,1)S(1)}, u32[]{:S(2)}, u32[]{:S(2)}) collective-permute-start(bf16[32,8,240]{2,1,0:T(8,128)(2,1)S(1)} %collective-permute-done.17), channel_id=1, source_target_pairs={{0,32},{32,64},{64,96},{96,128},{128,160},{160,192},{192,224},{224... | collective-permute-start | bytes 368648 | tf_op jit(solution)/shard_map/ppermute | solution.py:62
  70.3 8.0 %collective-permute-start.4 = (bf16[32,8,240]{2,1,0:T(8,128)(2,1)S(1)}, bf16[32,8,240]{2,1,0:T(8,128)(2,1)S(1)}, u32[]{:S(2)}, u32[]{:S(2)}) collective-permute-start(bf16[32,8,240]{2,1,0:T(8,128)(2,1)S(1)} %collective-permute-done.3), channel_id=1, source_target_pairs={{0,992},{32,0},{64,32},{96,64},{128,96},{160,128},{192,160},{224,1... | collective-permute-start | bytes 368648 | tf_op jit(solution)/shard_map/ppermute | solution.py:65
  75.7 8.1 %collective-permute-start.19 = (bf16[32,8,240]{2,1,0:T(8,128)(2,1)S(1)}, bf16[32,8,240]{2,1,0:T(8,128)(2,1)S(1)}, u32[]{:S(2)}, u32[]{:S(2)}) collective-permute-start(bf16[32,8,240]{2,1,0:T(8,128)(2,1)S(1)} %collective-permute-done.18), channel_id=1, source_target_pairs={{0,32},{32,64},{64,96},{96,128},{128,160},{160,192},{192,224},{224... | collective-permute-start | bytes 368648 | tf_op jit(solution)/shard_map/ppermute | solution.py:62
  78.3 8.1 %collective-permute-start.5 = (bf16[32,8,240]{2,1,0:T(8,128)(2,1)S(1)}, bf16[32,8,240]{2,1,0:T(8,128)(2,1)S(1)}, u32[]{:S(2)}, u32[]{:S(2)}) collective-permute-start(bf16[32,8,240]{2,1,0:T(8,128)(2,1)S(1)} %collective-permute-done.4), channel_id=1, source_target_pairs={{0,992},{32,0},{64,32},{96,64},{128,96},{160,128},{192,160},{224,1... | collective-permute-start | bytes 368648 | tf_op jit(solution)/shard_map/ppermute | solution.py:65
  83.8 8.1 %collective-permute-start.20 = (bf16[32,8,240]{2,1,0:T(8,128)(2,1)S(1)}, bf16[32,8,240]{2,1,0:T(8,128)(2,1)S(1)}, u32[]{:S(2)}, u32[]{:S(2)}) collective-permute-start(bf16[32,8,240]{2,1,0:T(8,128)(2,1)S(1)} %collective-permute-done.19), channel_id=1, source_target_pairs={{0,32},{32,64},{64,96},{96,128},{128,160},{160,192},{192,224},{224... | collective-permute-start | bytes 368648 | tf_op jit(solution)/shard_map/ppermute | solution.py:62
  86.4 8.1 %collective-permute-start.6 = (bf16[32,8,240]{2,1,0:T(8,128)(2,1)S(1)}, bf16[32,8,240]{2,1,0:T(8,128)(2,1)S(1)}, u32[]{:S(2)}, u32[]{:S(2)}) collective-permute-start(bf16[32,8,240]{2,1,0:T(8,128)(2,1)S(1)} %collective-permute-done.5), channel_id=1, source_target_pairs={{0,992},{32,0},{64,32},{96,64},{128,96},{160,128},{192,160},{224,1... | collective-permute-start | bytes 368648 | tf_op jit(solution)/shard_map/ppermute | solution.py:65
  91.8 8.4 %collective-permute-start.21 = (bf16[32,8,240]{2,1,0:T(8,128)(2,1)S(1)}, bf16[32,8,240]{2,1,0:T(8,128)(2,1)S(1)}, u32[]{:S(2)}, u32[]{:S(2)}) collective-permute-start(bf16[32,8,240]{2,1,0:T(8,128)(2,1)S(1)} %collective-permute-done.20), channel_id=1, source_target_pairs={{0,32},{32,64},{64,96},{96,128},{128,160},{160,192},{192,224},{224... | collective-permute-start | bytes 368648 | tf_op jit(solution)/shard_map/ppermute | solution.py:62
  94.5 9.1 %collective-permute-start.7 = (bf16[32,8,240]{2,1,0:T(8,128)(2,1)S(1)}, bf16[32,8,240]{2,1,0:T(8,128)(2,1)S(1)}, u32[]{:S(2)}, u32[]{:S(2)}) collective-permute-start(bf16[32,8,240]{2,1,0:T(8,128)(2,1)S(1)} %collective-permute-done.6), channel_id=1, source_target_pairs={{0,992},{32,0},{64,32},{96,64},{128,96},{160,128},{192,160},{224,1... | collective-permute-start | bytes 368648 | tf_op jit(solution)/shard_map/ppermute | solution.py:65
  100.3 9.2 %collective-permute-start.22 = (bf16[32,8,240]{2,1,0:T(8,128)(2,1)S(1)}, bf16[32,8,240]{2,1,0:T(8,128)(2,1)S(1)}, u32[]{:S(2)}, u32[]{:S(2)}) collective-permute-start(bf16[32,8,240]{2,1,0:T(8,128)(2,1)S(1)} %collective-permute-done.21), channel_id=1, source_target_pairs={{0,32},{32,64},{64,96},{96,128},{128,160},{160,192},{192,224},{224... | collective-permute-start | bytes 368648 | tf_op jit(solution)/shard_map/ppermute | solution.py:62
  103.5 9.0 %collective-permute-start.8 = (bf16[32,8,240]{2,1,0:T(8,128)(2,1)S(1)}, bf16[32,8,240]{2,1,0:T(8,128)(2,1)S(1)}, u32[]{:S(2)}, u32[]{:S(2)}) collective-permute-start(bf16[32,8,240]{2,1,0:T(8,128)(2,1)S(1)} %collective-permute-done.7), channel_id=1, source_target_pairs={{0,992},{32,0},{64,32},{96,64},{128,96},{160,128},{192,160},{224,1... | collective-permute-start | bytes 368648 | tf_op jit(solution)/shard_map/ppermute | solution.py:65
  109.5 9.0 %collective-permute-start.23 = (bf16[32,8,240]{2,1,0:T(8,128)(2,1)S(1)}, bf16[32,8,240]{2,1,0:T(8,128)(2,1)S(1)}, u32[]{:S(2)}, u32[]{:S(2)}) collective-permute-start(bf16[32,8,240]{2,1,0:T(8,128)(2,1)S(1)} %collective-permute-done.22), channel_id=1, source_target_pairs={{0,32},{32,64},{64,96},{96,128},{128,160},{160,192},{192,224},{224... | collective-permute-start | bytes 368648 | tf_op jit(solution)/shard_map/ppermute | solution.py:62
  112.5 8.6 %collective-permute-start.9 = (bf16[32,8,240]{2,1,0:T(8,128)(2,1)S(1)}, bf16[32,8,240]{2,1,0:T(8,128)(2,1)S(1)}, u32[]{:S(2)}, u32[]{:S(2)}) collective-permute-start(bf16[32,8,240]{2,1,0:T(8,128)(2,1)S(1)} %collective-permute-done.8), channel_id=1, source_target_pairs={{0,992},{32,0},{64,32},{96,64},{128,96},{160,128},{192,160},{224,1... | collective-permute-start | bytes 368648 | tf_op jit(solution)/shard_map/ppermute | solution.py:65
  118.5 8.2 %collective-permute-start.24 = (bf16[32,8,240]{2,1,0:T(8,128)(2,1)S(1)}, bf16[32,8,240]{2,1,0:T(8,128)(2,1)S(1)}, u32[]{:S(2)}, u32[]{:S(2)}) collective-permute-start(bf16[32,8,240]{2,1,0:T(8,128)(2,1)S(1)} %collective-permute-done.23), channel_id=1, source_target_pairs={{0,32},{32,64},{64,96},{96,128},{128,160},{160,192},{192,224},{224... | collective-permute-start | bytes 368648 | tf_op jit(solution)/shard_map/ppermute | solution.py:62
  121.1 8.2 %collective-permute-start.10 = (bf16[32,8,240]{2,1,0:T(8,128)(2,1)S(1)}, bf16[32,8,240]{2,1,0:T(8,128)(2,1)S(1)}, u32[]{:S(2)}, u32[]{:S(2)}) collective-permute-start(bf16[32,8,240]{2,1,0:T(8,128)(2,1)S(1)} %collective-permute-done.9), channel_id=1, source_target_pairs={{0,992},{32,0},{64,32},{96,64},{128,96},{160,128},{192,160},{224,1... | collective-permute-start | bytes 368648 | tf_op jit(solution)/shard_map/ppermute | solution.py:65
  126.7 8.1 %collective-permute-start.25 = (bf16[32,8,240]{2,1,0:T(8,128)(2,1)S(1)}, bf16[32,8,240]{2,1,0:T(8,128)(2,1)S(1)}, u32[]{:S(2)}, u32[]{:S(2)}) collective-permute-start(bf16[32,8,240]{2,1,0:T(8,128)(2,1)S(1)} %collective-permute-done.24), channel_id=1, source_target_pairs={{0,32},{32,64},{64,96},{96,128},{128,160},{160,192},{192,224},{224... | collective-permute-start | bytes 368648 | tf_op jit(solution)/shard_map/ppermute | solution.py:62
  129.3 8.1 %collective-permute-start.11 = (bf16[32,8,240]{2,1,0:T(8,128)(2,1)S(1)}, bf16[32,8,240]{2,1,0:T(8,128)(2,1)S(1)}, u32[]{:S(2)}, u32[]{:S(2)}) collective-permute-start(bf16[32,8,240]{2,1,0:T(8,128)(2,1)S(1)} %collective-permute-done.10), channel_id=1, source_target_pairs={{0,992},{32,0},{64,32},{96,64},{128,96},{160,128},{192,160},{224,1... | collective-permute-start | bytes 368648 | tf_op jit(solution)/shard_map/ppermute | solution.py:65
  134.7 8.1 %collective-permute-start.26 = (bf16[32,8,240]{2,1,0:T(8,128)(2,1)S(1)}, bf16[32,8,240]{2,1,0:T(8,128)(2,1)S(1)}, u32[]{:S(2)}, u32[]{:S(2)}) collective-permute-start(bf16[32,8,240]{2,1,0:T(8,128)(2,1)S(1)} %collective-permute-done.25), channel_id=1, source_target_pairs={{0,32},{32,64},{64,96},{96,128},{128,160},{160,192},{192,224},{224... | collective-permute-start | bytes 368648 | tf_op jit(solution)/shard_map/ppermute | solution.py:62
  137.3 8.1 %collective-permute-start.12 = (bf16[32,8,240]{2,1,0:T(8,128)(2,1)S(1)}, bf16[32,8,240]{2,1,0:T(8,128)(2,1)S(1)}, u32[]{:S(2)}, u32[]{:S(2)}) collective-permute-start(bf16[32,8,240]{2,1,0:T(8,128)(2,1)S(1)} %collective-permute-done.11), channel_id=1, source_target_pairs={{0,992},{32,0},{64,32},{96,64},{128,96},{160,128},{192,160},{224,1... | collective-permute-start | bytes 368648 | tf_op jit(solution)/shard_map/ppermute | solution.py:65
  142.8 8.1 %collective-permute-start.27 = (bf16[32,8,240]{2,1,0:T(8,128)(2,1)S(1)}, bf16[32,8,240]{2,1,0:T(8,128)(2,1)S(1)}, u32[]{:S(2)}, u32[]{:S(2)}) collective-permute-start(bf16[32,8,240]{2,1,0:T(8,128)(2,1)S(1)} %collective-permute-done.26), channel_id=1, source_target_pairs={{0,32},{32,64},{64,96},{96,128},{128,160},{160,192},{192,224},{224... | collective-permute-start | bytes 368648 | tf_op jit(solution)/shard_map/ppermute | solution.py:62
  145.4 8.1 %collective-permute-start.13 = (bf16[32,8,240]{2,1,0:T(8,128)(2,1)S(1)}, bf16[32,8,240]{2,1,0:T(8,128)(2,1)S(1)}, u32[]{:S(2)}, u32[]{:S(2)}) collective-permute-start(bf16[32,8,240]{2,1,0:T(8,128)(2,1)S(1)} %collective-permute-done.12), channel_id=1, source_target_pairs={{0,992},{32,0},{64,32},{96,64},{128,96},{160,128},{192,160},{224,1... | collective-permute-start | bytes 368648 | tf_op jit(solution)/shard_map/ppermute | solution.py:65
  150.9 8.1 %collective-permute-start.28 = (bf16[32,8,240]{2,1,0:T(8,128)(2,1)S(1)}, bf16[32,8,240]{2,1,0:T(8,128)(2,1)S(1)}, u32[]{:S(2)}, u32[]{:S(2)}) collective-permute-start(bf16[32,8,240]{2,1,0:T(8,128)(2,1)S(1)} %collective-permute-done.27), channel_id=1, source_target_pairs={{0,32},{32,64},{64,96},{96,128},{128,160},{160,192},{192,224},{224... | collective-permute-start | bytes 368648 | tf_op jit(solution)/shard_map/ppermute | solution.py:62
  153.5 15.6 %collective-permute-start.14 = (bf16[32,8,240]{2,1,0:T(8,128)(2,1)S(1)}, bf16[32,8,240]{2,1,0:T(8,128)(2,1)S(1)}, u32[]{:S(2)}, u32[]{:S(2)}) collective-permute-start(bf16[32,8,240]{2,1,0:T(8,128)(2,1)S(1)} %collective-permute-done.13), channel_id=1, source_target_pairs={{0,992},{32,0},{64,32},{96,64},{128,96},{160,128},{192,160},{224,1... | collective-permute-start | bytes 368648 | tf_op jit(solution)/shard_map/ppermute | solution.py:65
  158.9 8.1 %collective-permute-start.29 = (bf16[32,8,240]{2,1,0:T(8,128)(2,1)S(1)}, bf16[32,8,240]{2,1,0:T(8,128)(2,1)S(1)}, u32[]{:S(2)}, u32[]{:S(2)}) collective-permute-start(bf16[32,8,240]{2,1,0:T(8,128)(2,1)S(1)} %collective-permute-done.28), channel_id=1, source_target_pairs={{0,32},{32,64},{64,96},{96,128},{128,160},{160,192},{192,224},{224... | collective-permute-start | bytes 368648 | tf_op jit(solution)/shard_map/ppermute | solution.py:62
  167.0 8.1 %collective-permute-start.30 = (bf16[32,8,240]{2,1,0:T(8,128)(2,1)S(1)}, bf16[32,8,240]{2,1,0:T(8,128)(2,1)S(1)}, u32[]{:S(2)}, u32[]{:S(2)}) collective-permute-start(bf16[32,8,240]{2,1,0:T(8,128)(2,1)S(1)} %collective-permute-done.29), channel_id=1, source_target_pairs={{0,32},{32,64},{64,96},{96,128},{128,160},{160,192},{192,224},{224... | collective-permute-start | bytes 368648 | tf_op jit(solution)/shard_map/ppermute | solution.py:62
Sparse Core Ops, SparseCore 0:
  31.8 82.4 all-gather.1
